TPU v7x, 1024 devices: a whole 4x4x32 slice. The times are simulated.
1024 devices in a mesh: gx: 4 (over x), gy: 8 (over y, core), gz: 32 (over z).
Axes of the slice: x: 4, y: 4, z: 32, core: 2. Of those that a mesh axis runs over, the one named last changes fastest.
Arguments:
- right_side: float32 [32, 128, 8192], P('gx', 'gy', 'gz'), may hold values from -6 to 6
- coefficient: float32 [32, 128, 8192], P('gx', 'gy', 'gz'), may hold values from 0.3 to 3
- agg_weight: float32 [32, 128, 8192], P('gx', 'gy', 'gz'), may hold values from 0.03 to 0.1
- coarse_factor: float32 [8192, 8192], P(('gx', 'gy', 'gz')), may hold values from -0.25 to 0.25
Outputs:
- pressure_update: float32 [32, 128, 8192], P('gx', 'gy', 'gz')
- coarse_solution: float32 [8192], P(('gx', 'gy', 'gz'))
All inputs are finite; a program needn't handle non-finite values.
Results may differ from a plain program's by a relative error of at most 0.00024.
Values sent between devices are 32-bit elements; how exact they have to be, the bound alone decides.
No kernel may reach another device: no remote copies, remote signals or barrier semaphores. Data moves between devices by JAX's collectives and lax.ppermute only.
A program may use at most 32 MiB of HBM per device.

v0:
```python
import jax
import jax.numpy as jnp
import numpy as np
from jax import lax
from jax.sharding import PartitionSpec as P

ORDER = 7
CHEB = 4


highest = lax.Precision.HIGHEST
eig_high = 4.0
eig_low = 0.2
gll_inner = np.array(
    [
        -0.8717401485096066,
        -0.5917001814331423,
        -0.20929921790247888,
        0.20929921790247888,
        0.5917001814331423,
        0.8717401485096066,
    ]
)


def padded_2(cells, sides, width):
    for axis, dim in sides:
        count = lax.axis_size(axis)
        ends = count - 1
        head = lax.slice_in_dim(cells, 0, width, axis=dim)
        tail = lax.slice_in_dim(cells, cells.shape[dim] - width, cells.shape[dim], axis=dim)
        cells = jnp.concatenate(
            [
                lax.ppermute(tail, axis, [(i, (i + 1) % count) for i in range(ends)]),
                cells,
                lax.ppermute(head, axis, [((i + 1) % count, i) for i in range(ends)]),
            ],
            axis=dim,
        )
    return cells


def legendre_value(nodes, degree):
    previous = nodes * 0.0 + 1.0
    current = nodes
    for step in range(1, degree):
        following = ((2.0 * step + 1.0) * nodes * current - step * previous) / (step + 1.0)
        previous = current
        current = following
    return current


def gll_tables(poly_order):
    point_count = poly_order + 1
    gll_nodes = np.concatenate([np.array([-1.0]), gll_inner, np.array([1.0])])
    at_nodes = legendre_value(gll_nodes, poly_order)
    weights = 2.0 / (poly_order * point_count * at_nodes**2)
    differences = gll_nodes[:, None] - gll_nodes[None, :] + np.eye(point_count)
    derivative = at_nodes[:, None] / (at_nodes[None, :] * differences) * (1.0 - np.eye(point_count))
    end_value = poly_order * point_count / 4.0
    end_row = np.concatenate(
        [np.array([-end_value]), np.zeros(poly_order - 1), np.array([end_value])]
    )
    derivative = derivative + np.eye(point_count) * end_row[None, :]
    return (derivative, weights)


def forward_parts(field, mats):
    mat_x, mat_y, mat_z = mats
    size_x, size_y, size_z = field.shape
    grad_x = jnp.einsum("ia,ajk->ijk", mat_x, field, precision=highest)
    grad_y = jnp.einsum("ja,iak->ijk", mat_y, field, precision=highest)
    blocks = field.reshape(size_x, size_y, size_z // 128, 128)
    grad_z = jnp.einsum("ca,ijsa->ijsc", mat_z, blocks, precision=highest).reshape(field.shape)
    return (grad_x, grad_y, grad_z)


def backward_sum(parts, mats):
    mat_x, mat_y, mat_z = mats
    part_x, part_y, part_z = parts
    size_x, size_y, size_z = part_x.shape
    total = jnp.einsum("ai,ajk->ijk", mat_x, part_x, precision=highest)
    total = total + jnp.einsum("aj,iak->ijk", mat_y, part_y, precision=highest)
    blocks = part_z.reshape(size_x, size_y, size_z // 128, 128)
    total = total + jnp.einsum("ac,ijsa->ijsc", mat_z, blocks, precision=highest).reshape(
        part_x.shape
    )
    return total


def combine(padded, axis_dim, length, points):
    own = lax.slice_in_dim(padded, 1, length + 1, axis=axis_dim)
    left = lax.slice_in_dim(padded, 0, length, axis=axis_dim)
    right = lax.slice_in_dim(padded, 2, length + 2, axis=axis_dim)
    shape_list = [1, 1, 1]
    shape_list[axis_dim] = length
    position = (jnp.arange(length, dtype=jnp.int32) % points).reshape(shape_list)
    low_mask = (position == 0).astype(jnp.float32)
    high_mask = (position == points - 1).astype(jnp.float32)
    return own + low_mask * left + high_mask * right


def assemble(field, points):
    size_x, size_y, size_z = field.shape
    padded = padded_2(field, (("gx", 0), ("gy", 1), ("gz", 2)), 1)
    summed = combine(padded, 0, size_x, points)
    summed = combine(summed, 1, size_y, points)
    summed = combine(summed, 2, size_z, points)
    return summed


def per_device(right_side, coefficient, agg_weight, coarse_factor):
    points = ORDER + 1
    derivative, weights = gll_tables(ORDER)
    size_x, size_y, size_z = right_side.shape
    mat_x = jnp.asarray(np.kron(np.eye(size_x // points), derivative), dtype=jnp.float32)
    mat_y = jnp.asarray(np.kron(np.eye(size_y // points), derivative), dtype=jnp.float32)
    mat_z = jnp.asarray(np.kron(np.eye(128 // points), derivative), dtype=jnp.float32)
    mats = (mat_x, mat_y, mat_z)
    squares = (mat_x * mat_x, mat_y * mat_y, mat_z * mat_z)
    weight_x = jnp.asarray(np.tile(weights, size_x // points), dtype=jnp.float32)
    weight_y = jnp.asarray(np.tile(weights, size_y // points), dtype=jnp.float32)
    weight_z = jnp.asarray(np.tile(weights, size_z // points), dtype=jnp.float32)
    scaled = (
        coefficient * weight_x[:, None, None] * weight_y[None, :, None] * weight_z[None, None, :]
    )
    diagonal = assemble(backward_sum((scaled, scaled, scaled), squares), points)
    inverse = 1.0 / diagonal
    theta = (eig_high + eig_low) / 2.0
    delta = (eig_high - eig_low) / 2.0
    sigma = theta / delta
    residual = right_side
    direction = inverse * residual / theta
    smoothed = direction
    rho = 1.0 / sigma
    for sweep in range(CHEB):
        grads = forward_parts(direction, mats)
        local = backward_sum((scaled * grads[0], scaled * grads[1], scaled * grads[2]), mats)
        residual = residual - assemble(local, points)
        if sweep + 1 < CHEB:
            rho_new = 1.0 / (2.0 * sigma - rho)
            direction = rho_new * rho * direction + 2.0 * rho_new / delta * inverse * residual
            smoothed = smoothed + direction
            rho = rho_new
    aggregates = coarse_factor.shape[0]
    column_sums = jnp.sum(agg_weight * residual, axis=(0, 1))
    coarse_rhs = jnp.sum(column_sums.reshape(aggregates, size_z // aggregates), axis=1)
    partial_term = jnp.dot(coarse_rhs, coarse_factor, precision=highest)
    projected = lax.psum(partial_term, ("gx", "gy", "gz"))
    coarse_solution = jnp.dot(coarse_factor, projected, precision=highest)
    spread = jnp.repeat(coarse_solution, size_z // aggregates)
    pressure_update = smoothed + agg_weight * spread[None, None, :]
    return (pressure_update, coarse_solution)


def solution(mesh):
    return jax.shard_map(
        per_device,
        mesh=mesh,
        in_specs=(
            P("gx", "gy", "gz"),
            P("gx", "gy", "gz"),
            P("gx", "gy", "gz"),
            P(("gx", "gy", "gz"), None),
        ),
        out_specs=(P("gx", "gy", "gz"), P(("gx", "gy", "gz"))),
        check_vma=False,
    )
```

profile of v0, /device:TPU:24, one launch (start us, length us, event | category | flops | bytes accessed | tf_op | source)
XLA Modules:
  0.0 320.6 jit_solution(14255628673933377473)
XLA Ops:
  0.7 0.6 copy-done.9
  1.4 1.0 fusion.74
  2.7 0.4 copy-done.11
  3.4 0.4 copy-done.12
  4.2 3.4 %collective-permute-start = (f32[1,16,256]{2,0,1:T(1,128)S(1)}, f32[1,16,256]{2,0,1:T(1,128)S(1)}, u32[]{:S(2)}, u32[]{:S(2)}) collective-permute-start(f32[1,16,256]{2,0,1:T(1,128)S(1)} %get-tuple-element.42), channel_id=1, source_target_pairs={{0,256},{256,512},{512,768},{1,257},{257,513},{513,769},{2,258},{2... | collective-permute-start | bytes 49160 | tf_op jit(solution)/shard_map/ppermute | solution.py:34
  7.6 1.3 collective-permute-start.1
  9.0 4.2 %collective-permute-done.1 = f32[1,16,256]{2,0,1:T(1,128)S(1)} collective-permute-done((f32[1,16,256]{2,0,1:T(1,128)S(1)}, f32[1,16,256]{2,0,1:T(1,128)S(1)}, u32[]{:S(2)}, u32[]{:S(2)}) %collective-permute-start.1) | collective-permute-done | bytes 16416 | tf_op jit(solution)/shard_map/ppermute | solution.py:36
  13.2 1.9 collective-permute-start.2
  15.1 3.6 %collective-permute-start.3 = (f32[10,1,256]{2,0,1:T(8,128)S(1)}, f32[10,1,256]{2,0,1:T(8,128)S(1)}, u32[]{:S(2)}, u32[]{:S(2)}) collective-permute-start(f32[10,1,256]{2,0,1:T(8,128)S(1)} %get-tuple-element.33), channel_id=1, source_target_pairs={{32,0},{64,32},{96,64},{128,96},{160,128},{192,160},{224,192},{33,... | collective-permute-start | bytes 30728 | tf_op jit(solution)/shard_map/ppermute | solution.py:36
  18.8 1.4 collective-permute-done.3
  20.4 3.8 %collective-permute-start.4 = (f32[10,18,1]{2,0,1:T(8,128)S(1)}, f32[10,18,1]{2,0,1:T(8,128)S(1)}, u32[]{:S(2)}, u32[]{:S(2)}) collective-permute-start(f32[10,18,1]{2,0,1:T(8,128)S(1)} %get-tuple-element.22), channel_id=1, source_target_pairs={{0,1},{1,2},{2,3},{3,4},{4,5},{5,6},{6,7},{7,8},{8,9},{9,10},{10,1... | collective-permute-start | bytes 2168 | tf_op jit(solution)/shard_map/ppermute | solution.py:34
  24.2 1.3 collective-permute-start.5
  25.5 1.3 collective-permute-done.4
  26.9 4.4 %collective-permute-done.5 = f32[10,18,1]{2,0,1:T(8,128)S(1)} collective-permute-done((f32[10,18,1]{2,0,1:T(8,128)S(1)}, f32[10,18,1]{2,0,1:T(8,128)S(1)}, u32[]{:S(2)}, u32[]{:S(2)}) %collective-permute-start.5) | collective-permute-done | bytes 752 | tf_op jit(solution)/shard_map/ppermute | solution.py:36
  31.8 0.8 copy-done.3
  32.8 0.7 copy-done.2
  34.0 0.4 copy-done.4
  35.2 0.4 copy-done.6
  36.2 3.4 %collective-permute-start.6 = (f32[1,16,256]{2,0,1:T(1,128)S(1)}, f32[1,16,256]{2,0,1:T(1,128)S(1)}, u32[]{:S(2)}, u32[]{:S(2)}) collective-permute-start(f32[1,16,256]{2,0,1:T(1,128)S(1)} %get-tuple-element.40), channel_id=1, source_target_pairs={{0,256},{256,512},{512,768},{1,257},{257,513},{513,769},{2,258},{2... | collective-permute-start | bytes 49160 | tf_op jit(solution)/shard_map/ppermute | solution.py:34
  39.6 1.3 collective-permute-start.7
  41.0 4.2 %collective-permute-done.7 = f32[1,16,256]{2,0,1:T(1,128)S(1)} collective-permute-done((f32[1,16,256]{2,0,1:T(1,128)S(1)}, f32[1,16,256]{2,0,1:T(1,128)S(1)}, u32[]{:S(2)}, u32[]{:S(2)}) %collective-permute-start.7) | collective-permute-done | bytes 16416 | tf_op jit(solution)/shard_map/ppermute | solution.py:36
  45.3 1.9 collective-permute-start.8
  47.2 3.6 %collective-permute-start.9 = (f32[10,1,256]{2,0,1:T(8,128)S(1)}, f32[10,1,256]{2,0,1:T(8,128)S(1)}, u32[]{:S(2)}, u32[]{:S(2)}) collective-permute-start(f32[10,1,256]{2,0,1:T(8,128)S(1)} %get-tuple-element.31), channel_id=1, source_target_pairs={{32,0},{64,32},{96,64},{128,96},{160,128},{192,160},{224,192},{33,... | collective-permute-start | bytes 30728 | tf_op jit(solution)/shard_map/ppermute | solution.py:36
  50.8 1.4 collective-permute-done.9
  52.4 3.8 %collective-permute-start.10 = (f32[10,18,1]{2,0,1:T(8,128)S(1)}, f32[10,18,1]{2,0,1:T(8,128)S(1)}, u32[]{:S(2)}, u32[]{:S(2)}) collective-permute-start(f32[10,18,1]{2,0,1:T(8,128)S(1)} %get-tuple-element.20), channel_id=1, source_target_pairs={{0,1},{1,2},{2,3},{3,4},{4,5},{5,6},{6,7},{7,8},{8,9},{9,10},{10,1... | collective-permute-start | bytes 2168 | tf_op jit(solution)/shard_map/ppermute | solution.py:34
  56.2 1.3 collective-permute-start.11
  57.5 1.3 collective-permute-done.10
  58.9 5.4 %collective-permute-done.11 = f32[10,18,1]{2,0,1:T(8,128)S(1)} collective-permute-done((f32[10,18,1]{2,0,1:T(8,128)S(1)}, f32[10,18,1]{2,0,1:T(8,128)S(1)}, u32[]{:S(2)}, u32[]{:S(2)}) %collective-permute-start.11) | collective-permute-done | bytes 752 | tf_op jit(solution)/shard_map/ppermute | solution.py:36
  67.0 3.1 collective-permute-start.12
  70.1 1.3 collective-permute-start.13
  71.5 4.2 %collective-permute-done.13 = f32[1,16,256]{2,0,1:T(1,128)S(1)} collective-permute-done((f32[1,16,256]{2,0,1:T(1,128)S(1)}, f32[1,16,256]{2,0,1:T(1,128)S(1)}, u32[]{:S(2)}, u32[]{:S(2)}) %collective-permute-start.13) | collective-permute-done | bytes 16416 | tf_op jit(solution)/shard_map/ppermute | solution.py:36
  75.7 1.9 collective-permute-start.14
  77.7 3.6 %collective-permute-start.15 = (f32[10,1,256]{2,0,1:T(8,128)S(1)}, f32[10,1,256]{2,0,1:T(8,128)S(1)}, u32[]{:S(2)}, u32[]{:S(2)}) collective-permute-start(f32[10,1,256]{2,0,1:T(8,128)S(1)} %get-tuple-element.29), channel_id=1, source_target_pairs={{32,0},{64,32},{96,64},{128,96},{160,128},{192,160},{224,192},{33,... | collective-permute-start | bytes 30728 | tf_op jit(solution)/shard_map/ppermute | solution.py:36
  81.3 1.4 collective-permute-done.15
  82.9 5.1 %collective-permute-start.16 = (f32[10,18,1]{2,0,1:T(8,128)S(1)}, f32[10,18,1]{2,0,1:T(8,128)S(1)}, u32[]{:S(2)}, u32[]{:S(2)}) collective-permute-start(f32[10,18,1]{2,0,1:T(8,128)S(1)} %get-tuple-element.18), channel_id=1, source_target_pairs={{0,1},{1,2},{2,3},{3,4},{4,5},{5,6},{6,7},{7,8},{8,9},{9,10},{10,1... | collective-permute-start | bytes 2168 | tf_op jit(solution)/shard_map/ppermute | solution.py:34
  88.0 1.3 collective-permute-start.17
  89.3 1.3 collective-permute-done.16
  90.7 4.4 %collective-permute-done.17 = f32[10,18,1]{2,0,1:T(8,128)S(1)} collective-permute-done((f32[10,18,1]{2,0,1:T(8,128)S(1)}, f32[10,18,1]{2,0,1:T(8,128)S(1)}, u32[]{:S(2)}, u32[]{:S(2)}) %collective-permute-start.17) | collective-permute-done | bytes 752 | tf_op jit(solution)/shard_map/ppermute | solution.py:36
  97.8 1.9 collective-permute-start.18
  99.7 1.3 collective-permute-start.19
  101.1 4.2 %collective-permute-done.19 = f32[1,16,256]{2,0,1:T(1,128)S(1)} collective-permute-done((f32[1,16,256]{2,0,1:T(1,128)S(1)}, f32[1,16,256]{2,0,1:T(1,128)S(1)}, u32[]{:S(2)}, u32[]{:S(2)}) %collective-permute-start.19) | collective-permute-done | bytes 16416 | tf_op jit(solution)/shard_map/ppermute | solution.py:36
  105.4 1.9 collective-permute-start.20
  107.3 3.6 %collective-permute-start.21 = (f32[10,1,256]{2,0,1:T(8,128)S(1)}, f32[10,1,256]{2,0,1:T(8,128)S(1)}, u32[]{:S(2)}, u32[]{:S(2)}) collective-permute-start(f32[10,1,256]{2,0,1:T(8,128)S(1)} %get-tuple-element.27), channel_id=1, source_target_pairs={{32,0},{64,32},{96,64},{128,96},{160,128},{192,160},{224,192},{33,... | collective-permute-start | bytes 30728 | tf_op jit(solution)/shard_map/ppermute | solution.py:36
  111.0 1.4 collective-permute-done.21
  112.5 3.9 %collective-permute-start.22 = (f32[10,18,1]{2,0,1:T(8,128)S(1)}, f32[10,18,1]{2,0,1:T(8,128)S(1)}, u32[]{:S(2)}, u32[]{:S(2)}) collective-permute-start(f32[10,18,1]{2,0,1:T(8,128)S(1)} %get-tuple-element.16), channel_id=1, source_target_pairs={{0,1},{1,2},{2,3},{3,4},{4,5},{5,6},{6,7},{7,8},{8,9},{9,10},{10,1... | collective-permute-start | bytes 2168 | tf_op jit(solution)/shard_map/ppermute | solution.py:34
  116.5 1.3 collective-permute-start.23
  117.8 1.3 collective-permute-done.22
  119.1 4.4 %collective-permute-done.23 = f32[10,18,1]{2,0,1:T(8,128)S(1)} collective-permute-done((f32[10,18,1]{2,0,1:T(8,128)S(1)}, f32[10,18,1]{2,0,1:T(8,128)S(1)}, u32[]{:S(2)}, u32[]{:S(2)}) %collective-permute-start.23) | collective-permute-done | bytes 752 | tf_op jit(solution)/shard_map/ppermute | solution.py:36
  126.2 1.9 collective-permute-start.24
  128.1 1.3 collective-permute-start.25
  129.5 4.2 %collective-permute-done.25 = f32[1,16,256]{2,0,1:T(1,128)S(1)} collective-permute-done((f32[1,16,256]{2,0,1:T(1,128)S(1)}, f32[1,16,256]{2,0,1:T(1,128)S(1)}, u32[]{:S(2)}, u32[]{:S(2)}) %collective-permute-start.25) | collective-permute-done | bytes 16416 | tf_op jit(solution)/shard_map/ppermute | solution.py:36
  133.7 1.9 collective-permute-start.26
  135.7 3.6 %collective-permute-start.27 = (f32[10,1,256]{2,0,1:T(8,128)S(1)}, f32[10,1,256]{2,0,1:T(8,128)S(1)}, u32[]{:S(2)}, u32[]{:S(2)}) collective-permute-start(f32[10,1,256]{2,0,1:T(8,128)S(1)} %get-tuple-element.25), channel_id=1, source_target_pairs={{32,0},{64,32},{96,64},{128,96},{160,128},{192,160},{224,192},{33,... | collective-permute-start | bytes 30728 | tf_op jit(solution)/shard_map/ppermute | solution.py:36
  139.3 1.4 collective-permute-done.27
  140.9 4.8 %collective-permute-start.28 = (f32[10,18,1]{2,0,1:T(8,128)S(1)}, f32[10,18,1]{2,0,1:T(8,128)S(1)}, u32[]{:S(2)}, u32[]{:S(2)}) collective-permute-start(f32[10,18,1]{2,0,1:T(8,128)S(1)} %get-tuple-element.14), channel_id=1, source_target_pairs={{0,1},{1,2},{2,3},{3,4},{4,5},{5,6},{6,7},{7,8},{8,9},{9,10},{10,1... | collective-permute-start | bytes 2168 | tf_op jit(solution)/shard_map/ppermute | solution.py:34
  145.7 1.3 collective-permute-start.29
  147.0 1.3 collective-permute-done.28
  148.3 4.4 %collective-permute-done.29 = f32[10,18,1]{2,0,1:T(8,128)S(1)} collective-permute-done((f32[10,18,1]{2,0,1:T(8,128)S(1)}, f32[10,18,1]{2,0,1:T(8,128)S(1)}, u32[]{:S(2)}, u32[]{:S(2)}) %collective-permute-start.29) | collective-permute-done | bytes 752 | tf_op jit(solution)/shard_map/ppermute | solution.py:36
  153.3 0.8 copy-done.5
  154.4 0.4 fusion.76
  154.8 163.7 %psum.7 = f32[8192]{0:T(1024)S(1)} all-reduce(f32[8192]{0:T(1024)S(1)} %bitcast.142), channel_id=1, replica_groups=mesh['gx'=4,'gy'=8,'gz'=32] {'gx','gy','gz'}, use_global_device_ids=true, to_apply=%region_2.3 | all-reduce | flops 8192 | bytes 65536 | tf_op jit(solution)/shard_map/psum | solution.py:149
  318.5 0.7 convolution_bitcast_fusion.9
  319.3 0.5 copy-done.13
  319.9 0.7 copy.127
  (108 shorter events, 14.0 us)
Async XLA Ops:
  0.6 153.8 %copy-start = (f32[8,8192]{1,0:T(8,128)S(1)}, f32[8,8192]{1,0:T(8,128)}, u32[]{:S(2)}) copy-start(f32[8,8192]{1,0:T(8,128)} %param.13) | copy-start | bytes 786436
  0.6 0.7 copy-start.9
  0.7 0.7 copy-start.7
  0.7 0.7 copy-start.8
  0.7 1.7 copy-start.10
  0.7 1.7 copy-start.1
  2.4 0.7 copy-start.11
  3.1 0.7 copy-start.12
  4.2 4.8 %collective-permute-start = (f32[1,16,256]{2,0,1:T(1,128)S(1)}, f32[1,16,256]{2,0,1:T(1,128)S(1)}, u32[]{:S(2)}, u32[]{:S(2)}) collective-permute-start(f32[1,16,256]{2,0,1:T(1,128)S(1)} %get-tuple-element.42), channel_id=1, source_target_pairs={{0,256},{256,512},{512,768},{1,257},{257,513},{513,769},{2,258},{2... | collective-permute-start | bytes 49160 | tf_op jit(solution)/shard_map/ppermute | solution.py:34
  7.6 5.6 %collective-permute-start.1 = (f32[1,16,256]{2,0,1:T(1,128)S(1)}, f32[1,16,256]{2,0,1:T(1,128)S(1)}, u32[]{:S(2)}, u32[]{:S(2)}) collective-permute-start(f32[1,16,256]{2,0,1:T(1,128)S(1)} %get-tuple-element.43), channel_id=1, source_target_pairs={{256,0},{512,256},{768,512},{257,1},{513,257},{769,513},{258,2},{5... | collective-permute-start | bytes 49160 | tf_op jit(solution)/shard_map/ppermute | solution.py:36
  13.2 5.6 %collective-permute-start.2 = (f32[10,1,256]{2,0,1:T(8,128)S(1)}, f32[10,1,256]{2,0,1:T(8,128)S(1)}, u32[]{:S(2)}, u32[]{:S(2)}) collective-permute-start(f32[10,1,256]{2,0,1:T(8,128)S(1)} %get-tuple-element.32), channel_id=1, source_target_pairs={{0,32},{32,64},{64,96},{96,128},{128,160},{160,192},{192,224},{1,3... | collective-permute-start | bytes 30728 | tf_op jit(solution)/shard_map/ppermute | solution.py:34
  15.1 5.1 %collective-permute-start.3 = (f32[10,1,256]{2,0,1:T(8,128)S(1)}, f32[10,1,256]{2,0,1:T(8,128)S(1)}, u32[]{:S(2)}, u32[]{:S(2)}) collective-permute-start(f32[10,1,256]{2,0,1:T(8,128)S(1)} %get-tuple-element.33), channel_id=1, source_target_pairs={{32,0},{64,32},{96,64},{128,96},{160,128},{192,160},{224,192},{33,... | collective-permute-start | bytes 30728 | tf_op jit(solution)/shard_map/ppermute | solution.py:36
  20.4 6.5 %collective-permute-start.4 = (f32[10,18,1]{2,0,1:T(8,128)S(1)}, f32[10,18,1]{2,0,1:T(8,128)S(1)}, u32[]{:S(2)}, u32[]{:S(2)}) collective-permute-start(f32[10,18,1]{2,0,1:T(8,128)S(1)} %get-tuple-element.22), channel_id=1, source_target_pairs={{0,1},{1,2},{2,3},{3,4},{4,5},{5,6},{6,7},{7,8},{8,9},{9,10},{10,1... | collective-permute-start | bytes 2168 | tf_op jit(solution)/shard_map/ppermute | solution.py:34
  24.2 7.0 %collective-permute-start.5 = (f32[10,18,1]{2,0,1:T(8,128)S(1)}, f32[10,18,1]{2,0,1:T(8,128)S(1)}, u32[]{:S(2)}, u32[]{:S(2)}) collective-permute-start(f32[10,18,1]{2,0,1:T(8,128)S(1)} %get-tuple-element.23), channel_id=1, source_target_pairs={{1,0},{2,1},{3,2},{4,3},{5,4},{6,5},{7,6},{8,7},{9,8},{10,9},{11,1... | collective-permute-start | bytes 2168 | tf_op jit(solution)/shard_map/ppermute | solution.py:36
  31.7 0.9 copy-start.3
  32.6 0.8 copy-start.2
  33.7 0.7 copy-start.4
  34.9 0.7 copy-start.6
  36.2 4.8 %collective-permute-start.6 = (f32[1,16,256]{2,0,1:T(1,128)S(1)}, f32[1,16,256]{2,0,1:T(1,128)S(1)}, u32[]{:S(2)}, u32[]{:S(2)}) collective-permute-start(f32[1,16,256]{2,0,1:T(1,128)S(1)} %get-tuple-element.40), channel_id=1, source_target_pairs={{0,256},{256,512},{512,768},{1,257},{257,513},{513,769},{2,258},{2... | collective-permute-start | bytes 49160 | tf_op jit(solution)/shard_map/ppermute | solution.py:34
  39.6 5.6 %collective-permute-start.7 = (f32[1,16,256]{2,0,1:T(1,128)S(1)}, f32[1,16,256]{2,0,1:T(1,128)S(1)}, u32[]{:S(2)}, u32[]{:S(2)}) collective-permute-start(f32[1,16,256]{2,0,1:T(1,128)S(1)} %get-tuple-element.41), channel_id=1, source_target_pairs={{256,0},{512,256},{768,512},{257,1},{513,257},{769,513},{258,2},{5... | collective-permute-start | bytes 49160 | tf_op jit(solution)/shard_map/ppermute | solution.py:36
  45.3 5.6 %collective-permute-start.8 = (f32[10,1,256]{2,0,1:T(8,128)S(1)}, f32[10,1,256]{2,0,1:T(8,128)S(1)}, u32[]{:S(2)}, u32[]{:S(2)}) collective-permute-start(f32[10,1,256]{2,0,1:T(8,128)S(1)} %get-tuple-element.30), channel_id=1, source_target_pairs={{0,32},{32,64},{64,96},{96,128},{128,160},{160,192},{192,224},{1,3... | collective-permute-start | bytes 30728 | tf_op jit(solution)/shard_map/ppermute | solution.py:34
  47.2 5.1 %collective-permute-start.9 = (f32[10,1,256]{2,0,1:T(8,128)S(1)}, f32[10,1,256]{2,0,1:T(8,128)S(1)}, u32[]{:S(2)}, u32[]{:S(2)}) collective-permute-start(f32[10,1,256]{2,0,1:T(8,128)S(1)} %get-tuple-element.31), channel_id=1, source_target_pairs={{32,0},{64,32},{96,64},{128,96},{160,128},{192,160},{224,192},{33,... | collective-permute-start | bytes 30728 | tf_op jit(solution)/shard_map/ppermute | solution.py:36
  52.4 6.5 %collective-permute-start.10 = (f32[10,18,1]{2,0,1:T(8,128)S(1)}, f32[10,18,1]{2,0,1:T(8,128)S(1)}, u32[]{:S(2)}, u32[]{:S(2)}) collective-permute-start(f32[10,18,1]{2,0,1:T(8,128)S(1)} %get-tuple-element.20), channel_id=1, source_target_pairs={{0,1},{1,2},{2,3},{3,4},{4,5},{5,6},{6,7},{7,8},{8,9},{9,10},{10,1... | collective-permute-start | bytes 2168 | tf_op jit(solution)/shard_map/ppermute | solution.py:34
  56.2 8.0 %collective-permute-start.11 = (f32[10,18,1]{2,0,1:T(8,128)S(1)}, f32[10,18,1]{2,0,1:T(8,128)S(1)}, u32[]{:S(2)}, u32[]{:S(2)}) collective-permute-start(f32[10,18,1]{2,0,1:T(8,128)S(1)} %get-tuple-element.21), channel_id=1, source_target_pairs={{1,0},{2,1},{3,2},{4,3},{5,4},{6,5},{7,6},{8,7},{9,8},{10,9},{11,1... | collective-permute-start | bytes 2168 | tf_op jit(solution)/shard_map/ppermute | solution.py:36
  67.0 4.5 %collective-permute-start.12 = (f32[1,16,256]{2,0,1:T(1,128)S(1)}, f32[1,16,256]{2,0,1:T(1,128)S(1)}, u32[]{:S(2)}, u32[]{:S(2)}) collective-permute-start(f32[1,16,256]{2,0,1:T(1,128)S(1)} %get-tuple-element.38), channel_id=1, source_target_pairs={{0,256},{256,512},{512,768},{1,257},{257,513},{513,769},{2,258},{2... | collective-permute-start | bytes 49160 | tf_op jit(solution)/shard_map/ppermute | solution.py:34
  70.1 5.6 %collective-permute-start.13 = (f32[1,16,256]{2,0,1:T(1,128)S(1)}, f32[1,16,256]{2,0,1:T(1,128)S(1)}, u32[]{:S(2)}, u32[]{:S(2)}) collective-permute-start(f32[1,16,256]{2,0,1:T(1,128)S(1)} %get-tuple-element.39), channel_id=1, source_target_pairs={{256,0},{512,256},{768,512},{257,1},{513,257},{769,513},{258,2},{5... | collective-permute-start | bytes 49160 | tf_op jit(solution)/shard_map/ppermute | solution.py:36
  75.7 5.6 %collective-permute-start.14 = (f32[10,1,256]{2,0,1:T(8,128)S(1)}, f32[10,1,256]{2,0,1:T(8,128)S(1)}, u32[]{:S(2)}, u32[]{:S(2)}) collective-permute-start(f32[10,1,256]{2,0,1:T(8,128)S(1)} %get-tuple-element.28), channel_id=1, source_target_pairs={{0,32},{32,64},{64,96},{96,128},{128,160},{160,192},{192,224},{1,3... | collective-permute-start | bytes 30728 | tf_op jit(solution)/shard_map/ppermute | solution.py:34
  77.7 5.1 %collective-permute-start.15 = (f32[10,1,256]{2,0,1:T(8,128)S(1)}, f32[10,1,256]{2,0,1:T(8,128)S(1)}, u32[]{:S(2)}, u32[]{:S(2)}) collective-permute-start(f32[10,1,256]{2,0,1:T(8,128)S(1)} %get-tuple-element.29), channel_id=1, source_target_pairs={{32,0},{64,32},{96,64},{128,96},{160,128},{192,160},{224,192},{33,... | collective-permute-start | bytes 30728 | tf_op jit(solution)/shard_map/ppermute | solution.py:36
  82.9 7.8 %collective-permute-start.16 = (f32[10,18,1]{2,0,1:T(8,128)S(1)}, f32[10,18,1]{2,0,1:T(8,128)S(1)}, u32[]{:S(2)}, u32[]{:S(2)}) collective-permute-start(f32[10,18,1]{2,0,1:T(8,128)S(1)} %get-tuple-element.18), channel_id=1, source_target_pairs={{0,1},{1,2},{2,3},{3,4},{4,5},{5,6},{6,7},{7,8},{8,9},{9,10},{10,1... | collective-permute-start | bytes 2168 | tf_op jit(solution)/shard_map/ppermute | solution.py:34
  88.0 7.0 %collective-permute-start.17 = (f32[10,18,1]{2,0,1:T(8,128)S(1)}, f32[10,18,1]{2,0,1:T(8,128)S(1)}, u32[]{:S(2)}, u32[]{:S(2)}) collective-permute-start(f32[10,18,1]{2,0,1:T(8,128)S(1)} %get-tuple-element.19), channel_id=1, source_target_pairs={{1,0},{2,1},{3,2},{4,3},{5,4},{6,5},{7,6},{8,7},{9,8},{10,9},{11,1... | collective-permute-start | bytes 2168 | tf_op jit(solution)/shard_map/ppermute | solution.py:36
  97.8 3.4 %collective-permute-start.18 = (f32[1,16,256]{2,0,1:T(1,128)S(1)}, f32[1,16,256]{2,0,1:T(1,128)S(1)}, u32[]{:S(2)}, u32[]{:S(2)}) collective-permute-start(f32[1,16,256]{2,0,1:T(1,128)S(1)} %get-tuple-element.36), channel_id=1, source_target_pairs={{0,256},{256,512},{512,768},{1,257},{257,513},{513,769},{2,258},{2... | collective-permute-start | bytes 49160 | tf_op jit(solution)/shard_map/ppermute | solution.py:34
  99.7 5.6 %collective-permute-start.19 = (f32[1,16,256]{2,0,1:T(1,128)S(1)}, f32[1,16,256]{2,0,1:T(1,128)S(1)}, u32[]{:S(2)}, u32[]{:S(2)}) collective-permute-start(f32[1,16,256]{2,0,1:T(1,128)S(1)} %get-tuple-element.37), channel_id=1, source_target_pairs={{256,0},{512,256},{768,512},{257,1},{513,257},{769,513},{258,2},{5... | collective-permute-start | bytes 49160 | tf_op jit(solution)/shard_map/ppermute | solution.py:36
  105.4 5.6 %collective-permute-start.20 = (f32[10,1,256]{2,0,1:T(8,128)S(1)}, f32[10,1,256]{2,0,1:T(8,128)S(1)}, u32[]{:S(2)}, u32[]{:S(2)}) collective-permute-start(f32[10,1,256]{2,0,1:T(8,128)S(1)} %get-tuple-element.26), channel_id=1, source_target_pairs={{0,32},{32,64},{64,96},{96,128},{128,160},{160,192},{192,224},{1,3... | collective-permute-start | bytes 30728 | tf_op jit(solution)/shard_map/ppermute | solution.py:34
  107.3 5.1 %collective-permute-start.21 = (f32[10,1,256]{2,0,1:T(8,128)S(1)}, f32[10,1,256]{2,0,1:T(8,128)S(1)}, u32[]{:S(2)}, u32[]{:S(2)}) collective-permute-start(f32[10,1,256]{2,0,1:T(8,128)S(1)} %get-tuple-element.27), channel_id=1, source_target_pairs={{32,0},{64,32},{96,64},{128,96},{160,128},{192,160},{224,192},{33,... | collective-permute-start | bytes 30728 | tf_op jit(solution)/shard_map/ppermute | solution.py:36
  112.5 6.6 %collective-permute-start.22 = (f32[10,18,1]{2,0,1:T(8,128)S(1)}, f32[10,18,1]{2,0,1:T(8,128)S(1)}, u32[]{:S(2)}, u32[]{:S(2)}) collective-permute-start(f32[10,18,1]{2,0,1:T(8,128)S(1)} %get-tuple-element.16), channel_id=1, source_target_pairs={{0,1},{1,2},{2,3},{3,4},{4,5},{5,6},{6,7},{7,8},{8,9},{9,10},{10,1... | collective-permute-start | bytes 2168 | tf_op jit(solution)/shard_map/ppermute | solution.py:34
  116.5 7.0 %collective-permute-start.23 = (f32[10,18,1]{2,0,1:T(8,128)S(1)}, f32[10,18,1]{2,0,1:T(8,128)S(1)}, u32[]{:S(2)}, u32[]{:S(2)}) collective-permute-start(f32[10,18,1]{2,0,1:T(8,128)S(1)} %get-tuple-element.17), channel_id=1, source_target_pairs={{1,0},{2,1},{3,2},{4,3},{5,4},{6,5},{7,6},{8,7},{9,8},{10,9},{11,1... | collective-permute-start | bytes 2168 | tf_op jit(solution)/shard_map/ppermute | solution.py:36
  126.2 3.4 %collective-permute-start.24 = (f32[1,16,256]{2,0,1:T(1,128)S(1)}, f32[1,16,256]{2,0,1:T(1,128)S(1)}, u32[]{:S(2)}, u32[]{:S(2)}) collective-permute-start(f32[1,16,256]{2,0,1:T(1,128)S(1)} %get-tuple-element.34), channel_id=1, source_target_pairs={{0,256},{256,512},{512,768},{1,257},{257,513},{513,769},{2,258},{2... | collective-permute-start | bytes 49160 | tf_op jit(solution)/shard_map/ppermute | solution.py:34
  128.1 5.6 %collective-permute-start.25 = (f32[1,16,256]{2,0,1:T(1,128)S(1)}, f32[1,16,256]{2,0,1:T(1,128)S(1)}, u32[]{:S(2)}, u32[]{:S(2)}) collective-permute-start(f32[1,16,256]{2,0,1:T(1,128)S(1)} %get-tuple-element.35), channel_id=1, source_target_pairs={{256,0},{512,256},{768,512},{257,1},{513,257},{769,513},{258,2},{5... | collective-permute-start | bytes 49160 | tf_op jit(solution)/shard_map/ppermute | solution.py:36
  133.7 5.6 %collective-permute-start.26 = (f32[10,1,256]{2,0,1:T(8,128)S(1)}, f32[10,1,256]{2,0,1:T(8,128)S(1)}, u32[]{:S(2)}, u32[]{:S(2)}) collective-permute-start(f32[10,1,256]{2,0,1:T(8,128)S(1)} %get-tuple-element.24), channel_id=1, source_target_pairs={{0,32},{32,64},{64,96},{96,128},{128,160},{160,192},{192,224},{1,3... | collective-permute-start | bytes 30728 | tf_op jit(solution)/shard_map/ppermute | solution.py:34
  135.7 5.1 %collective-permute-start.27 = (f32[10,1,256]{2,0,1:T(8,128)S(1)}, f32[10,1,256]{2,0,1:T(8,128)S(1)}, u32[]{:S(2)}, u32[]{:S(2)}) collective-permute-start(f32[10,1,256]{2,0,1:T(8,128)S(1)} %get-tuple-element.25), channel_id=1, source_target_pairs={{32,0},{64,32},{96,64},{128,96},{160,128},{192,160},{224,192},{33,... | collective-permute-start | bytes 30728 | tf_op jit(solution)/shard_map/ppermute | solution.py:36
  140.9 7.4 %collective-permute-start.28 = (f32[10,18,1]{2,0,1:T(8,128)S(1)}, f32[10,18,1]{2,0,1:T(8,128)S(1)}, u32[]{:S(2)}, u32[]{:S(2)}) collective-permute-start(f32[10,18,1]{2,0,1:T(8,128)S(1)} %get-tuple-element.14), channel_id=1, source_target_pairs={{0,1},{1,2},{2,3},{3,4},{4,5},{5,6},{6,7},{7,8},{8,9},{9,10},{10,1... | collective-permute-start | bytes 2168 | tf_op jit(solution)/shard_map/ppermute | solution.py:34
  145.7 7.0 %collective-permute-start.29 = (f32[10,18,1]{2,0,1:T(8,128)S(1)}, f32[10,18,1]{2,0,1:T(8,128)S(1)}, u32[]{:S(2)}, u32[]{:S(2)}) collective-permute-start(f32[10,18,1]{2,0,1:T(8,128)S(1)} %get-tuple-element.15), channel_id=1, source_target_pairs={{1,0},{2,1},{3,2},{4,3},{5,4},{6,5},{7,6},{8,7},{9,8},{10,9},{11,1... | collective-permute-start | bytes 2168 | tf_op jit(solution)/shard_map/ppermute | solution.py:36
  153.1 0.9 copy-start.5
  319.2 0.5 copy-start.13
where the time goes:
time: 324 us; the launch traced here: 321 us
  blocking collectives  164 us (51%)
  starting transfers between devices  76 us (23%)
  waiting for transfers between devices  58.4 us (18%)
  matrix products  8.82 us (3%)
  local copies, waits for them, and re-layouts  6.52 us (2%)
  other arithmetic  5.69 us (2%)
    psum x1, blocking collectives, per_device(): projected = lax.psum(partial_term, ('gx', 'gy', 'gz'))  164 us
    ppermute x15, waiting for transfers between devices, padded_2(): lax.ppermute(head, axis, [((i + 1) % count, i) for i in range(ends)])  51 us
    ppermute x15, starting transfers between devices, padded_2(): lax.ppermute(tail, axis, [(i, (i + 1) % count) for i in range(ends)])  44.8 us
    ppermute x15, starting transfers between devices, padded_2(): lax.ppermute(head, axis, [((i + 1) % count, i) for i in range(ends)])  31.1 us
    ppermute x15, waiting for transfers between devices, padded_2(): lax.ppermute(tail, axis, [(i, (i + 1) % count) for i in range(ends)])  7.36 us
  transfers between devices with their start and end apart: 30, of which 25 were waited for; matrix products, arithmetic and copies ran while one was open for 0% of the time, Pallas kernels for 0%

commit v1 on v0

--- a/solution.py
+++ b/solution.py
@@ -38,6 +38,16 @@
             axis=dim,
         )
     return cells
+
+
+def butterfly_sum(value, axes):
+    for axis in axes:
+        count = lax.axis_size(axis)
+        stride = 1
+        while stride < count:
+            value = value + lax.ppermute(value, axis, [(i, i ^ stride) for i in range(count)])
+            stride *= 2
+    return value
 
 
 def legendre_value(nodes, degree):
@@ -146,7 +156,7 @@
     column_sums = jnp.sum(agg_weight * residual, axis=(0, 1))
     coarse_rhs = jnp.sum(column_sums.reshape(aggregates, size_z // aggregates), axis=1)
     partial_term = jnp.dot(coarse_rhs, coarse_factor, precision=highest)
-    projected = lax.psum(partial_term, ("gx", "gy", "gz"))
+    projected = butterfly_sum(partial_term, ("gy", "gz", "gx"))
     coarse_solution = jnp.dot(coarse_factor, projected, precision=highest)
     spread = jnp.repeat(coarse_solution, size_z // aggregates)
     pressure_update = smoothed + agg_weight * spread[None, None, :]

time: 324 us -> 258 us (0.80)
  blocking collectives: 164 us -> 0 us
  starting transfers between devices: 76 us -> 144 us
  waiting for transfers between devices: 58.4 us -> 87.3 us
    psum x1 -> x0, blocking collectives: 164 us -> none  [per_device(): projected = lax.psum(partial_term, ('gx', 'gy', 'gz'))]
    ppermute x0 -> x10, starting transfers between devices: none -> 68.2 us  [butterfly_sum(): lax.ppermute(value, axis, [(i, i ^ stride) for i in range(count)])]
    ppermute x0 -> x10, waiting for transfers between devices: none -> 28.9 us  [butterfly_sum(): lax.ppermute(value, axis, [(i, i ^ stride) for i in range(count)])]
  transfers between devices with their start and end apart: 30 -> 40, of which waited for: 25 -> 35; matrix products, arithmetic and copies ran while one was open for 0% -> 0% of each run, Pallas kernels for 0% -> 0%
where the time goes in v1:
time: 258 us; the launch traced here: 254 us
  starting transfers between devices  144 us (56%)
  waiting for transfers between devices  87.3 us (34%)
  matrix products  8.82 us (3%)
  local copies, waits for them, and re-layouts  6.52 us (3%)
  other arithmetic  5.75 us (2%)
    ppermute x10, starting transfers between devices, butterfly_sum(): lax.ppermute(value, axis, [(i, i ^ stride) for i in range(count)])  68.2 us
    ppermute x15, waiting for transfers between devices, padded_2(): lax.ppermute(head, axis, [((i + 1) % count, i) for i in range(ends)])  51 us
    ppermute x15, starting transfers between devices, padded_2(): lax.ppermute(tail, axis, [(i, (i + 1) % count) for i in range(ends)])  44.8 us
    ppermute x15, starting transfers between devices, padded_2(): lax.ppermute(head, axis, [((i + 1) % count, i) for i in range(ends)])  31.1 us
    ppermute x10, waiting for transfers between devices, butterfly_sum(): lax.ppermute(value, axis, [(i, i ^ stride) for i in range(count)])  28.9 us
    ppermute x15, waiting for transfers between devices, padded_2(): lax.ppermute(tail, axis, [(i, (i + 1) % count) for i in range(ends)])  7.36 us
    unnamed x29, local copies, waits for them, and re-layouts  5.7 us
  transfers between devices with their start and end apart: 40, of which 35 were waited for; matrix products, arithmetic and copies ran while one was open for 0% of the time, Pallas kernels for 0%

profile of v1, /device:TPU:24, one launch (start us, length us, event | category | flops | bytes accessed | tf_op | source)
XLA Modules:
  0.0 254.1 jit_solution(11344530363665737241)
XLA Ops:
  4.2 3.4 %collective-permute-start = (f32[1,16,256]{2,0,1:T(1,128)S(1)}, f32[1,16,256]{2,0,1:T(1,128)S(1)}, u32[]{:S(2)}, u32[]{:S(2)}) collective-permute-start(f32[1,16,256]{2,0,1:T(1,128)S(1)} %get-tuple-element.42), channel_id=1, source_target_pairs={{0,256},{256,512},{512,768},{1,257},{257,513},{513,769},{2,258},{2... | collective-permute-start | bytes 49160 | tf_op jit(solution)/shard_map/ppermute | solution.py:34
  7.6 1.3 collective-permute-start.1
  9.0 4.2 %collective-permute-done.1 = f32[1,16,256]{2,0,1:T(1,128)S(1)} collective-permute-done((f32[1,16,256]{2,0,1:T(1,128)S(1)}, f32[1,16,256]{2,0,1:T(1,128)S(1)}, u32[]{:S(2)}, u32[]{:S(2)}) %collective-permute-start.1) | collective-permute-done | bytes 16416 | tf_op jit(solution)/shard_map/ppermute | solution.py:36
  13.2 1.9 collective-permute-start.2
  15.1 3.6 %collective-permute-start.3 = (f32[10,1,256]{2,0,1:T(8,128)S(1)}, f32[10,1,256]{2,0,1:T(8,128)S(1)}, u32[]{:S(2)}, u32[]{:S(2)}) collective-permute-start(f32[10,1,256]{2,0,1:T(8,128)S(1)} %get-tuple-element.33), channel_id=1, source_target_pairs={{32,0},{64,32},{96,64},{128,96},{160,128},{192,160},{224,192},{33,... | collective-permute-start | bytes 30728 | tf_op jit(solution)/shard_map/ppermute | solution.py:36
  18.8 1.4 collective-permute-done.3
  20.4 3.8 %collective-permute-start.4 = (f32[10,18,1]{2,0,1:T(8,128)S(1)}, f32[10,18,1]{2,0,1:T(8,128)S(1)}, u32[]{:S(2)}, u32[]{:S(2)}) collective-permute-start(f32[10,18,1]{2,0,1:T(8,128)S(1)} %get-tuple-element.22), channel_id=1, source_target_pairs={{0,1},{1,2},{2,3},{3,4},{4,5},{5,6},{6,7},{7,8},{8,9},{9,10},{10,1... | collective-permute-start | bytes 2168 | tf_op jit(solution)/shard_map/ppermute | solution.py:34
  24.2 1.3 collective-permute-start.5
  25.5 1.3 collective-permute-done.4
  26.9 4.4 %collective-permute-done.5 = f32[10,18,1]{2,0,1:T(8,128)S(1)} collective-permute-done((f32[10,18,1]{2,0,1:T(8,128)S(1)}, f32[10,18,1]{2,0,1:T(8,128)S(1)}, u32[]{:S(2)}, u32[]{:S(2)}) %collective-permute-start.5) | collective-permute-done | bytes 752 | tf_op jit(solution)/shard_map/ppermute | solution.py:36
  36.2 3.4 %collective-permute-start.6 = (f32[1,16,256]{2,0,1:T(1,128)S(1)}, f32[1,16,256]{2,0,1:T(1,128)S(1)}, u32[]{:S(2)}, u32[]{:S(2)}) collective-permute-start(f32[1,16,256]{2,0,1:T(1,128)S(1)} %get-tuple-element.40), channel_id=1, source_target_pairs={{0,256},{256,512},{512,768},{1,257},{257,513},{513,769},{2,258},{2... | collective-permute-start | bytes 49160 | tf_op jit(solution)/shard_map/ppermute | solution.py:34
  39.6 1.3 collective-permute-start.7
  41.0 4.2 %collective-permute-done.7 = f32[1,16,256]{2,0,1:T(1,128)S(1)} collective-permute-done((f32[1,16,256]{2,0,1:T(1,128)S(1)}, f32[1,16,256]{2,0,1:T(1,128)S(1)}, u32[]{:S(2)}, u32[]{:S(2)}) %collective-permute-start.7) | collective-permute-done | bytes 16416 | tf_op jit(solution)/shard_map/ppermute | solution.py:36
  45.3 1.9 collective-permute-start.8
  47.2 3.6 %collective-permute-start.9 = (f32[10,1,256]{2,0,1:T(8,128)S(1)}, f32[10,1,256]{2,0,1:T(8,128)S(1)}, u32[]{:S(2)}, u32[]{:S(2)}) collective-permute-start(f32[10,1,256]{2,0,1:T(8,128)S(1)} %get-tuple-element.31), channel_id=1, source_target_pairs={{32,0},{64,32},{96,64},{128,96},{160,128},{192,160},{224,192},{33,... | collective-permute-start | bytes 30728 | tf_op jit(solution)/shard_map/ppermute | solution.py:36
  50.8 1.4 collective-permute-done.9
  52.4 3.8 %collective-permute-start.10 = (f32[10,18,1]{2,0,1:T(8,128)S(1)}, f32[10,18,1]{2,0,1:T(8,128)S(1)}, u32[]{:S(2)}, u32[]{:S(2)}) collective-permute-start(f32[10,18,1]{2,0,1:T(8,128)S(1)} %get-tuple-element.20), channel_id=1, source_target_pairs={{0,1},{1,2},{2,3},{3,4},{4,5},{5,6},{6,7},{7,8},{8,9},{9,10},{10,1... | collective-permute-start | bytes 2168 | tf_op jit(solution)/shard_map/ppermute | solution.py:34
  56.2 1.3 collective-permute-start.11
  57.5 1.3 collective-permute-done.10
  58.9 5.4 %collective-permute-done.11 = f32[10,18,1]{2,0,1:T(8,128)S(1)} collective-permute-done((f32[10,18,1]{2,0,1:T(8,128)S(1)}, f32[10,18,1]{2,0,1:T(8,128)S(1)}, u32[]{:S(2)}, u32[]{:S(2)}) %collective-permute-start.11) | collective-permute-done | bytes 752 | tf_op jit(solution)/shard_map/ppermute | solution.py:36
  67.0 3.1 %collective-permute-start.12 = (f32[1,16,256]{2,0,1:T(1,128)S(1)}, f32[1,16,256]{2,0,1:T(1,128)S(1)}, u32[]{:S(2)}, u32[]{:S(2)}) collective-permute-start(f32[1,16,256]{2,0,1:T(1,128)S(1)} %get-tuple-element.38), channel_id=1, source_target_pairs={{0,256},{256,512},{512,768},{1,257},{257,513},{513,769},{2,258},{2... | collective-permute-start | bytes 49160 | tf_op jit(solution)/shard_map/ppermute | solution.py:34
  71.5 4.2 %collective-permute-done.13 = f32[1,16,256]{2,0,1:T(1,128)S(1)} collective-permute-done((f32[1,16,256]{2,0,1:T(1,128)S(1)}, f32[1,16,256]{2,0,1:T(1,128)S(1)}, u32[]{:S(2)}, u32[]{:S(2)}) %collective-permute-start.13) | collective-permute-done | bytes 16416 | tf_op jit(solution)/shard_map/ppermute | solution.py:36
  75.7 1.9 collective-permute-start.14
  77.7 3.6 %collective-permute-start.15 = (f32[10,1,256]{2,0,1:T(8,128)S(1)}, f32[10,1,256]{2,0,1:T(8,128)S(1)}, u32[]{:S(2)}, u32[]{:S(2)}) collective-permute-start(f32[10,1,256]{2,0,1:T(8,128)S(1)} %get-tuple-element.29), channel_id=1, source_target_pairs={{32,0},{64,32},{96,64},{128,96},{160,128},{192,160},{224,192},{33,... | collective-permute-start | bytes 30728 | tf_op jit(solution)/shard_map/ppermute | solution.py:36
  81.3 1.4 collective-permute-done.15
  82.9 5.1 %collective-permute-start.16 = (f32[10,18,1]{2,0,1:T(8,128)S(1)}, f32[10,18,1]{2,0,1:T(8,128)S(1)}, u32[]{:S(2)}, u32[]{:S(2)}) collective-permute-start(f32[10,18,1]{2,0,1:T(8,128)S(1)} %get-tuple-element.18), channel_id=1, source_target_pairs={{0,1},{1,2},{2,3},{3,4},{4,5},{5,6},{6,7},{7,8},{8,9},{9,10},{10,1... | collective-permute-start | bytes 2168 | tf_op jit(solution)/shard_map/ppermute | solution.py:34
  89.3 1.3 collective-permute-done.16
  90.7 4.4 %collective-permute-done.17 = f32[10,18,1]{2,0,1:T(8,128)S(1)} collective-permute-done((f32[10,18,1]{2,0,1:T(8,128)S(1)}, f32[10,18,1]{2,0,1:T(8,128)S(1)}, u32[]{:S(2)}, u32[]{:S(2)}) %collective-permute-start.17) | collective-permute-done | bytes 752 | tf_op jit(solution)/shard_map/ppermute | solution.py:36
  97.8 1.9 collective-permute-start.18
  101.1 4.2 %collective-permute-done.19 = f32[1,16,256]{2,0,1:T(1,128)S(1)} collective-permute-done((f32[1,16,256]{2,0,1:T(1,128)S(1)}, f32[1,16,256]{2,0,1:T(1,128)S(1)}, u32[]{:S(2)}, u32[]{:S(2)}) %collective-permute-start.19) | collective-permute-done | bytes 16416 | tf_op jit(solution)/shard_map/ppermute | solution.py:36
  105.4 1.9 collective-permute-start.20
  107.3 3.6 %collective-permute-start.21 = (f32[10,1,256]{2,0,1:T(8,128)S(1)}, f32[10,1,256]{2,0,1:T(8,128)S(1)}, u32[]{:S(2)}, u32[]{:S(2)}) collective-permute-start(f32[10,1,256]{2,0,1:T(8,128)S(1)} %get-tuple-element.27), channel_id=1, source_target_pairs={{32,0},{64,32},{96,64},{128,96},{160,128},{192,160},{224,192},{33,... | collective-permute-start | bytes 30728 | tf_op jit(solution)/shard_map/ppermute | solution.py:36
  111.0 1.4 collective-permute-done.21
  112.5 3.9 %collective-permute-start.22 = (f32[10,18,1]{2,0,1:T(8,128)S(1)}, f32[10,18,1]{2,0,1:T(8,128)S(1)}, u32[]{:S(2)}, u32[]{:S(2)}) collective-permute-start(f32[10,18,1]{2,0,1:T(8,128)S(1)} %get-tuple-element.16), channel_id=1, source_target_pairs={{0,1},{1,2},{2,3},{3,4},{4,5},{5,6},{6,7},{7,8},{8,9},{9,10},{10,1... | collective-permute-start | bytes 2168 | tf_op jit(solution)/shard_map/ppermute | solution.py:34
  116.5 1.3 collective-permute-start.23
  117.8 1.3 collective-permute-done.22
  119.1 4.4 %collective-permute-done.23 = f32[10,18,1]{2,0,1:T(8,128)S(1)} collective-permute-done((f32[10,18,1]{2,0,1:T(8,128)S(1)}, f32[10,18,1]{2,0,1:T(8,128)S(1)}, u32[]{:S(2)}, u32[]{:S(2)}) %collective-permute-start.23) | collective-permute-done | bytes 752 | tf_op jit(solution)/shard_map/ppermute | solution.py:36
  126.2 1.9 collective-permute-start.24
  129.5 4.2 %collective-permute-done.25 = f32[1,16,256]{2,0,1:T(1,128)S(1)} collective-permute-done((f32[1,16,256]{2,0,1:T(1,128)S(1)}, f32[1,16,256]{2,0,1:T(1,128)S(1)}, u32[]{:S(2)}, u32[]{:S(2)}) %collective-permute-start.25) | collective-permute-done | bytes 16416 | tf_op jit(solution)/shard_map/ppermute | solution.py:36
  133.7 1.9 collective-permute-start.26
  135.7 3.6 %collective-permute-start.27 = (f32[10,1,256]{2,0,1:T(8,128)S(1)}, f32[10,1,256]{2,0,1:T(8,128)S(1)}, u32[]{:S(2)}, u32[]{:S(2)}) collective-permute-start(f32[10,1,256]{2,0,1:T(8,128)S(1)} %get-tuple-element.25), channel_id=1, source_target_pairs={{32,0},{64,32},{96,64},{128,96},{160,128},{192,160},{224,192},{33,... | collective-permute-start | bytes 30728 | tf_op jit(solution)/shard_map/ppermute | solution.py:36
  139.3 1.4 collective-permute-done.27
  140.9 4.8 %collective-permute-start.28 = (f32[10,18,1]{2,0,1:T(8,128)S(1)}, f32[10,18,1]{2,0,1:T(8,128)S(1)}, u32[]{:S(2)}, u32[]{:S(2)}) collective-permute-start(f32[10,18,1]{2,0,1:T(8,128)S(1)} %get-tuple-element.14), channel_id=1, source_target_pairs={{0,1},{1,2},{2,3},{3,4},{4,5},{5,6},{6,7},{7,8},{8,9},{9,10},{10,1... | collective-permute-start | bytes 2168 | tf_op jit(solution)/shard_map/ppermute | solution.py:34
  147.0 1.3 collective-permute-done.28
  148.3 4.4 %collective-permute-done.29 = f32[10,18,1]{2,0,1:T(8,128)S(1)} collective-permute-done((f32[10,18,1]{2,0,1:T(8,128)S(1)}, f32[10,18,1]{2,0,1:T(8,128)S(1)}, u32[]{:S(2)}, u32[]{:S(2)}) %collective-permute-start.29) | collective-permute-done | bytes 752 | tf_op jit(solution)/shard_map/ppermute | solution.py:36
  154.8 1.9 collective-permute-start.30
  157.9 4.6 %collective-permute-start.31 = (f32[8192]{0:T(1024)S(1)}, f32[8192]{0:T(1024)S(1)}, u32[]{:S(2)}, u32[]{:S(2)}) collective-permute-start(f32[8192]{0:T(1024)S(1)} %add.337), channel_id=1, source_target_pairs={{0,64},{32,96},{64,0},{96,32},{128,192},{160,224},{192,128},{224,1... | collective-permute-start | bytes 98312 | tf_op jit(solution)/shard_map/ppermute | solution.py:48
  162.5 1.9 collective-permute-done.31
  164.4 6.7 %collective-permute-start.32 = (f32[8192]{0:T(1024)S(1)}, f32[8192]{0:T(1024)S(1)}, u32[]{:S(2)}, u32[]{:S(2)}) collective-permute-start(f32[8192]{0:T(1024)S(1)} %add.338), channel_id=1, source_target_pairs={{0,128},{32,160},{64,192},{96,224},{128,0},{160,32},{192,64},{224,... | collective-permute-start | bytes 98312 | tf_op jit(solution)/shard_map/ppermute | solution.py:48
  171.1 1.9 collective-permute-done.32
  173.0 5.1 %collective-permute-start.33 = (f32[8192]{0:T(1024)S(1)}, f32[8192]{0:T(1024)S(1)}, u32[]{:S(2)}, u32[]{:S(2)}) collective-permute-start(f32[8192]{0:T(1024)S(1)} %add.339), channel_id=1, source_target_pairs={{0,1},{1,0},{2,3},{3,2},{4,5},{5,4},{6,7},{7,6},{8,9},{9,8},{10,11... | collective-permute-start | bytes 98312 | tf_op jit(solution)/shard_map/ppermute | solution.py:48
  178.1 1.9 collective-permute-done.33
  180.0 5.1 %collective-permute-start.34 = (f32[8192]{0:T(1024)S(1)}, f32[8192]{0:T(1024)S(1)}, u32[]{:S(2)}, u32[]{:S(2)}) collective-permute-start(f32[8192]{0:T(1024)S(1)} %add.340), channel_id=1, source_target_pairs={{0,2},{1,3},{2,0},{3,1},{4,6},{5,7},{6,4},{7,5},{8,10},{9,11},{10,... | collective-permute-start | bytes 98312 | tf_op jit(solution)/shard_map/ppermute | solution.py:48
  185.1 1.9 collective-permute-done.34
  187.0 9.1 %collective-permute-start.35 = (f32[8192]{0:T(1024)S(1)}, f32[8192]{0:T(1024)S(1)}, u32[]{:S(2)}, u32[]{:S(2)}) collective-permute-start(f32[8192]{0:T(1024)S(1)} %add.341), channel_id=1, source_target_pairs={{0,4},{1,5},{2,6},{3,7},{4,0},{5,1},{6,2},{7,3},{8,12},{9,13},{10,... | collective-permute-start | bytes 98312 | tf_op jit(solution)/shard_map/ppermute | solution.py:48
  196.1 1.9 collective-permute-done.35
  197.9 14.5 %collective-permute-start.36 = (f32[8192]{0:T(1024)S(1)}, f32[8192]{0:T(1024)S(1)}, u32[]{:S(2)}, u32[]{:S(2)}) collective-permute-start(f32[8192]{0:T(1024)S(1)} %add.342), channel_id=1, source_target_pairs={{0,8},{1,9},{2,10},{3,11},{4,12},{5,13},{6,14},{7,15},{8,0},{9,1},... | collective-permute-start | bytes 98312 | tf_op jit(solution)/shard_map/ppermute | solution.py:48
  212.5 2.2 collective-permute-done.36
  214.7 17.2 %collective-permute-start.37 = (f32[8192]{0:T(1024)S(1)}, f32[8192]{0:T(1024)S(1)}, u32[]{:S(2)}, u32[]{:S(2)}) collective-permute-start(f32[8192]{0:T(1024)S(1)} %add.343), channel_id=1, source_target_pairs={{0,16},{1,17},{2,18},{3,19},{4,20},{5,21},{6,22},{7,23},{8,24},{9,... | collective-permute-start | bytes 98312 | tf_op jit(solution)/shard_map/ppermute | solution.py:48
  232.0 6.9 %collective-permute-done.37 = f32[8192]{0:T(1024)S(1)} collective-permute-done((f32[8192]{0:T(1024)S(1)}, f32[8192]{0:T(1024)S(1)}, u32[]{:S(2)}, u32[]{:S(2)}) %collective-permute-start.37) | collective-permute-done | bytes 32800 | tf_op jit(solution)/shard_map/ppermute | solution.py:48
  238.9 1.9 collective-permute-start.38
  240.8 3.9 %collective-permute-done.38 = f32[8192]{0:T(1024)S(1)} collective-permute-done((f32[8192]{0:T(1024)S(1)}, f32[8192]{0:T(1024)S(1)}, u32[]{:S(2)}, u32[]{:S(2)}) %collective-permute-start.38) | collective-permute-done | bytes 32800 | tf_op jit(solution)/shard_map/ppermute | solution.py:48
  244.7 2.0 collective-permute-start.39
  246.6 5.3 %collective-permute-done.39 = f32[8192]{0:T(1024)S(1)} collective-permute-done((f32[8192]{0:T(1024)S(1)}, f32[8192]{0:T(1024)S(1)}, u32[]{:S(2)}, u32[]{:S(2)}) %collective-permute-start.39) | collective-permute-done | bytes 32800 | tf_op jit(solution)/shard_map/ppermute | solution.py:48
  (137 shorter events, 29.3 us)
Async XLA Ops:
  0.6 153.8 %copy-start = (f32[8,8192]{1,0:T(8,128)S(1)}, f32[8,8192]{1,0:T(8,128)}, u32[]{:S(2)}) copy-start(f32[8,8192]{1,0:T(8,128)} %param.13) | copy-start | bytes 786436
  0.6 0.7 copy-start.9
  0.7 0.7 copy-start.7
  0.7 0.7 copy-start.8
  0.7 1.7 copy-start.10
  0.7 1.7 copy-start.1
  2.4 0.7 copy-start.11
  3.1 0.7 copy-start.12
  4.2 4.8 %collective-permute-start = (f32[1,16,256]{2,0,1:T(1,128)S(1)}, f32[1,16,256]{2,0,1:T(1,128)S(1)}, u32[]{:S(2)}, u32[]{:S(2)}) collective-permute-start(f32[1,16,256]{2,0,1:T(1,128)S(1)} %get-tuple-element.42), channel_id=1, source_target_pairs={{0,256},{256,512},{512,768},{1,257},{257,513},{513,769},{2,258},{2... | collective-permute-start | bytes 49160 | tf_op jit(solution)/shard_map/ppermute | solution.py:34
  7.6 5.6 %collective-permute-start.1 = (f32[1,16,256]{2,0,1:T(1,128)S(1)}, f32[1,16,256]{2,0,1:T(1,128)S(1)}, u32[]{:S(2)}, u32[]{:S(2)}) collective-permute-start(f32[1,16,256]{2,0,1:T(1,128)S(1)} %get-tuple-element.43), channel_id=1, source_target_pairs={{256,0},{512,256},{768,512},{257,1},{513,257},{769,513},{258,2},{5... | collective-permute-start | bytes 49160 | tf_op jit(solution)/shard_map/ppermute | solution.py:36
  13.2 5.6 %collective-permute-start.2 = (f32[10,1,256]{2,0,1:T(8,128)S(1)}, f32[10,1,256]{2,0,1:T(8,128)S(1)}, u32[]{:S(2)}, u32[]{:S(2)}) collective-permute-start(f32[10,1,256]{2,0,1:T(8,128)S(1)} %get-tuple-element.32), channel_id=1, source_target_pairs={{0,32},{32,64},{64,96},{96,128},{128,160},{160,192},{192,224},{1,3... | collective-permute-start | bytes 30728 | tf_op jit(solution)/shard_map/ppermute | solution.py:34
  15.1 5.1 %collective-permute-start.3 = (f32[10,1,256]{2,0,1:T(8,128)S(1)}, f32[10,1,256]{2,0,1:T(8,128)S(1)}, u32[]{:S(2)}, u32[]{:S(2)}) collective-permute-start(f32[10,1,256]{2,0,1:T(8,128)S(1)} %get-tuple-element.33), channel_id=1, source_target_pairs={{32,0},{64,32},{96,64},{128,96},{160,128},{192,160},{224,192},{33,... | collective-permute-start | bytes 30728 | tf_op jit(solution)/shard_map/ppermute | solution.py:36
  20.4 6.5 %collective-permute-start.4 = (f32[10,18,1]{2,0,1:T(8,128)S(1)}, f32[10,18,1]{2,0,1:T(8,128)S(1)}, u32[]{:S(2)}, u32[]{:S(2)}) collective-permute-start(f32[10,18,1]{2,0,1:T(8,128)S(1)} %get-tuple-element.22), channel_id=1, source_target_pairs={{0,1},{1,2},{2,3},{3,4},{4,5},{5,6},{6,7},{7,8},{8,9},{9,10},{10,1... | collective-permute-start | bytes 2168 | tf_op jit(solution)/shard_map/ppermute | solution.py:34
  24.2 7.0 %collective-permute-start.5 = (f32[10,18,1]{2,0,1:T(8,128)S(1)}, f32[10,18,1]{2,0,1:T(8,128)S(1)}, u32[]{:S(2)}, u32[]{:S(2)}) collective-permute-start(f32[10,18,1]{2,0,1:T(8,128)S(1)} %get-tuple-element.23), channel_id=1, source_target_pairs={{1,0},{2,1},{3,2},{4,3},{5,4},{6,5},{7,6},{8,7},{9,8},{10,9},{11,1... | collective-permute-start | bytes 2168 | tf_op jit(solution)/shard_map/ppermute | solution.py:36
  31.7 0.9 copy-start.3
  32.6 0.8 copy-start.2
  33.7 0.7 copy-start.4
  34.9 0.7 copy-start.6
  36.2 4.8 %collective-permute-start.6 = (f32[1,16,256]{2,0,1:T(1,128)S(1)}, f32[1,16,256]{2,0,1:T(1,128)S(1)}, u32[]{:S(2)}, u32[]{:S(2)}) collective-permute-start(f32[1,16,256]{2,0,1:T(1,128)S(1)} %get-tuple-element.40), channel_id=1, source_target_pairs={{0,256},{256,512},{512,768},{1,257},{257,513},{513,769},{2,258},{2... | collective-permute-start | bytes 49160 | tf_op jit(solution)/shard_map/ppermute | solution.py:34
  39.6 5.6 %collective-permute-start.7 = (f32[1,16,256]{2,0,1:T(1,128)S(1)}, f32[1,16,256]{2,0,1:T(1,128)S(1)}, u32[]{:S(2)}, u32[]{:S(2)}) collective-permute-start(f32[1,16,256]{2,0,1:T(1,128)S(1)} %get-tuple-element.41), channel_id=1, source_target_pairs={{256,0},{512,256},{768,512},{257,1},{513,257},{769,513},{258,2},{5... | collective-permute-start | bytes 49160 | tf_op jit(solution)/shard_map/ppermute | solution.py:36
  45.3 5.6 %collective-permute-start.8 = (f32[10,1,256]{2,0,1:T(8,128)S(1)}, f32[10,1,256]{2,0,1:T(8,128)S(1)}, u32[]{:S(2)}, u32[]{:S(2)}) collective-permute-start(f32[10,1,256]{2,0,1:T(8,128)S(1)} %get-tuple-element.30), channel_id=1, source_target_pairs={{0,32},{32,64},{64,96},{96,128},{128,160},{160,192},{192,224},{1,3... | collective-permute-start | bytes 30728 | tf_op jit(solution)/shard_map/ppermute | solution.py:34
  47.2 5.1 %collective-permute-start.9 = (f32[10,1,256]{2,0,1:T(8,128)S(1)}, f32[10,1,256]{2,0,1:T(8,128)S(1)}, u32[]{:S(2)}, u32[]{:S(2)}) collective-permute-start(f32[10,1,256]{2,0,1:T(8,128)S(1)} %get-tuple-element.31), channel_id=1, source_target_pairs={{32,0},{64,32},{96,64},{128,96},{160,128},{192,160},{224,192},{33,... | collective-permute-start | bytes 30728 | tf_op jit(solution)/shard_map/ppermute | solution.py:36
  52.4 6.5 %collective-permute-start.10 = (f32[10,18,1]{2,0,1:T(8,128)S(1)}, f32[10,18,1]{2,0,1:T(8,128)S(1)}, u32[]{:S(2)}, u32[]{:S(2)}) collective-permute-start(f32[10,18,1]{2,0,1:T(8,128)S(1)} %get-tuple-element.20), channel_id=1, source_target_pairs={{0,1},{1,2},{2,3},{3,4},{4,5},{5,6},{6,7},{7,8},{8,9},{9,10},{10,1... | collective-permute-start | bytes 2168 | tf_op jit(solution)/shard_map/ppermute | solution.py:34
  56.2 8.0 %collective-permute-start.11 = (f32[10,18,1]{2,0,1:T(8,128)S(1)}, f32[10,18,1]{2,0,1:T(8,128)S(1)}, u32[]{:S(2)}, u32[]{:S(2)}) collective-permute-start(f32[10,18,1]{2,0,1:T(8,128)S(1)} %get-tuple-element.21), channel_id=1, source_target_pairs={{1,0},{2,1},{3,2},{4,3},{5,4},{6,5},{7,6},{8,7},{9,8},{10,9},{11,1... | collective-permute-start | bytes 2168 | tf_op jit(solution)/shard_map/ppermute | solution.py:36
  67.0 4.5 %collective-permute-start.12 = (f32[1,16,256]{2,0,1:T(1,128)S(1)}, f32[1,16,256]{2,0,1:T(1,128)S(1)}, u32[]{:S(2)}, u32[]{:S(2)}) collective-permute-start(f32[1,16,256]{2,0,1:T(1,128)S(1)} %get-tuple-element.38), channel_id=1, source_target_pairs={{0,256},{256,512},{512,768},{1,257},{257,513},{513,769},{2,258},{2... | collective-permute-start | bytes 49160 | tf_op jit(solution)/shard_map/ppermute | solution.py:34
  70.1 5.6 %collective-permute-start.13 = (f32[1,16,256]{2,0,1:T(1,128)S(1)}, f32[1,16,256]{2,0,1:T(1,128)S(1)}, u32[]{:S(2)}, u32[]{:S(2)}) collective-permute-start(f32[1,16,256]{2,0,1:T(1,128)S(1)} %get-tuple-element.39), channel_id=1, source_target_pairs={{256,0},{512,256},{768,512},{257,1},{513,257},{769,513},{258,2},{5... | collective-permute-start | bytes 49160 | tf_op jit(solution)/shard_map/ppermute | solution.py:36
  75.7 5.6 %collective-permute-start.14 = (f32[10,1,256]{2,0,1:T(8,128)S(1)}, f32[10,1,256]{2,0,1:T(8,128)S(1)}, u32[]{:S(2)}, u32[]{:S(2)}) collective-permute-start(f32[10,1,256]{2,0,1:T(8,128)S(1)} %get-tuple-element.28), channel_id=1, source_target_pairs={{0,32},{32,64},{64,96},{96,128},{128,160},{160,192},{192,224},{1,3... | collective-permute-start | bytes 30728 | tf_op jit(solution)/shard_map/ppermute | solution.py:34
  77.7 5.1 %collective-permute-start.15 = (f32[10,1,256]{2,0,1:T(8,128)S(1)}, f32[10,1,256]{2,0,1:T(8,128)S(1)}, u32[]{:S(2)}, u32[]{:S(2)}) collective-permute-start(f32[10,1,256]{2,0,1:T(8,128)S(1)} %get-tuple-element.29), channel_id=1, source_target_pairs={{32,0},{64,32},{96,64},{128,96},{160,128},{192,160},{224,192},{33,... | collective-permute-start | bytes 30728 | tf_op jit(solution)/shard_map/ppermute | solution.py:36
  82.9 7.8 %collective-permute-start.16 = (f32[10,18,1]{2,0,1:T(8,128)S(1)}, f32[10,18,1]{2,0,1:T(8,128)S(1)}, u32[]{:S(2)}, u32[]{:S(2)}) collective-permute-start(f32[10,18,1]{2,0,1:T(8,128)S(1)} %get-tuple-element.18), channel_id=1, source_target_pairs={{0,1},{1,2},{2,3},{3,4},{4,5},{5,6},{6,7},{7,8},{8,9},{9,10},{10,1... | collective-permute-start | bytes 2168 | tf_op jit(solution)/shard_map/ppermute | solution.py:34
  88.0 7.0 %collective-permute-start.17 = (f32[10,18,1]{2,0,1:T(8,128)S(1)}, f32[10,18,1]{2,0,1:T(8,128)S(1)}, u32[]{:S(2)}, u32[]{:S(2)}) collective-permute-start(f32[10,18,1]{2,0,1:T(8,128)S(1)} %get-tuple-element.19), channel_id=1, source_target_pairs={{1,0},{2,1},{3,2},{4,3},{5,4},{6,5},{7,6},{8,7},{9,8},{10,9},{11,1... | collective-permute-start | bytes 2168 | tf_op jit(solution)/shard_map/ppermute | solution.py:36
  97.8 3.4 %collective-permute-start.18 = (f32[1,16,256]{2,0,1:T(1,128)S(1)}, f32[1,16,256]{2,0,1:T(1,128)S(1)}, u32[]{:S(2)}, u32[]{:S(2)}) collective-permute-start(f32[1,16,256]{2,0,1:T(1,128)S(1)} %get-tuple-element.36), channel_id=1, source_target_pairs={{0,256},{256,512},{512,768},{1,257},{257,513},{513,769},{2,258},{2... | collective-permute-start | bytes 49160 | tf_op jit(solution)/shard_map/ppermute | solution.py:34
  99.7 5.6 %collective-permute-start.19 = (f32[1,16,256]{2,0,1:T(1,128)S(1)}, f32[1,16,256]{2,0,1:T(1,128)S(1)}, u32[]{:S(2)}, u32[]{:S(2)}) collective-permute-start(f32[1,16,256]{2,0,1:T(1,128)S(1)} %get-tuple-element.37), channel_id=1, source_target_pairs={{256,0},{512,256},{768,512},{257,1},{513,257},{769,513},{258,2},{5... | collective-permute-start | bytes 49160 | tf_op jit(solution)/shard_map/ppermute | solution.py:36
  105.4 5.6 %collective-permute-start.20 = (f32[10,1,256]{2,0,1:T(8,128)S(1)}, f32[10,1,256]{2,0,1:T(8,128)S(1)}, u32[]{:S(2)}, u32[]{:S(2)}) collective-permute-start(f32[10,1,256]{2,0,1:T(8,128)S(1)} %get-tuple-element.26), channel_id=1, source_target_pairs={{0,32},{32,64},{64,96},{96,128},{128,160},{160,192},{192,224},{1,3... | collective-permute-start | bytes 30728 | tf_op jit(solution)/shard_map/ppermute | solution.py:34
  107.3 5.1 %collective-permute-start.21 = (f32[10,1,256]{2,0,1:T(8,128)S(1)}, f32[10,1,256]{2,0,1:T(8,128)S(1)}, u32[]{:S(2)}, u32[]{:S(2)}) collective-permute-start(f32[10,1,256]{2,0,1:T(8,128)S(1)} %get-tuple-element.27), channel_id=1, source_target_pairs={{32,0},{64,32},{96,64},{128,96},{160,128},{192,160},{224,192},{33,... | collective-permute-start | bytes 30728 | tf_op jit(solution)/shard_map/ppermute | solution.py:36
  112.5 6.6 %collective-permute-start.22 = (f32[10,18,1]{2,0,1:T(8,128)S(1)}, f32[10,18,1]{2,0,1:T(8,128)S(1)}, u32[]{:S(2)}, u32[]{:S(2)}) collective-permute-start(f32[10,18,1]{2,0,1:T(8,128)S(1)} %get-tuple-element.16), channel_id=1, source_target_pairs={{0,1},{1,2},{2,3},{3,4},{4,5},{5,6},{6,7},{7,8},{8,9},{9,10},{10,1... | collective-permute-start | bytes 2168 | tf_op jit(solution)/shard_map/ppermute | solution.py:34
  116.5 7.0 %collective-permute-start.23 = (f32[10,18,1]{2,0,1:T(8,128)S(1)}, f32[10,18,1]{2,0,1:T(8,128)S(1)}, u32[]{:S(2)}, u32[]{:S(2)}) collective-permute-start(f32[10,18,1]{2,0,1:T(8,128)S(1)} %get-tuple-element.17), channel_id=1, source_target_pairs={{1,0},{2,1},{3,2},{4,3},{5,4},{6,5},{7,6},{8,7},{9,8},{10,9},{11,1... | collective-permute-start | bytes 2168 | tf_op jit(solution)/shard_map/ppermute | solution.py:36
  126.2 3.4 %collective-permute-start.24 = (f32[1,16,256]{2,0,1:T(1,128)S(1)}, f32[1,16,256]{2,0,1:T(1,128)S(1)}, u32[]{:S(2)}, u32[]{:S(2)}) collective-permute-start(f32[1,16,256]{2,0,1:T(1,128)S(1)} %get-tuple-element.34), channel_id=1, source_target_pairs={{0,256},{256,512},{512,768},{1,257},{257,513},{513,769},{2,258},{2... | collective-permute-start | bytes 49160 | tf_op jit(solution)/shard_map/ppermute | solution.py:34
  128.1 5.6 %collective-permute-start.25 = (f32[1,16,256]{2,0,1:T(1,128)S(1)}, f32[1,16,256]{2,0,1:T(1,128)S(1)}, u32[]{:S(2)}, u32[]{:S(2)}) collective-permute-start(f32[1,16,256]{2,0,1:T(1,128)S(1)} %get-tuple-element.35), channel_id=1, source_target_pairs={{256,0},{512,256},{768,512},{257,1},{513,257},{769,513},{258,2},{5... | collective-permute-start | bytes 49160 | tf_op jit(solution)/shard_map/ppermute | solution.py:36
  133.7 5.6 %collective-permute-start.26 = (f32[10,1,256]{2,0,1:T(8,128)S(1)}, f32[10,1,256]{2,0,1:T(8,128)S(1)}, u32[]{:S(2)}, u32[]{:S(2)}) collective-permute-start(f32[10,1,256]{2,0,1:T(8,128)S(1)} %get-tuple-element.24), channel_id=1, source_target_pairs={{0,32},{32,64},{64,96},{96,128},{128,160},{160,192},{192,224},{1,3... | collective-permute-start | bytes 30728 | tf_op jit(solution)/shard_map/ppermute | solution.py:34
  135.7 5.1 %collective-permute-start.27 = (f32[10,1,256]{2,0,1:T(8,128)S(1)}, f32[10,1,256]{2,0,1:T(8,128)S(1)}, u32[]{:S(2)}, u32[]{:S(2)}) collective-permute-start(f32[10,1,256]{2,0,1:T(8,128)S(1)} %get-tuple-element.25), channel_id=1, source_target_pairs={{32,0},{64,32},{96,64},{128,96},{160,128},{192,160},{224,192},{33,... | collective-permute-start | bytes 30728 | tf_op jit(solution)/shard_map/ppermute | solution.py:36
  140.9 7.4 %collective-permute-start.28 = (f32[10,18,1]{2,0,1:T(8,128)S(1)}, f32[10,18,1]{2,0,1:T(8,128)S(1)}, u32[]{:S(2)}, u32[]{:S(2)}) collective-permute-start(f32[10,18,1]{2,0,1:T(8,128)S(1)} %get-tuple-element.14), channel_id=1, source_target_pairs={{0,1},{1,2},{2,3},{3,4},{4,5},{5,6},{6,7},{7,8},{8,9},{9,10},{10,1... | collective-permute-start | bytes 2168 | tf_op jit(solution)/shard_map/ppermute | solution.py:34
  145.7 7.0 %collective-permute-start.29 = (f32[10,18,1]{2,0,1:T(8,128)S(1)}, f32[10,18,1]{2,0,1:T(8,128)S(1)}, u32[]{:S(2)}, u32[]{:S(2)}) collective-permute-start(f32[10,18,1]{2,0,1:T(8,128)S(1)} %get-tuple-element.15), channel_id=1, source_target_pairs={{1,0},{2,1},{3,2},{4,3},{5,4},{6,5},{7,6},{8,7},{9,8},{10,9},{11,1... | collective-permute-start | bytes 2168 | tf_op jit(solution)/shard_map/ppermute | solution.py:36
  153.1 0.9 copy-start.5
  154.8 3.1 %collective-permute-start.30 = (f32[8192]{0:T(1024)S(1)}, f32[8192]{0:T(1024)S(1)}, u32[]{:S(2)}, u32[]{:S(2)}) collective-permute-start(f32[8192]{0:T(1024)S(1)} %bitcast.142), channel_id=1, source_target_pairs={{0,32},{32,0},{64,96},{96,64},{128,160},{160,128},{192,224},{224,1... | collective-permute-start | bytes 98312 | tf_op jit(solution)/shard_map/ppermute | solution.py:48
  157.9 6.5 %collective-permute-start.31 = (f32[8192]{0:T(1024)S(1)}, f32[8192]{0:T(1024)S(1)}, u32[]{:S(2)}, u32[]{:S(2)}) collective-permute-start(f32[8192]{0:T(1024)S(1)} %add.337), channel_id=1, source_target_pairs={{0,64},{32,96},{64,0},{96,32},{128,192},{160,224},{192,128},{224,1... | collective-permute-start | bytes 98312 | tf_op jit(solution)/shard_map/ppermute | solution.py:48
  164.4 8.6 %collective-permute-start.32 = (f32[8192]{0:T(1024)S(1)}, f32[8192]{0:T(1024)S(1)}, u32[]{:S(2)}, u32[]{:S(2)}) collective-permute-start(f32[8192]{0:T(1024)S(1)} %add.338), channel_id=1, source_target_pairs={{0,128},{32,160},{64,192},{96,224},{128,0},{160,32},{192,64},{224,... | collective-permute-start | bytes 98312 | tf_op jit(solution)/shard_map/ppermute | solution.py:48
  173.0 7.0 %collective-permute-start.33 = (f32[8192]{0:T(1024)S(1)}, f32[8192]{0:T(1024)S(1)}, u32[]{:S(2)}, u32[]{:S(2)}) collective-permute-start(f32[8192]{0:T(1024)S(1)} %add.339), channel_id=1, source_target_pairs={{0,1},{1,0},{2,3},{3,2},{4,5},{5,4},{6,7},{7,6},{8,9},{9,8},{10,11... | collective-permute-start | bytes 98312 | tf_op jit(solution)/shard_map/ppermute | solution.py:48
  180.0 7.0 %collective-permute-start.34 = (f32[8192]{0:T(1024)S(1)}, f32[8192]{0:T(1024)S(1)}, u32[]{:S(2)}, u32[]{:S(2)}) collective-permute-start(f32[8192]{0:T(1024)S(1)} %add.340), channel_id=1, source_target_pairs={{0,2},{1,3},{2,0},{3,1},{4,6},{5,7},{6,4},{7,5},{8,10},{9,11},{10,... | collective-permute-start | bytes 98312 | tf_op jit(solution)/shard_map/ppermute | solution.py:48
  187.0 11.0 %collective-permute-start.35 = (f32[8192]{0:T(1024)S(1)}, f32[8192]{0:T(1024)S(1)}, u32[]{:S(2)}, u32[]{:S(2)}) collective-permute-start(f32[8192]{0:T(1024)S(1)} %add.341), channel_id=1, source_target_pairs={{0,4},{1,5},{2,6},{3,7},{4,0},{5,1},{6,2},{7,3},{8,12},{9,13},{10,... | collective-permute-start | bytes 98312 | tf_op jit(solution)/shard_map/ppermute | solution.py:48
  197.9 16.8 %collective-permute-start.36 = (f32[8192]{0:T(1024)S(1)}, f32[8192]{0:T(1024)S(1)}, u32[]{:S(2)}, u32[]{:S(2)}) collective-permute-start(f32[8192]{0:T(1024)S(1)} %add.342), channel_id=1, source_target_pairs={{0,8},{1,9},{2,10},{3,11},{4,12},{5,13},{6,14},{7,15},{8,0},{9,1},... | collective-permute-start | bytes 98312 | tf_op jit(solution)/shard_map/ppermute | solution.py:48
  214.7 24.1 %collective-permute-start.37 = (f32[8192]{0:T(1024)S(1)}, f32[8192]{0:T(1024)S(1)}, u32[]{:S(2)}, u32[]{:S(2)}) collective-permute-start(f32[8192]{0:T(1024)S(1)} %add.343), channel_id=1, source_target_pairs={{0,16},{1,17},{2,18},{3,19},{4,20},{5,21},{6,22},{7,23},{8,24},{9,... | collective-permute-start | bytes 98312 | tf_op jit(solution)/shard_map/ppermute | solution.py:48
  238.9 5.8 %collective-permute-start.38 = (f32[8192]{0:T(1024)S(1)}, f32[8192]{0:T(1024)S(1)}, u32[]{:S(2)}, u32[]{:S(2)}) collective-permute-start(f32[8192]{0:T(1024)S(1)} %add.344), channel_id=1, source_target_pairs={{0,256},{256,0},{512,768},{768,512},{1,257},{257,1},{513,769},{769... | collective-permute-start | bytes 98312 | tf_op jit(solution)/shard_map/ppermute | solution.py:48
  244.7 7.3 %collective-permute-start.39 = (f32[8192]{0:T(1024)S(1)}, f32[8192]{0:T(1024)S(1)}, u32[]{:S(2)}, u32[]{:S(2)}) collective-permute-start(f32[8192]{0:T(1024)S(1)} %add.345), channel_id=1, source_target_pairs={{0,512},{256,768},{512,0},{768,256},{1,513},{257,769},{513,1},{769... | collective-permute-start | bytes 98312 | tf_op jit(solution)/shard_map/ppermute | solution.py:48
  252.7 0.5 copy-start.13

commit v2 on v1

--- a/solution.py
+++ b/solution.py
@@ -29,12 +29,10 @@
         ends = count - 1
         head = lax.slice_in_dim(cells, 0, width, axis=dim)
         tail = lax.slice_in_dim(cells, cells.shape[dim] - width, cells.shape[dim], axis=dim)
+        from_prev = lax.ppermute(jnp.squeeze(tail, dim), axis, [(i, i + 1) for i in range(ends)])
+        from_next = lax.ppermute(jnp.squeeze(head, dim), axis, [(i + 1, i) for i in range(ends)])
         cells = jnp.concatenate(
-            [
-                lax.ppermute(tail, axis, [(i, (i + 1) % count) for i in range(ends)]),
-                cells,
-                lax.ppermute(head, axis, [((i + 1) % count, i) for i in range(ends)]),
-            ],
+            [jnp.expand_dims(from_prev, dim), cells, jnp.expand_dims(from_next, dim)],
             axis=dim,
         )
     return cells
@@ -112,7 +110,7 @@
 
 def assemble(field, points):
     size_x, size_y, size_z = field.shape
-    padded = padded_2(field, (("gx", 0), ("gy", 1), ("gz", 2)), 1)
+    padded = padded_2(field, (("gz", 2), ("gy", 1), ("gx", 0)), 1)
     summed = combine(padded, 0, size_x, points)
     summed = combine(summed, 1, size_y, points)
     summed = combine(summed, 2, size_z, points)

time: 258 us -> 250 us (0.969)
  waiting for transfers between devices: 87.3 us -> 73.1 us
  starting transfers between devices: 144 us -> 150 us
  local copies, waits for them, and re-layouts: 6.52 us -> 9.34 us
    ppermute x30, waiting for transfers between devices: 58.4 us -> 45.1 us  [the longest x15 41 us: padded_2(): lax.ppermute(jnp.squeeze(head, dim), axis, [(i + 1, i) for i in range(end...]
    ppermute x30, starting transfers between devices: 76 us -> 81.9 us  [the longest x15 50.6 us: padded_2(): lax.ppermute(jnp.squeeze(tail, dim), axis, [(i, i + 1) for i in range(end...]
  transfers between devices with their start and end apart: 40 -> 40, of which waited for: 35 -> 29; matrix products, arithmetic and copies ran while one was open for 0% -> 1% of each run, Pallas kernels for 0% -> 0%
where the time goes in v2:
time: 250 us; the launch traced here: 248 us
  starting transfers between devices  150 us (60%)
  waiting for transfers between devices  73.1 us (29%)
  local copies, waits for them, and re-layouts  9.34 us (4%)
  matrix products  8.83 us (4%)
  other arithmetic  5.29 us (2%)
    ppermute x10, starting transfers between devices, butterfly_sum(): lax.ppermute(value, axis, [(i, i ^ stride) for i in range(count)])  67.9 us
    ppermute x15, starting transfers between devices, padded_2(): lax.ppermute(jnp.squeeze(tail, dim), axis, [(i, i + 1) for i in range(end...  50.6 us
    ppermute x15, waiting for transfers between devices, padded_2(): lax.ppermute(jnp.squeeze(head, dim), axis, [(i + 1, i) for i in range(end...  41 us
    ppermute x15, starting transfers between devices, padded_2(): lax.ppermute(jnp.squeeze(head, dim), axis, [(i + 1, i) for i in range(end...  31.3 us
    ppermute x10, waiting for transfers between devices, butterfly_sum(): lax.ppermute(value, axis, [(i, i ^ stride) for i in range(count)])  28 us
    unnamed x29, local copies, waits for them, and re-layouts  5.7 us
  transfers between devices with their start and end apart: 40, of which 29 were waited for; matrix products, arithmetic and copies ran while one was open for 1% of the time, Pallas kernels for 0%

profile of v2, /device:TPU:24, one launch (start us, length us, event | category | flops | bytes accessed | tf_op | source)
XLA Modules:
  0.0 248.1 jit_solution(7000109301863416282)
XLA Ops:
  4.3 1.3 collective-permute-start.1
  5.8 4.5 %collective-permute-start = (f32[8,16]{1,0:T(8,128)S(1)}, f32[8,16]{1,0:T(8,128)S(1)}, u32[]{:S(2)}, u32[]{:S(2)}) collective-permute-start(f32[8,16]{1,0:T(8,128)S(1)} %bitcast.243), channel_id=1, source_target_pairs={{0,1},{1,2},{2,3},{3,4},{4,5},{5,6},{6,7},{7,8},{8,9},{9,10},{10,1... | collective-permute-start | bytes 1544 | tf_op jit(solution)/shard_map/ppermute | solution.py:32
  10.3 1.3 collective-permute-done
  12.0 1.9 collective-permute-start.2
  14.0 3.6 %collective-permute-start.3 = (f32[8,258]{1,0:T(8,128)S(1)}, f32[8,258]{1,0:T(8,128)S(1)}, u32[]{:S(2)}, u32[]{:S(2)}) collective-permute-start(f32[8,258]{1,0:T(8,128)S(1)} %get-tuple-element.43), channel_id=1, source_target_pairs={{32,0},{64,32},{96,64},{128,96},{160,128},{192,160},{224,192},{33,... | collective-permute-start | bytes 24776 | tf_op jit(solution)/shard_map/ppermute | solution.py:33
  17.7 1.3 collective-permute-done.3
  19.1 3.4 %collective-permute-start.4 = (f32[18,258]{1,0:T(8,128)S(1)}, f32[18,258]{1,0:T(8,128)S(1)}, u32[]{:S(2)}, u32[]{:S(2)}) collective-permute-start(f32[18,258]{1,0:T(8,128)S(1)} %get-tuple-element.26), channel_id=1, source_target_pairs={{0,256},{256,512},{512,768},{1,257},{257,513},{513,769},{2,258},{2... | collective-permute-start | bytes 55736 | tf_op jit(solution)/shard_map/ppermute | solution.py:32
  22.6 1.3 collective-permute-start.5
  24.2 4.2 %collective-permute-done.5 = f32[18,258]{1,0:T(8,128)S(1)} collective-permute-done((f32[18,258]{1,0:T(8,128)S(1)}, f32[18,258]{1,0:T(8,128)S(1)}, u32[]{:S(2)}, u32[]{:S(2)}) %collective-permute-start.5) | collective-permute-done | bytes 18608 | tf_op jit(solution)/shard_map/ppermute | solution.py:33
  33.2 4.2 %collective-permute-start.6 = (f32[8,16]{1,0:T(8,128)S(1)}, f32[8,16]{1,0:T(8,128)S(1)}, u32[]{:S(2)}, u32[]{:S(2)}) collective-permute-start(f32[8,16]{1,0:T(8,128)S(1)} %bitcast.235), channel_id=1, source_target_pairs={{0,1},{1,2},{2,3},{3,4},{4,5},{5,6},{6,7},{7,8},{8,9},{9,10},{10,1... | collective-permute-start | bytes 1544 | tf_op jit(solution)/shard_map/ppermute | solution.py:32
  37.6 1.3 collective-permute-start.7
  39.0 4.1 %collective-permute-done.7 = f32[8,16]{1,0:T(8,128)S(1)} collective-permute-done((f32[8,16]{1,0:T(8,128)S(1)}, f32[8,16]{1,0:T(8,128)S(1)}, u32[]{:S(2)}, u32[]{:S(2)}) %collective-permute-start.7) | collective-permute-done | bytes 544 | tf_op jit(solution)/shard_map/ppermute | solution.py:33
  43.3 1.9 collective-permute-start.8
  45.3 3.6 %collective-permute-start.9 = (f32[8,258]{1,0:T(8,128)S(1)}, f32[8,258]{1,0:T(8,128)S(1)}, u32[]{:S(2)}, u32[]{:S(2)}) collective-permute-start(f32[8,258]{1,0:T(8,128)S(1)} %get-tuple-element.41), channel_id=1, source_target_pairs={{32,0},{64,32},{96,64},{128,96},{160,128},{192,160},{224,192},{33,... | collective-permute-start | bytes 24776 | tf_op jit(solution)/shard_map/ppermute | solution.py:33
  49.0 1.3 collective-permute-done.9
  50.4 3.4 %collective-permute-start.10 = (f32[18,258]{1,0:T(8,128)S(1)}, f32[18,258]{1,0:T(8,128)S(1)}, u32[]{:S(2)}, u32[]{:S(2)}) collective-permute-start(f32[18,258]{1,0:T(8,128)S(1)} %get-tuple-element.24), channel_id=1, source_target_pairs={{0,256},{256,512},{512,768},{1,257},{257,513},{513,769},{2,258},{2... | collective-permute-start | bytes 55736 | tf_op jit(solution)/shard_map/ppermute | solution.py:32
  53.8 1.3 collective-permute-start.11
  55.4 4.2 %collective-permute-done.11 = f32[18,258]{1,0:T(8,128)S(1)} collective-permute-done((f32[18,258]{1,0:T(8,128)S(1)}, f32[18,258]{1,0:T(8,128)S(1)}, u32[]{:S(2)}, u32[]{:S(2)}) %collective-permute-start.11) | collective-permute-done | bytes 18608 | tf_op jit(solution)/shard_map/ppermute | solution.py:33
  62.3 4.6 %collective-permute-start.12 = (f32[8,16]{1,0:T(8,128)S(1)}, f32[8,16]{1,0:T(8,128)S(1)}, u32[]{:S(2)}, u32[]{:S(2)}) collective-permute-start(f32[8,16]{1,0:T(8,128)S(1)} %bitcast.237), channel_id=1, source_target_pairs={{0,1},{1,2},{2,3},{3,4},{4,5},{5,6},{6,7},{7,8},{8,9},{9,10},{10,1... | collective-permute-start | bytes 1544 | tf_op jit(solution)/shard_map/ppermute | solution.py:32
  67.0 1.3 collective-permute-start.13
  68.4 5.5 %collective-permute-done.13 = f32[8,16]{1,0:T(8,128)S(1)} collective-permute-done((f32[8,16]{1,0:T(8,128)S(1)}, f32[8,16]{1,0:T(8,128)S(1)}, u32[]{:S(2)}, u32[]{:S(2)}) %collective-permute-start.13) | collective-permute-done | bytes 544 | tf_op jit(solution)/shard_map/ppermute | solution.py:33
  74.2 1.9 collective-permute-start.14
  76.2 3.6 %collective-permute-start.15 = (f32[8,258]{1,0:T(8,128)S(1)}, f32[8,258]{1,0:T(8,128)S(1)}, u32[]{:S(2)}, u32[]{:S(2)}) collective-permute-start(f32[8,258]{1,0:T(8,128)S(1)} %get-tuple-element.39), channel_id=1, source_target_pairs={{32,0},{64,32},{96,64},{128,96},{160,128},{192,160},{224,192},{33,... | collective-permute-start | bytes 24776 | tf_op jit(solution)/shard_map/ppermute | solution.py:33
  79.9 1.3 collective-permute-done.15
  81.3 3.1 %collective-permute-start.16 = (f32[18,258]{1,0:T(8,128)S(1)}, f32[18,258]{1,0:T(8,128)S(1)}, u32[]{:S(2)}, u32[]{:S(2)}) collective-permute-start(f32[18,258]{1,0:T(8,128)S(1)} %get-tuple-element.22), channel_id=1, source_target_pairs={{0,256},{256,512},{512,768},{1,257},{257,513},{513,769},{2,258},{2... | collective-permute-start | bytes 55736 | tf_op jit(solution)/shard_map/ppermute | solution.py:32
  84.4 1.3 collective-permute-start.17
  86.0 4.2 %collective-permute-done.17 = f32[18,258]{1,0:T(8,128)S(1)} collective-permute-done((f32[18,258]{1,0:T(8,128)S(1)}, f32[18,258]{1,0:T(8,128)S(1)}, u32[]{:S(2)}, u32[]{:S(2)}) %collective-permute-start.17) | collective-permute-done | bytes 18608 | tf_op jit(solution)/shard_map/ppermute | solution.py:33
  93.0 5.1 %collective-permute-start.18 = (f32[8,16]{1,0:T(8,128)S(1)}, f32[8,16]{1,0:T(8,128)S(1)}, u32[]{:S(2)}, u32[]{:S(2)}) collective-permute-start(f32[8,16]{1,0:T(8,128)S(1)} %bitcast.239), channel_id=1, source_target_pairs={{0,1},{1,2},{2,3},{3,4},{4,5},{5,6},{6,7},{7,8},{8,9},{9,10},{10,1... | collective-permute-start | bytes 1544 | tf_op jit(solution)/shard_map/ppermute | solution.py:32
  98.2 1.3 collective-permute-start.19
  99.7 4.1 %collective-permute-done.19 = f32[8,16]{1,0:T(8,128)S(1)} collective-permute-done((f32[8,16]{1,0:T(8,128)S(1)}, f32[8,16]{1,0:T(8,128)S(1)}, u32[]{:S(2)}, u32[]{:S(2)}) %collective-permute-start.19) | collective-permute-done | bytes 544 | tf_op jit(solution)/shard_map/ppermute | solution.py:33
  104.0 1.9 collective-permute-start.20
  106.0 3.6 %collective-permute-start.21 = (f32[8,258]{1,0:T(8,128)S(1)}, f32[8,258]{1,0:T(8,128)S(1)}, u32[]{:S(2)}, u32[]{:S(2)}) collective-permute-start(f32[8,258]{1,0:T(8,128)S(1)} %get-tuple-element.37), channel_id=1, source_target_pairs={{32,0},{64,32},{96,64},{128,96},{160,128},{192,160},{224,192},{33,... | collective-permute-start | bytes 24776 | tf_op jit(solution)/shard_map/ppermute | solution.py:33
  109.7 1.3 collective-permute-done.21
  111.1 1.3 collective-permute-start.23
  112.4 4.5 %collective-permute-start.22 = (f32[18,258]{1,0:T(8,128)S(1)}, f32[18,258]{1,0:T(8,128)S(1)}, u32[]{:S(2)}, u32[]{:S(2)}) collective-permute-start(f32[18,258]{1,0:T(8,128)S(1)} %get-tuple-element.19), channel_id=1, source_target_pairs={{0,256},{256,512},{512,768},{1,257},{257,513},{513,769},{2,258},{2... | collective-permute-start | bytes 55736 | tf_op jit(solution)/shard_map/ppermute | solution.py:32
  116.9 1.6 collective-permute-done.22
  121.2 3.9 %collective-permute-start.24 = (f32[8,16]{1,0:T(8,128)S(1)}, f32[8,16]{1,0:T(8,128)S(1)}, u32[]{:S(2)}, u32[]{:S(2)}) collective-permute-start(f32[8,16]{1,0:T(8,128)S(1)} %bitcast.241), channel_id=1, source_target_pairs={{0,1},{1,2},{2,3},{3,4},{4,5},{5,6},{6,7},{7,8},{8,9},{9,10},{10,1... | collective-permute-start | bytes 1544 | tf_op jit(solution)/shard_map/ppermute | solution.py:32
  125.2 1.5 collective-permute-start.25
  126.8 3.9 %collective-permute-done.25 = f32[8,16]{1,0:T(8,128)S(1)} collective-permute-done((f32[8,16]{1,0:T(8,128)S(1)}, f32[8,16]{1,0:T(8,128)S(1)}, u32[]{:S(2)}, u32[]{:S(2)}) %collective-permute-start.25) | collective-permute-done | bytes 544 | tf_op jit(solution)/shard_map/ppermute | solution.py:33
  131.0 1.9 collective-permute-start.26
  132.9 3.6 %collective-permute-start.27 = (f32[8,258]{1,0:T(8,128)S(1)}, f32[8,258]{1,0:T(8,128)S(1)}, u32[]{:S(2)}, u32[]{:S(2)}) collective-permute-start(f32[8,258]{1,0:T(8,128)S(1)} %get-tuple-element.35), channel_id=1, source_target_pairs={{32,0},{64,32},{96,64},{128,96},{160,128},{192,160},{224,192},{33,... | collective-permute-start | bytes 24776 | tf_op jit(solution)/shard_map/ppermute | solution.py:33
  136.7 1.3 collective-permute-done.27
  138.1 4.2 %collective-permute-start.28 = (f32[18,258]{1,0:T(8,128)S(1)}, f32[18,258]{1,0:T(8,128)S(1)}, u32[]{:S(2)}, u32[]{:S(2)}) collective-permute-start(f32[18,258]{1,0:T(8,128)S(1)} %get-tuple-element.16), channel_id=1, source_target_pairs={{0,256},{256,512},{512,768},{1,257},{257,513},{513,769},{2,258},{2... | collective-permute-start | bytes 55736 | tf_op jit(solution)/shard_map/ppermute | solution.py:32
  142.3 1.3 collective-permute-start.29
  143.9 4.2 %collective-permute-done.29 = f32[18,258]{1,0:T(8,128)S(1)} collective-permute-done((f32[18,258]{1,0:T(8,128)S(1)}, f32[18,258]{1,0:T(8,128)S(1)}, u32[]{:S(2)}, u32[]{:S(2)}) %collective-permute-start.29) | collective-permute-done | bytes 18608 | tf_op jit(solution)/shard_map/ppermute | solution.py:33
  150.0 1.9 collective-permute-start.30
  153.1 3.2 %collective-permute-start.31 = (f32[8192]{0:T(1024)S(1)}, f32[8192]{0:T(1024)S(1)}, u32[]{:S(2)}, u32[]{:S(2)}) collective-permute-start(f32[8192]{0:T(1024)S(1)} %add.337), channel_id=1, source_target_pairs={{0,64},{32,96},{64,0},{96,32},{128,192},{160,224},{192,128},{224,1... | collective-permute-start | bytes 98312 | tf_op jit(solution)/shard_map/ppermute | solution.py:46
  156.3 2.6 %collective-permute-done.31 = f32[8192]{0:T(1024)S(1)} collective-permute-done((f32[8192]{0:T(1024)S(1)}, f32[8192]{0:T(1024)S(1)}, u32[]{:S(2)}, u32[]{:S(2)}) %collective-permute-start.31) | collective-permute-done | bytes 32800 | tf_op jit(solution)/shard_map/ppermute | solution.py:46
  158.9 3.5 %collective-permute-start.32 = (f32[8192]{0:T(1024)S(1)}, f32[8192]{0:T(1024)S(1)}, u32[]{:S(2)}, u32[]{:S(2)}) collective-permute-start(f32[8192]{0:T(1024)S(1)} %add.338), channel_id=1, source_target_pairs={{0,128},{32,160},{64,192},{96,224},{128,0},{160,32},{192,64},{224,... | collective-permute-start | bytes 98312 | tf_op jit(solution)/shard_map/ppermute | solution.py:46
  162.4 3.8 %collective-permute-done.32 = f32[8192]{0:T(1024)S(1)} collective-permute-done((f32[8192]{0:T(1024)S(1)}, f32[8192]{0:T(1024)S(1)}, u32[]{:S(2)}, u32[]{:S(2)}) %collective-permute-start.32) | collective-permute-done | bytes 32800 | tf_op jit(solution)/shard_map/ppermute | solution.py:46
  166.2 4.8 %collective-permute-start.33 = (f32[8192]{0:T(1024)S(1)}, f32[8192]{0:T(1024)S(1)}, u32[]{:S(2)}, u32[]{:S(2)}) collective-permute-start(f32[8192]{0:T(1024)S(1)} %add.339), channel_id=1, source_target_pairs={{0,1},{1,0},{2,3},{3,2},{4,5},{5,4},{6,7},{7,6},{8,9},{9,8},{10,11... | collective-permute-start | bytes 98312 | tf_op jit(solution)/shard_map/ppermute | solution.py:46
  171.0 1.9 collective-permute-done.33
  172.9 6.6 %collective-permute-start.34 = (f32[8192]{0:T(1024)S(1)}, f32[8192]{0:T(1024)S(1)}, u32[]{:S(2)}, u32[]{:S(2)}) collective-permute-start(f32[8192]{0:T(1024)S(1)} %add.340), channel_id=1, source_target_pairs={{0,2},{1,3},{2,0},{3,1},{4,6},{5,7},{6,4},{7,5},{8,10},{9,11},{10,... | collective-permute-start | bytes 98312 | tf_op jit(solution)/shard_map/ppermute | solution.py:46
  179.4 1.9 collective-permute-done.34
  181.3 9.1 %collective-permute-start.35 = (f32[8192]{0:T(1024)S(1)}, f32[8192]{0:T(1024)S(1)}, u32[]{:S(2)}, u32[]{:S(2)}) collective-permute-start(f32[8192]{0:T(1024)S(1)} %add.341), channel_id=1, source_target_pairs={{0,4},{1,5},{2,6},{3,7},{4,0},{5,1},{6,2},{7,3},{8,12},{9,13},{10,... | collective-permute-start | bytes 98312 | tf_op jit(solution)/shard_map/ppermute | solution.py:46
  190.4 1.9 collective-permute-done.35
  192.3 14.5 %collective-permute-start.36 = (f32[8192]{0:T(1024)S(1)}, f32[8192]{0:T(1024)S(1)}, u32[]{:S(2)}, u32[]{:S(2)}) collective-permute-start(f32[8192]{0:T(1024)S(1)} %add.342), channel_id=1, source_target_pairs={{0,8},{1,9},{2,10},{3,11},{4,12},{5,13},{6,14},{7,15},{8,0},{9,1},... | collective-permute-start | bytes 98312 | tf_op jit(solution)/shard_map/ppermute | solution.py:46
  206.8 1.9 collective-permute-done.36
  208.8 20.5 %collective-permute-start.37 = (f32[8192]{0:T(1024)S(1)}, f32[8192]{0:T(1024)S(1)}, u32[]{:S(2)}, u32[]{:S(2)}) collective-permute-start(f32[8192]{0:T(1024)S(1)} %add.343), channel_id=1, source_target_pairs={{0,16},{1,17},{2,18},{3,19},{4,20},{5,21},{6,22},{7,23},{8,24},{9,... | collective-permute-start | bytes 98312 | tf_op jit(solution)/shard_map/ppermute | solution.py:46
  229.2 3.7 %collective-permute-done.37 = f32[8192]{0:T(1024)S(1)} collective-permute-done((f32[8192]{0:T(1024)S(1)}, f32[8192]{0:T(1024)S(1)}, u32[]{:S(2)}, u32[]{:S(2)}) %collective-permute-start.37) | collective-permute-done | bytes 32800 | tf_op jit(solution)/shard_map/ppermute | solution.py:46
  232.9 1.9 collective-permute-start.38
  234.8 3.9 %collective-permute-done.38 = f32[8192]{0:T(1024)S(1)} collective-permute-done((f32[8192]{0:T(1024)S(1)}, f32[8192]{0:T(1024)S(1)}, u32[]{:S(2)}, u32[]{:S(2)}) %collective-permute-start.38) | collective-permute-done | bytes 32800 | tf_op jit(solution)/shard_map/ppermute | solution.py:46
  238.7 2.0 collective-permute-start.39
  240.7 5.3 %collective-permute-done.39 = f32[8192]{0:T(1024)S(1)} collective-permute-done((f32[8192]{0:T(1024)S(1)}, f32[8192]{0:T(1024)S(1)}, u32[]{:S(2)}, u32[]{:S(2)}) %collective-permute-start.39) | collective-permute-done | bytes 32800 | tf_op jit(solution)/shard_map/ppermute | solution.py:46
  (180 shorter events, 25.9 us)
Async XLA Ops:
  0.6 149.0 %copy-start = (f32[8,8192]{1,0:T(8,128)S(1)}, f32[8,8192]{1,0:T(8,128)}, u32[]{:S(2)}) copy-start(f32[8,8192]{1,0:T(8,128)} %param.13) | copy-start | bytes 786436
  0.6 0.7 copy-start.9
  0.7 0.7 copy-start.7
  0.7 0.7 copy-start.8
  0.7 1.7 copy-start.10
  0.7 1.7 copy-start.1
  2.4 0.7 copy-start.11
  3.1 0.7 copy-start.12
  4.3 7.4 %collective-permute-start.1 = (f32[8,16]{1,0:T(8,128)S(1)}, f32[8,16]{1,0:T(8,128)S(1)}, u32[]{:S(2)}, u32[]{:S(2)}) collective-permute-start(f32[8,16]{1,0:T(8,128)S(1)} %bitcast.233), channel_id=1, source_target_pairs={{1,0},{2,1},{3,2},{4,3},{5,4},{6,5},{7,6},{8,7},{9,8},{10,9},{11,1... | collective-permute-start | bytes 1544 | tf_op jit(solution)/shard_map/ppermute | solution.py:33
  5.8 5.9 %collective-permute-start = (f32[8,16]{1,0:T(8,128)S(1)}, f32[8,16]{1,0:T(8,128)S(1)}, u32[]{:S(2)}, u32[]{:S(2)}) collective-permute-start(f32[8,16]{1,0:T(8,128)S(1)} %bitcast.243), channel_id=1, source_target_pairs={{0,1},{1,2},{2,3},{3,4},{4,5},{5,6},{6,7},{7,8},{8,9},{9,10},{10,1... | collective-permute-start | bytes 1544 | tf_op jit(solution)/shard_map/ppermute | solution.py:32
  12.0 5.6 %collective-permute-start.2 = (f32[8,258]{1,0:T(8,128)S(1)}, f32[8,258]{1,0:T(8,128)S(1)}, u32[]{:S(2)}, u32[]{:S(2)}) collective-permute-start(f32[8,258]{1,0:T(8,128)S(1)} %get-tuple-element.42), channel_id=1, source_target_pairs={{0,32},{32,64},{64,96},{96,128},{128,160},{160,192},{192,224},{1,3... | collective-permute-start | bytes 24776 | tf_op jit(solution)/shard_map/ppermute | solution.py:32
  14.0 5.0 %collective-permute-start.3 = (f32[8,258]{1,0:T(8,128)S(1)}, f32[8,258]{1,0:T(8,128)S(1)}, u32[]{:S(2)}, u32[]{:S(2)}) collective-permute-start(f32[8,258]{1,0:T(8,128)S(1)} %get-tuple-element.43), channel_id=1, source_target_pairs={{32,0},{64,32},{96,64},{128,96},{160,128},{192,160},{224,192},{33,... | collective-permute-start | bytes 24776 | tf_op jit(solution)/shard_map/ppermute | solution.py:33
  19.1 5.0 %collective-permute-start.4 = (f32[18,258]{1,0:T(8,128)S(1)}, f32[18,258]{1,0:T(8,128)S(1)}, u32[]{:S(2)}, u32[]{:S(2)}) collective-permute-start(f32[18,258]{1,0:T(8,128)S(1)} %get-tuple-element.26), channel_id=1, source_target_pairs={{0,256},{256,512},{512,768},{1,257},{257,513},{513,769},{2,258},{2... | collective-permute-start | bytes 55736 | tf_op jit(solution)/shard_map/ppermute | solution.py:32
  22.6 5.9 %collective-permute-start.5 = (f32[18,258]{1,0:T(8,128)S(1)}, f32[18,258]{1,0:T(8,128)S(1)}, u32[]{:S(2)}, u32[]{:S(2)}) collective-permute-start(f32[18,258]{1,0:T(8,128)S(1)} %get-tuple-element.27), channel_id=1, source_target_pairs={{256,0},{512,256},{768,512},{257,1},{513,257},{769,513},{258,2},{5... | collective-permute-start | bytes 55736 | tf_op jit(solution)/shard_map/ppermute | solution.py:33
  28.6 0.9 copy-start.3
  29.5 0.8 copy-start.2
  30.6 0.7 copy-start.4
  31.7 0.7 copy-start.6
  33.2 5.6 %collective-permute-start.6 = (f32[8,16]{1,0:T(8,128)S(1)}, f32[8,16]{1,0:T(8,128)S(1)}, u32[]{:S(2)}, u32[]{:S(2)}) collective-permute-start(f32[8,16]{1,0:T(8,128)S(1)} %bitcast.235), channel_id=1, source_target_pairs={{0,1},{1,2},{2,3},{3,4},{4,5},{5,6},{6,7},{7,8},{8,9},{9,10},{10,1... | collective-permute-start | bytes 1544 | tf_op jit(solution)/shard_map/ppermute | solution.py:32
  37.6 5.5 %collective-permute-start.7 = (f32[8,16]{1,0:T(8,128)S(1)}, f32[8,16]{1,0:T(8,128)S(1)}, u32[]{:S(2)}, u32[]{:S(2)}) collective-permute-start(f32[8,16]{1,0:T(8,128)S(1)} %bitcast.245), channel_id=1, source_target_pairs={{1,0},{2,1},{3,2},{4,3},{5,4},{6,5},{7,6},{8,7},{9,8},{10,9},{11,1... | collective-permute-start | bytes 1544 | tf_op jit(solution)/shard_map/ppermute | solution.py:33
  43.3 5.6 %collective-permute-start.8 = (f32[8,258]{1,0:T(8,128)S(1)}, f32[8,258]{1,0:T(8,128)S(1)}, u32[]{:S(2)}, u32[]{:S(2)}) collective-permute-start(f32[8,258]{1,0:T(8,128)S(1)} %get-tuple-element.40), channel_id=1, source_target_pairs={{0,32},{32,64},{64,96},{96,128},{128,160},{160,192},{192,224},{1,3... | collective-permute-start | bytes 24776 | tf_op jit(solution)/shard_map/ppermute | solution.py:32
  45.3 5.0 %collective-permute-start.9 = (f32[8,258]{1,0:T(8,128)S(1)}, f32[8,258]{1,0:T(8,128)S(1)}, u32[]{:S(2)}, u32[]{:S(2)}) collective-permute-start(f32[8,258]{1,0:T(8,128)S(1)} %get-tuple-element.41), channel_id=1, source_target_pairs={{32,0},{64,32},{96,64},{128,96},{160,128},{192,160},{224,192},{33,... | collective-permute-start | bytes 24776 | tf_op jit(solution)/shard_map/ppermute | solution.py:33
  50.4 5.0 %collective-permute-start.10 = (f32[18,258]{1,0:T(8,128)S(1)}, f32[18,258]{1,0:T(8,128)S(1)}, u32[]{:S(2)}, u32[]{:S(2)}) collective-permute-start(f32[18,258]{1,0:T(8,128)S(1)} %get-tuple-element.24), channel_id=1, source_target_pairs={{0,256},{256,512},{512,768},{1,257},{257,513},{513,769},{2,258},{2... | collective-permute-start | bytes 55736 | tf_op jit(solution)/shard_map/ppermute | solution.py:32
  53.8 5.9 %collective-permute-start.11 = (f32[18,258]{1,0:T(8,128)S(1)}, f32[18,258]{1,0:T(8,128)S(1)}, u32[]{:S(2)}, u32[]{:S(2)}) collective-permute-start(f32[18,258]{1,0:T(8,128)S(1)} %get-tuple-element.25), channel_id=1, source_target_pairs={{256,0},{512,256},{768,512},{257,1},{513,257},{769,513},{258,2},{5... | collective-permute-start | bytes 55736 | tf_op jit(solution)/shard_map/ppermute | solution.py:33
  62.3 6.0 %collective-permute-start.12 = (f32[8,16]{1,0:T(8,128)S(1)}, f32[8,16]{1,0:T(8,128)S(1)}, u32[]{:S(2)}, u32[]{:S(2)}) collective-permute-start(f32[8,16]{1,0:T(8,128)S(1)} %bitcast.237), channel_id=1, source_target_pairs={{0,1},{1,2},{2,3},{3,4},{4,5},{5,6},{6,7},{7,8},{8,9},{9,10},{10,1... | collective-permute-start | bytes 1544 | tf_op jit(solution)/shard_map/ppermute | solution.py:32
  67.0 7.0 %collective-permute-start.13 = (f32[8,16]{1,0:T(8,128)S(1)}, f32[8,16]{1,0:T(8,128)S(1)}, u32[]{:S(2)}, u32[]{:S(2)}) collective-permute-start(f32[8,16]{1,0:T(8,128)S(1)} %bitcast.247), channel_id=1, source_target_pairs={{1,0},{2,1},{3,2},{4,3},{5,4},{6,5},{7,6},{8,7},{9,8},{10,9},{11,1... | collective-permute-start | bytes 1544 | tf_op jit(solution)/shard_map/ppermute | solution.py:33
  74.2 5.6 %collective-permute-start.14 = (f32[8,258]{1,0:T(8,128)S(1)}, f32[8,258]{1,0:T(8,128)S(1)}, u32[]{:S(2)}, u32[]{:S(2)}) collective-permute-start(f32[8,258]{1,0:T(8,128)S(1)} %get-tuple-element.38), channel_id=1, source_target_pairs={{0,32},{32,64},{64,96},{96,128},{128,160},{160,192},{192,224},{1,3... | collective-permute-start | bytes 24776 | tf_op jit(solution)/shard_map/ppermute | solution.py:32
  76.2 5.0 %collective-permute-start.15 = (f32[8,258]{1,0:T(8,128)S(1)}, f32[8,258]{1,0:T(8,128)S(1)}, u32[]{:S(2)}, u32[]{:S(2)}) collective-permute-start(f32[8,258]{1,0:T(8,128)S(1)} %get-tuple-element.39), channel_id=1, source_target_pairs={{32,0},{64,32},{96,64},{128,96},{160,128},{192,160},{224,192},{33,... | collective-permute-start | bytes 24776 | tf_op jit(solution)/shard_map/ppermute | solution.py:33
  81.3 4.7 %collective-permute-start.16 = (f32[18,258]{1,0:T(8,128)S(1)}, f32[18,258]{1,0:T(8,128)S(1)}, u32[]{:S(2)}, u32[]{:S(2)}) collective-permute-start(f32[18,258]{1,0:T(8,128)S(1)} %get-tuple-element.22), channel_id=1, source_target_pairs={{0,256},{256,512},{512,768},{1,257},{257,513},{513,769},{2,258},{2... | collective-permute-start | bytes 55736 | tf_op jit(solution)/shard_map/ppermute | solution.py:32
  84.4 5.9 %collective-permute-start.17 = (f32[18,258]{1,0:T(8,128)S(1)}, f32[18,258]{1,0:T(8,128)S(1)}, u32[]{:S(2)}, u32[]{:S(2)}) collective-permute-start(f32[18,258]{1,0:T(8,128)S(1)} %get-tuple-element.23), channel_id=1, source_target_pairs={{256,0},{512,256},{768,512},{257,1},{513,257},{769,513},{258,2},{5... | collective-permute-start | bytes 55736 | tf_op jit(solution)/shard_map/ppermute | solution.py:33
  93.0 6.6 %collective-permute-start.18 = (f32[8,16]{1,0:T(8,128)S(1)}, f32[8,16]{1,0:T(8,128)S(1)}, u32[]{:S(2)}, u32[]{:S(2)}) collective-permute-start(f32[8,16]{1,0:T(8,128)S(1)} %bitcast.239), channel_id=1, source_target_pairs={{0,1},{1,2},{2,3},{3,4},{4,5},{5,6},{6,7},{7,8},{8,9},{9,10},{10,1... | collective-permute-start | bytes 1544 | tf_op jit(solution)/shard_map/ppermute | solution.py:32
  98.2 5.5 %collective-permute-start.19 = (f32[8,16]{1,0:T(8,128)S(1)}, f32[8,16]{1,0:T(8,128)S(1)}, u32[]{:S(2)}, u32[]{:S(2)}) collective-permute-start(f32[8,16]{1,0:T(8,128)S(1)} %bitcast.249), channel_id=1, source_target_pairs={{1,0},{2,1},{3,2},{4,3},{5,4},{6,5},{7,6},{8,7},{9,8},{10,9},{11,1... | collective-permute-start | bytes 1544 | tf_op jit(solution)/shard_map/ppermute | solution.py:33
  104.0 5.6 %collective-permute-start.20 = (f32[8,258]{1,0:T(8,128)S(1)}, f32[8,258]{1,0:T(8,128)S(1)}, u32[]{:S(2)}, u32[]{:S(2)}) collective-permute-start(f32[8,258]{1,0:T(8,128)S(1)} %get-tuple-element.36), channel_id=1, source_target_pairs={{0,32},{32,64},{64,96},{96,128},{128,160},{160,192},{192,224},{1,3... | collective-permute-start | bytes 24776 | tf_op jit(solution)/shard_map/ppermute | solution.py:32
  106.0 5.0 %collective-permute-start.21 = (f32[8,258]{1,0:T(8,128)S(1)}, f32[8,258]{1,0:T(8,128)S(1)}, u32[]{:S(2)}, u32[]{:S(2)}) collective-permute-start(f32[8,258]{1,0:T(8,128)S(1)} %get-tuple-element.37), channel_id=1, source_target_pairs={{32,0},{64,32},{96,64},{128,96},{160,128},{192,160},{224,192},{33,... | collective-permute-start | bytes 24776 | tf_op jit(solution)/shard_map/ppermute | solution.py:33
  111.1 5.9 %collective-permute-start.23 = (f32[18,258]{1,0:T(8,128)S(1)}, f32[18,258]{1,0:T(8,128)S(1)}, u32[]{:S(2)}, u32[]{:S(2)}) collective-permute-start(f32[18,258]{1,0:T(8,128)S(1)} %get-tuple-element.18), channel_id=1, source_target_pairs={{256,0},{512,256},{768,512},{257,1},{513,257},{769,513},{258,2},{5... | collective-permute-start | bytes 55736 | tf_op jit(solution)/shard_map/ppermute | solution.py:33
  112.4 6.2 %collective-permute-start.22 = (f32[18,258]{1,0:T(8,128)S(1)}, f32[18,258]{1,0:T(8,128)S(1)}, u32[]{:S(2)}, u32[]{:S(2)}) collective-permute-start(f32[18,258]{1,0:T(8,128)S(1)} %get-tuple-element.19), channel_id=1, source_target_pairs={{0,256},{256,512},{512,768},{1,257},{257,513},{513,769},{2,258},{2... | collective-permute-start | bytes 55736 | tf_op jit(solution)/shard_map/ppermute | solution.py:32
  121.2 5.5 %collective-permute-start.24 = (f32[8,16]{1,0:T(8,128)S(1)}, f32[8,16]{1,0:T(8,128)S(1)}, u32[]{:S(2)}, u32[]{:S(2)}) collective-permute-start(f32[8,16]{1,0:T(8,128)S(1)} %bitcast.241), channel_id=1, source_target_pairs={{0,1},{1,2},{2,3},{3,4},{4,5},{5,6},{6,7},{7,8},{8,9},{9,10},{10,1... | collective-permute-start | bytes 1544 | tf_op jit(solution)/shard_map/ppermute | solution.py:32
  125.2 5.5 %collective-permute-start.25 = (f32[8,16]{1,0:T(8,128)S(1)}, f32[8,16]{1,0:T(8,128)S(1)}, u32[]{:S(2)}, u32[]{:S(2)}) collective-permute-start(f32[8,16]{1,0:T(8,128)S(1)} %bitcast.251), channel_id=1, source_target_pairs={{1,0},{2,1},{3,2},{4,3},{5,4},{6,5},{7,6},{8,7},{9,8},{10,9},{11,1... | collective-permute-start | bytes 1544 | tf_op jit(solution)/shard_map/ppermute | solution.py:33
  131.0 5.6 %collective-permute-start.26 = (f32[8,258]{1,0:T(8,128)S(1)}, f32[8,258]{1,0:T(8,128)S(1)}, u32[]{:S(2)}, u32[]{:S(2)}) collective-permute-start(f32[8,258]{1,0:T(8,128)S(1)} %get-tuple-element.34), channel_id=1, source_target_pairs={{0,32},{32,64},{64,96},{96,128},{128,160},{160,192},{192,224},{1,3... | collective-permute-start | bytes 24776 | tf_op jit(solution)/shard_map/ppermute | solution.py:32
  132.9 5.0 %collective-permute-start.27 = (f32[8,258]{1,0:T(8,128)S(1)}, f32[8,258]{1,0:T(8,128)S(1)}, u32[]{:S(2)}, u32[]{:S(2)}) collective-permute-start(f32[8,258]{1,0:T(8,128)S(1)} %get-tuple-element.35), channel_id=1, source_target_pairs={{32,0},{64,32},{96,64},{128,96},{160,128},{192,160},{224,192},{33,... | collective-permute-start | bytes 24776 | tf_op jit(solution)/shard_map/ppermute | solution.py:33
  138.1 5.9 %collective-permute-start.28 = (f32[18,258]{1,0:T(8,128)S(1)}, f32[18,258]{1,0:T(8,128)S(1)}, u32[]{:S(2)}, u32[]{:S(2)}) collective-permute-start(f32[18,258]{1,0:T(8,128)S(1)} %get-tuple-element.16), channel_id=1, source_target_pairs={{0,256},{256,512},{512,768},{1,257},{257,513},{513,769},{2,258},{2... | collective-permute-start | bytes 55736 | tf_op jit(solution)/shard_map/ppermute | solution.py:32
  142.3 5.9 %collective-permute-start.29 = (f32[18,258]{1,0:T(8,128)S(1)}, f32[18,258]{1,0:T(8,128)S(1)}, u32[]{:S(2)}, u32[]{:S(2)}) collective-permute-start(f32[18,258]{1,0:T(8,128)S(1)} %get-tuple-element.17), channel_id=1, source_target_pairs={{256,0},{512,256},{768,512},{257,1},{513,257},{769,513},{258,2},{5... | collective-permute-start | bytes 55736 | tf_op jit(solution)/shard_map/ppermute | solution.py:33
  148.4 0.9 copy-start.5
  150.0 3.1 %collective-permute-start.30 = (f32[8192]{0:T(1024)S(1)}, f32[8192]{0:T(1024)S(1)}, u32[]{:S(2)}, u32[]{:S(2)}) collective-permute-start(f32[8192]{0:T(1024)S(1)} %bitcast.216), channel_id=1, source_target_pairs={{0,32},{32,0},{64,96},{96,64},{128,160},{160,128},{192,224},{224,1... | collective-permute-start | bytes 98312 | tf_op jit(solution)/shard_map/ppermute | solution.py:46
  153.1 5.8 %collective-permute-start.31 = (f32[8192]{0:T(1024)S(1)}, f32[8192]{0:T(1024)S(1)}, u32[]{:S(2)}, u32[]{:S(2)}) collective-permute-start(f32[8192]{0:T(1024)S(1)} %add.337), channel_id=1, source_target_pairs={{0,64},{32,96},{64,0},{96,32},{128,192},{160,224},{192,128},{224,1... | collective-permute-start | bytes 98312 | tf_op jit(solution)/shard_map/ppermute | solution.py:46
  158.9 7.3 %collective-permute-start.32 = (f32[8192]{0:T(1024)S(1)}, f32[8192]{0:T(1024)S(1)}, u32[]{:S(2)}, u32[]{:S(2)}) collective-permute-start(f32[8192]{0:T(1024)S(1)} %add.338), channel_id=1, source_target_pairs={{0,128},{32,160},{64,192},{96,224},{128,0},{160,32},{192,64},{224,... | collective-permute-start | bytes 98312 | tf_op jit(solution)/shard_map/ppermute | solution.py:46
  166.2 6.6 %collective-permute-start.33 = (f32[8192]{0:T(1024)S(1)}, f32[8192]{0:T(1024)S(1)}, u32[]{:S(2)}, u32[]{:S(2)}) collective-permute-start(f32[8192]{0:T(1024)S(1)} %add.339), channel_id=1, source_target_pairs={{0,1},{1,0},{2,3},{3,2},{4,5},{5,4},{6,7},{7,6},{8,9},{9,8},{10,11... | collective-permute-start | bytes 98312 | tf_op jit(solution)/shard_map/ppermute | solution.py:46
  172.9 8.5 %collective-permute-start.34 = (f32[8192]{0:T(1024)S(1)}, f32[8192]{0:T(1024)S(1)}, u32[]{:S(2)}, u32[]{:S(2)}) collective-permute-start(f32[8192]{0:T(1024)S(1)} %add.340), channel_id=1, source_target_pairs={{0,2},{1,3},{2,0},{3,1},{4,6},{5,7},{6,4},{7,5},{8,10},{9,11},{10,... | collective-permute-start | bytes 98312 | tf_op jit(solution)/shard_map/ppermute | solution.py:46
  181.3 11.0 %collective-permute-start.35 = (f32[8192]{0:T(1024)S(1)}, f32[8192]{0:T(1024)S(1)}, u32[]{:S(2)}, u32[]{:S(2)}) collective-permute-start(f32[8192]{0:T(1024)S(1)} %add.341), channel_id=1, source_target_pairs={{0,4},{1,5},{2,6},{3,7},{4,0},{5,1},{6,2},{7,3},{8,12},{9,13},{10,... | collective-permute-start | bytes 98312 | tf_op jit(solution)/shard_map/ppermute | solution.py:46
  192.3 16.5 %collective-permute-start.36 = (f32[8192]{0:T(1024)S(1)}, f32[8192]{0:T(1024)S(1)}, u32[]{:S(2)}, u32[]{:S(2)}) collective-permute-start(f32[8192]{0:T(1024)S(1)} %add.342), channel_id=1, source_target_pairs={{0,8},{1,9},{2,10},{3,11},{4,12},{5,13},{6,14},{7,15},{8,0},{9,1},... | collective-permute-start | bytes 98312 | tf_op jit(solution)/shard_map/ppermute | solution.py:46
  208.8 24.1 %collective-permute-start.37 = (f32[8192]{0:T(1024)S(1)}, f32[8192]{0:T(1024)S(1)}, u32[]{:S(2)}, u32[]{:S(2)}) collective-permute-start(f32[8192]{0:T(1024)S(1)} %add.343), channel_id=1, source_target_pairs={{0,16},{1,17},{2,18},{3,19},{4,20},{5,21},{6,22},{7,23},{8,24},{9,... | collective-permute-start | bytes 98312 | tf_op jit(solution)/shard_map/ppermute | solution.py:46
  232.9 5.8 %collective-permute-start.38 = (f32[8192]{0:T(1024)S(1)}, f32[8192]{0:T(1024)S(1)}, u32[]{:S(2)}, u32[]{:S(2)}) collective-permute-start(f32[8192]{0:T(1024)S(1)} %add.344), channel_id=1, source_target_pairs={{0,256},{256,0},{512,768},{768,512},{1,257},{257,1},{513,769},{769... | collective-permute-start | bytes 98312 | tf_op jit(solution)/shard_map/ppermute | solution.py:46
  238.7 7.3 %collective-permute-start.39 = (f32[8192]{0:T(1024)S(1)}, f32[8192]{0:T(1024)S(1)}, u32[]{:S(2)}, u32[]{:S(2)}) collective-permute-start(f32[8192]{0:T(1024)S(1)} %add.345), channel_id=1, source_target_pairs={{0,512},{256,768},{512,0},{768,256},{1,513},{257,769},{513,1},{769... | collective-permute-start | bytes 98312 | tf_op jit(solution)/shard_map/ppermute | solution.py:46
  246.7 0.5 copy-start.13

commit v3 on v2

--- a/solution.py
+++ b/solution.py
@@ -38,13 +38,25 @@
     return cells
 
 
+def exchange(value, axis, masks):
+    count = lax.axis_size(axis)
+    parts = [lax.ppermute(value, axis, [(i, i ^ mask) for i in range(count)]) for mask in masks]
+    for part in parts:
+        value = value + part
+    return value
+
+
 def butterfly_sum(value, axes):
     for axis in axes:
         count = lax.axis_size(axis)
         stride = 1
         while stride < count:
-            value = value + lax.ppermute(value, axis, [(i, i ^ stride) for i in range(count)])
-            stride *= 2
+            if count == 4 * stride and count >= 32:
+                value = exchange(value, axis, [stride, 2 * stride, 3 * stride])
+                stride *= 4
+            else:
+                value = exchange(value, axis, [stride])
+                stride *= 2
     return value
 
 

time: 250 us -> 252 us (level)
  waiting for transfers between devices: 73.1 us -> 79.1 us
  starting transfers between devices: 150 us -> 145 us
    ppermute x10 -> x11, waiting for transfers between devices: 28 us -> 34 us  [exchange(): lax.ppermute(value, axis, [(i, i ^ mask) for i in range(count)])]
    ppermute x10 -> x11, starting transfers between devices: 67.9 us -> 63.3 us  [exchange(): lax.ppermute(value, axis, [(i, i ^ mask) for i in range(count)])]
  transfers between devices with their start and end apart: 40 -> 41, of which waited for: 29 -> 29; matrix products, arithmetic and copies ran while one was open for 1% -> 1% of each run, Pallas kernels for 0% -> 0%
where the time goes in v3:
time: 252 us; the launch traced here: 250 us
  starting transfers between devices  145 us (58%)
  waiting for transfers between devices  79.1 us (31%)
  local copies, waits for them, and re-layouts  9.34 us (4%)
  matrix products  8.83 us (4%)
  other arithmetic  5.29 us (2%)
    ppermute x11, starting transfers between devices, exchange(): lax.ppermute(value, axis, [(i, i ^ mask) for i in range(count)])  63.3 us
    ppermute x15, starting transfers between devices, padded_2(): lax.ppermute(jnp.squeeze(tail, dim), axis, [(i, i + 1) for i in range(end...  50.6 us
    ppermute x15, waiting for transfers between devices, padded_2(): lax.ppermute(jnp.squeeze(head, dim), axis, [(i + 1, i) for i in range(end...  41 us
    ppermute x11, waiting for transfers between devices, exchange(): lax.ppermute(value, axis, [(i, i ^ mask) for i in range(count)])  34 us
    ppermute x15, starting transfers between devices, padded_2(): lax.ppermute(jnp.squeeze(head, dim), axis, [(i + 1, i) for i in range(end...  31.3 us
    unnamed x29, local copies, waits for them, and re-layouts  5.7 us
  transfers between devices with their start and end apart: 41, of which 29 were waited for; matrix products, arithmetic and copies ran while one was open for 1% of the time, Pallas kernels for 0%

profile of v3, /device:TPU:24, one launch (start us, length us, event | category | flops | bytes accessed | tf_op | source)
XLA Modules:
  0.0 249.6 jit_solution(10010964313762821625)
XLA Ops:
  4.3 1.3 collective-permute-start.1
  5.8 4.5 %collective-permute-start = (f32[8,16]{1,0:T(8,128)S(1)}, f32[8,16]{1,0:T(8,128)S(1)}, u32[]{:S(2)}, u32[]{:S(2)}) collective-permute-start(f32[8,16]{1,0:T(8,128)S(1)} %bitcast.243), channel_id=1, source_target_pairs={{0,1},{1,2},{2,3},{3,4},{4,5},{5,6},{6,7},{7,8},{8,9},{9,10},{10,1... | collective-permute-start | bytes 1544 | tf_op jit(solution)/shard_map/ppermute | solution.py:32
  10.3 1.3 collective-permute-done
  12.0 1.9 collective-permute-start.2
  14.0 3.6 %collective-permute-start.3 = (f32[8,258]{1,0:T(8,128)S(1)}, f32[8,258]{1,0:T(8,128)S(1)}, u32[]{:S(2)}, u32[]{:S(2)}) collective-permute-start(f32[8,258]{1,0:T(8,128)S(1)} %get-tuple-element.43), channel_id=1, source_target_pairs={{32,0},{64,32},{96,64},{128,96},{160,128},{192,160},{224,192},{33,... | collective-permute-start | bytes 24776 | tf_op jit(solution)/shard_map/ppermute | solution.py:33
  17.7 1.3 collective-permute-done.3
  19.1 3.4 %collective-permute-start.4 = (f32[18,258]{1,0:T(8,128)S(1)}, f32[18,258]{1,0:T(8,128)S(1)}, u32[]{:S(2)}, u32[]{:S(2)}) collective-permute-start(f32[18,258]{1,0:T(8,128)S(1)} %get-tuple-element.26), channel_id=1, source_target_pairs={{0,256},{256,512},{512,768},{1,257},{257,513},{513,769},{2,258},{2... | collective-permute-start | bytes 55736 | tf_op jit(solution)/shard_map/ppermute | solution.py:32
  22.6 1.3 collective-permute-start.5
  24.2 4.2 %collective-permute-done.5 = f32[18,258]{1,0:T(8,128)S(1)} collective-permute-done((f32[18,258]{1,0:T(8,128)S(1)}, f32[18,258]{1,0:T(8,128)S(1)}, u32[]{:S(2)}, u32[]{:S(2)}) %collective-permute-start.5) | collective-permute-done | bytes 18608 | tf_op jit(solution)/shard_map/ppermute | solution.py:33
  33.2 4.2 %collective-permute-start.6 = (f32[8,16]{1,0:T(8,128)S(1)}, f32[8,16]{1,0:T(8,128)S(1)}, u32[]{:S(2)}, u32[]{:S(2)}) collective-permute-start(f32[8,16]{1,0:T(8,128)S(1)} %bitcast.235), channel_id=1, source_target_pairs={{0,1},{1,2},{2,3},{3,4},{4,5},{5,6},{6,7},{7,8},{8,9},{9,10},{10,1... | collective-permute-start | bytes 1544 | tf_op jit(solution)/shard_map/ppermute | solution.py:32
  37.6 1.3 collective-permute-start.7
  39.0 4.1 %collective-permute-done.7 = f32[8,16]{1,0:T(8,128)S(1)} collective-permute-done((f32[8,16]{1,0:T(8,128)S(1)}, f32[8,16]{1,0:T(8,128)S(1)}, u32[]{:S(2)}, u32[]{:S(2)}) %collective-permute-start.7) | collective-permute-done | bytes 544 | tf_op jit(solution)/shard_map/ppermute | solution.py:33
  43.3 1.9 collective-permute-start.8
  45.3 3.6 %collective-permute-start.9 = (f32[8,258]{1,0:T(8,128)S(1)}, f32[8,258]{1,0:T(8,128)S(1)}, u32[]{:S(2)}, u32[]{:S(2)}) collective-permute-start(f32[8,258]{1,0:T(8,128)S(1)} %get-tuple-element.41), channel_id=1, source_target_pairs={{32,0},{64,32},{96,64},{128,96},{160,128},{192,160},{224,192},{33,... | collective-permute-start | bytes 24776 | tf_op jit(solution)/shard_map/ppermute | solution.py:33
  49.0 1.3 collective-permute-done.9
  50.4 3.4 %collective-permute-start.10 = (f32[18,258]{1,0:T(8,128)S(1)}, f32[18,258]{1,0:T(8,128)S(1)}, u32[]{:S(2)}, u32[]{:S(2)}) collective-permute-start(f32[18,258]{1,0:T(8,128)S(1)} %get-tuple-element.24), channel_id=1, source_target_pairs={{0,256},{256,512},{512,768},{1,257},{257,513},{513,769},{2,258},{2... | collective-permute-start | bytes 55736 | tf_op jit(solution)/shard_map/ppermute | solution.py:32
  53.8 1.3 collective-permute-start.11
  55.4 4.2 %collective-permute-done.11 = f32[18,258]{1,0:T(8,128)S(1)} collective-permute-done((f32[18,258]{1,0:T(8,128)S(1)}, f32[18,258]{1,0:T(8,128)S(1)}, u32[]{:S(2)}, u32[]{:S(2)}) %collective-permute-start.11) | collective-permute-done | bytes 18608 | tf_op jit(solution)/shard_map/ppermute | solution.py:33
  62.3 4.6 %collective-permute-start.12 = (f32[8,16]{1,0:T(8,128)S(1)}, f32[8,16]{1,0:T(8,128)S(1)}, u32[]{:S(2)}, u32[]{:S(2)}) collective-permute-start(f32[8,16]{1,0:T(8,128)S(1)} %bitcast.237), channel_id=1, source_target_pairs={{0,1},{1,2},{2,3},{3,4},{4,5},{5,6},{6,7},{7,8},{8,9},{9,10},{10,1... | collective-permute-start | bytes 1544 | tf_op jit(solution)/shard_map/ppermute | solution.py:32
  67.0 1.3 collective-permute-start.13
  68.4 5.5 %collective-permute-done.13 = f32[8,16]{1,0:T(8,128)S(1)} collective-permute-done((f32[8,16]{1,0:T(8,128)S(1)}, f32[8,16]{1,0:T(8,128)S(1)}, u32[]{:S(2)}, u32[]{:S(2)}) %collective-permute-start.13) | collective-permute-done | bytes 544 | tf_op jit(solution)/shard_map/ppermute | solution.py:33
  74.2 1.9 collective-permute-start.14
  76.2 3.6 %collective-permute-start.15 = (f32[8,258]{1,0:T(8,128)S(1)}, f32[8,258]{1,0:T(8,128)S(1)}, u32[]{:S(2)}, u32[]{:S(2)}) collective-permute-start(f32[8,258]{1,0:T(8,128)S(1)} %get-tuple-element.39), channel_id=1, source_target_pairs={{32,0},{64,32},{96,64},{128,96},{160,128},{192,160},{224,192},{33,... | collective-permute-start | bytes 24776 | tf_op jit(solution)/shard_map/ppermute | solution.py:33
  79.9 1.3 collective-permute-done.15
  81.3 3.1 %collective-permute-start.16 = (f32[18,258]{1,0:T(8,128)S(1)}, f32[18,258]{1,0:T(8,128)S(1)}, u32[]{:S(2)}, u32[]{:S(2)}) collective-permute-start(f32[18,258]{1,0:T(8,128)S(1)} %get-tuple-element.22), channel_id=1, source_target_pairs={{0,256},{256,512},{512,768},{1,257},{257,513},{513,769},{2,258},{2... | collective-permute-start | bytes 55736 | tf_op jit(solution)/shard_map/ppermute | solution.py:32
  84.4 1.3 collective-permute-start.17
  86.0 4.2 %collective-permute-done.17 = f32[18,258]{1,0:T(8,128)S(1)} collective-permute-done((f32[18,258]{1,0:T(8,128)S(1)}, f32[18,258]{1,0:T(8,128)S(1)}, u32[]{:S(2)}, u32[]{:S(2)}) %collective-permute-start.17) | collective-permute-done | bytes 18608 | tf_op jit(solution)/shard_map/ppermute | solution.py:33
  93.0 5.1 %collective-permute-start.18 = (f32[8,16]{1,0:T(8,128)S(1)}, f32[8,16]{1,0:T(8,128)S(1)}, u32[]{:S(2)}, u32[]{:S(2)}) collective-permute-start(f32[8,16]{1,0:T(8,128)S(1)} %bitcast.239), channel_id=1, source_target_pairs={{0,1},{1,2},{2,3},{3,4},{4,5},{5,6},{6,7},{7,8},{8,9},{9,10},{10,1... | collective-permute-start | bytes 1544 | tf_op jit(solution)/shard_map/ppermute | solution.py:32
  98.2 1.3 collective-permute-start.19
  99.7 4.1 %collective-permute-done.19 = f32[8,16]{1,0:T(8,128)S(1)} collective-permute-done((f32[8,16]{1,0:T(8,128)S(1)}, f32[8,16]{1,0:T(8,128)S(1)}, u32[]{:S(2)}, u32[]{:S(2)}) %collective-permute-start.19) | collective-permute-done | bytes 544 | tf_op jit(solution)/shard_map/ppermute | solution.py:33
  104.0 1.9 collective-permute-start.20
  106.0 3.6 %collective-permute-start.21 = (f32[8,258]{1,0:T(8,128)S(1)}, f32[8,258]{1,0:T(8,128)S(1)}, u32[]{:S(2)}, u32[]{:S(2)}) collective-permute-start(f32[8,258]{1,0:T(8,128)S(1)} %get-tuple-element.37), channel_id=1, source_target_pairs={{32,0},{64,32},{96,64},{128,96},{160,128},{192,160},{224,192},{33,... | collective-permute-start | bytes 24776 | tf_op jit(solution)/shard_map/ppermute | solution.py:33
  109.7 1.3 collective-permute-done.21
  111.1 1.3 collective-permute-start.23
  112.4 4.5 %collective-permute-start.22 = (f32[18,258]{1,0:T(8,128)S(1)}, f32[18,258]{1,0:T(8,128)S(1)}, u32[]{:S(2)}, u32[]{:S(2)}) collective-permute-start(f32[18,258]{1,0:T(8,128)S(1)} %get-tuple-element.19), channel_id=1, source_target_pairs={{0,256},{256,512},{512,768},{1,257},{257,513},{513,769},{2,258},{2... | collective-permute-start | bytes 55736 | tf_op jit(solution)/shard_map/ppermute | solution.py:32
  116.9 1.6 collective-permute-done.22
  121.2 3.9 %collective-permute-start.24 = (f32[8,16]{1,0:T(8,128)S(1)}, f32[8,16]{1,0:T(8,128)S(1)}, u32[]{:S(2)}, u32[]{:S(2)}) collective-permute-start(f32[8,16]{1,0:T(8,128)S(1)} %bitcast.241), channel_id=1, source_target_pairs={{0,1},{1,2},{2,3},{3,4},{4,5},{5,6},{6,7},{7,8},{8,9},{9,10},{10,1... | collective-permute-start | bytes 1544 | tf_op jit(solution)/shard_map/ppermute | solution.py:32
  125.2 1.5 collective-permute-start.25
  126.8 3.9 %collective-permute-done.25 = f32[8,16]{1,0:T(8,128)S(1)} collective-permute-done((f32[8,16]{1,0:T(8,128)S(1)}, f32[8,16]{1,0:T(8,128)S(1)}, u32[]{:S(2)}, u32[]{:S(2)}) %collective-permute-start.25) | collective-permute-done | bytes 544 | tf_op jit(solution)/shard_map/ppermute | solution.py:33
  131.0 1.9 collective-permute-start.26
  132.9 3.6 %collective-permute-start.27 = (f32[8,258]{1,0:T(8,128)S(1)}, f32[8,258]{1,0:T(8,128)S(1)}, u32[]{:S(2)}, u32[]{:S(2)}) collective-permute-start(f32[8,258]{1,0:T(8,128)S(1)} %get-tuple-element.35), channel_id=1, source_target_pairs={{32,0},{64,32},{96,64},{128,96},{160,128},{192,160},{224,192},{33,... | collective-permute-start | bytes 24776 | tf_op jit(solution)/shard_map/ppermute | solution.py:33
  136.7 1.3 collective-permute-done.27
  138.1 4.2 %collective-permute-start.28 = (f32[18,258]{1,0:T(8,128)S(1)}, f32[18,258]{1,0:T(8,128)S(1)}, u32[]{:S(2)}, u32[]{:S(2)}) collective-permute-start(f32[18,258]{1,0:T(8,128)S(1)} %get-tuple-element.16), channel_id=1, source_target_pairs={{0,256},{256,512},{512,768},{1,257},{257,513},{513,769},{2,258},{2... | collective-permute-start | bytes 55736 | tf_op jit(solution)/shard_map/ppermute | solution.py:32
  142.3 1.3 collective-permute-start.29
  143.9 4.2 %collective-permute-done.29 = f32[18,258]{1,0:T(8,128)S(1)} collective-permute-done((f32[18,258]{1,0:T(8,128)S(1)}, f32[18,258]{1,0:T(8,128)S(1)}, u32[]{:S(2)}, u32[]{:S(2)}) %collective-permute-start.29) | collective-permute-done | bytes 18608 | tf_op jit(solution)/shard_map/ppermute | solution.py:33
  150.0 1.9 collective-permute-start.30
  153.1 3.2 %collective-permute-start.31 = (f32[8192]{0:T(1024)S(1)}, f32[8192]{0:T(1024)S(1)}, u32[]{:S(2)}, u32[]{:S(2)}) collective-permute-start(f32[8192]{0:T(1024)S(1)} %add.340), channel_id=1, source_target_pairs={{0,64},{32,96},{64,0},{96,32},{128,192},{160,224},{192,128},{224,1... | collective-permute-start | bytes 98312 | tf_op jit(solution)/shard_map/ppermute | solution.py:43
  156.3 2.6 %collective-permute-done.31 = f32[8192]{0:T(1024)S(1)} collective-permute-done((f32[8192]{0:T(1024)S(1)}, f32[8192]{0:T(1024)S(1)}, u32[]{:S(2)}, u32[]{:S(2)}) %collective-permute-start.31) | collective-permute-done | bytes 32800 | tf_op jit(solution)/shard_map/ppermute | solution.py:43
  158.9 3.5 %collective-permute-start.32 = (f32[8192]{0:T(1024)S(1)}, f32[8192]{0:T(1024)S(1)}, u32[]{:S(2)}, u32[]{:S(2)}) collective-permute-start(f32[8192]{0:T(1024)S(1)} %add.341), channel_id=1, source_target_pairs={{0,128},{32,160},{64,192},{96,224},{128,0},{160,32},{192,64},{224,... | collective-permute-start | bytes 98312 | tf_op jit(solution)/shard_map/ppermute | solution.py:43
  162.4 3.8 %collective-permute-done.32 = f32[8192]{0:T(1024)S(1)} collective-permute-done((f32[8192]{0:T(1024)S(1)}, f32[8192]{0:T(1024)S(1)}, u32[]{:S(2)}, u32[]{:S(2)}) %collective-permute-start.32) | collective-permute-done | bytes 32800 | tf_op jit(solution)/shard_map/ppermute | solution.py:43
  166.2 4.8 %collective-permute-start.33 = (f32[8192]{0:T(1024)S(1)}, f32[8192]{0:T(1024)S(1)}, u32[]{:S(2)}, u32[]{:S(2)}) collective-permute-start(f32[8192]{0:T(1024)S(1)} %add.342), channel_id=1, source_target_pairs={{0,1},{1,0},{2,3},{3,2},{4,5},{5,4},{6,7},{7,6},{8,9},{9,8},{10,11... | collective-permute-start | bytes 98312 | tf_op jit(solution)/shard_map/ppermute | solution.py:43
  171.0 1.9 collective-permute-done.33
  172.9 6.6 %collective-permute-start.34 = (f32[8192]{0:T(1024)S(1)}, f32[8192]{0:T(1024)S(1)}, u32[]{:S(2)}, u32[]{:S(2)}) collective-permute-start(f32[8192]{0:T(1024)S(1)} %add.343), channel_id=1, source_target_pairs={{0,2},{1,3},{2,0},{3,1},{4,6},{5,7},{6,4},{7,5},{8,10},{9,11},{10,... | collective-permute-start | bytes 98312 | tf_op jit(solution)/shard_map/ppermute | solution.py:43
  179.4 1.9 collective-permute-done.34
  181.3 9.1 %collective-permute-start.35 = (f32[8192]{0:T(1024)S(1)}, f32[8192]{0:T(1024)S(1)}, u32[]{:S(2)}, u32[]{:S(2)}) collective-permute-start(f32[8192]{0:T(1024)S(1)} %add.344), channel_id=1, source_target_pairs={{0,4},{1,5},{2,6},{3,7},{4,0},{5,1},{6,2},{7,3},{8,12},{9,13},{10,... | collective-permute-start | bytes 98312 | tf_op jit(solution)/shard_map/ppermute | solution.py:43
  190.4 1.9 collective-permute-done.35
  192.3 16.4 %collective-permute-start.38 = (f32[8192]{0:T(1024)S(1)}, f32[8192]{0:T(1024)S(1)}, u32[]{:S(2)}, u32[]{:S(2)}) collective-permute-start(f32[8192]{0:T(1024)S(1)} %add.345), channel_id=1, source_target_pairs={{0,24},{1,25},{2,26},{3,27},{4,28},{5,29},{6,30},{7,31},{8,16},{9,... | collective-permute-start | bytes 98312 | tf_op jit(solution)/shard_map/ppermute | solution.py:43
  208.7 10.1 %collective-permute-start.37 = (f32[8192]{0:T(1024)S(1)}, f32[8192]{0:T(1024)S(1)}, u32[]{:S(2)}, u32[]{:S(2)}) collective-permute-start(f32[8192]{0:T(1024)S(1)} %add.345), channel_id=1, source_target_pairs={{0,16},{1,17},{2,18},{3,19},{4,20},{5,21},{6,22},{7,23},{8,24},{9,... | collective-permute-start | bytes 98312 | tf_op jit(solution)/shard_map/ppermute | solution.py:43
  218.8 3.9 %collective-permute-start.36 = (f32[8192]{0:T(1024)S(1)}, f32[8192]{0:T(1024)S(1)}, u32[]{:S(2)}, u32[]{:S(2)}) collective-permute-start(f32[8192]{0:T(1024)S(1)} %add.345), channel_id=1, source_target_pairs={{0,8},{1,9},{2,10},{3,11},{4,12},{5,13},{6,14},{7,15},{8,0},{9,1},... | collective-permute-start | bytes 98312 | tf_op jit(solution)/shard_map/ppermute | solution.py:43
  222.8 10.3 %collective-permute-done.37 = f32[8192]{0:T(1024)S(1)} collective-permute-done((f32[8192]{0:T(1024)S(1)}, f32[8192]{0:T(1024)S(1)}, u32[]{:S(2)}, u32[]{:S(2)}) %collective-permute-start.37) | collective-permute-done | bytes 32800 | tf_op jit(solution)/shard_map/ppermute | solution.py:43
  234.4 1.9 collective-permute-start.39
  236.3 3.9 %collective-permute-done.39 = f32[8192]{0:T(1024)S(1)} collective-permute-done((f32[8192]{0:T(1024)S(1)}, f32[8192]{0:T(1024)S(1)}, u32[]{:S(2)}, u32[]{:S(2)}) %collective-permute-start.39) | collective-permute-done | bytes 32800 | tf_op jit(solution)/shard_map/ppermute | solution.py:43
  240.2 2.0 collective-permute-start.40
  242.1 5.3 %collective-permute-done.40 = f32[8192]{0:T(1024)S(1)} collective-permute-done((f32[8192]{0:T(1024)S(1)}, f32[8192]{0:T(1024)S(1)}, u32[]{:S(2)}, u32[]{:S(2)}) %collective-permute-start.40) | collective-permute-done | bytes 32800 | tf_op jit(solution)/shard_map/ppermute | solution.py:43
  (181 shorter events, 27.1 us)
Async XLA Ops:
  0.6 149.0 %copy-start = (f32[8,8192]{1,0:T(8,128)S(1)}, f32[8,8192]{1,0:T(8,128)}, u32[]{:S(2)}) copy-start(f32[8,8192]{1,0:T(8,128)} %param.13) | copy-start | bytes 786436
  0.6 0.7 copy-start.9
  0.7 0.7 copy-start.7
  0.7 0.7 copy-start.8
  0.7 1.7 copy-start.10
  0.7 1.7 copy-start.1
  2.4 0.7 copy-start.11
  3.1 0.7 copy-start.12
  4.3 7.4 %collective-permute-start.1 = (f32[8,16]{1,0:T(8,128)S(1)}, f32[8,16]{1,0:T(8,128)S(1)}, u32[]{:S(2)}, u32[]{:S(2)}) collective-permute-start(f32[8,16]{1,0:T(8,128)S(1)} %bitcast.233), channel_id=1, source_target_pairs={{1,0},{2,1},{3,2},{4,3},{5,4},{6,5},{7,6},{8,7},{9,8},{10,9},{11,1... | collective-permute-start | bytes 1544 | tf_op jit(solution)/shard_map/ppermute | solution.py:33
  5.8 5.9 %collective-permute-start = (f32[8,16]{1,0:T(8,128)S(1)}, f32[8,16]{1,0:T(8,128)S(1)}, u32[]{:S(2)}, u32[]{:S(2)}) collective-permute-start(f32[8,16]{1,0:T(8,128)S(1)} %bitcast.243), channel_id=1, source_target_pairs={{0,1},{1,2},{2,3},{3,4},{4,5},{5,6},{6,7},{7,8},{8,9},{9,10},{10,1... | collective-permute-start | bytes 1544 | tf_op jit(solution)/shard_map/ppermute | solution.py:32
  12.0 5.6 %collective-permute-start.2 = (f32[8,258]{1,0:T(8,128)S(1)}, f32[8,258]{1,0:T(8,128)S(1)}, u32[]{:S(2)}, u32[]{:S(2)}) collective-permute-start(f32[8,258]{1,0:T(8,128)S(1)} %get-tuple-element.42), channel_id=1, source_target_pairs={{0,32},{32,64},{64,96},{96,128},{128,160},{160,192},{192,224},{1,3... | collective-permute-start | bytes 24776 | tf_op jit(solution)/shard_map/ppermute | solution.py:32
  14.0 5.0 %collective-permute-start.3 = (f32[8,258]{1,0:T(8,128)S(1)}, f32[8,258]{1,0:T(8,128)S(1)}, u32[]{:S(2)}, u32[]{:S(2)}) collective-permute-start(f32[8,258]{1,0:T(8,128)S(1)} %get-tuple-element.43), channel_id=1, source_target_pairs={{32,0},{64,32},{96,64},{128,96},{160,128},{192,160},{224,192},{33,... | collective-permute-start | bytes 24776 | tf_op jit(solution)/shard_map/ppermute | solution.py:33
  19.1 5.0 %collective-permute-start.4 = (f32[18,258]{1,0:T(8,128)S(1)}, f32[18,258]{1,0:T(8,128)S(1)}, u32[]{:S(2)}, u32[]{:S(2)}) collective-permute-start(f32[18,258]{1,0:T(8,128)S(1)} %get-tuple-element.26), channel_id=1, source_target_pairs={{0,256},{256,512},{512,768},{1,257},{257,513},{513,769},{2,258},{2... | collective-permute-start | bytes 55736 | tf_op jit(solution)/shard_map/ppermute | solution.py:32
  22.6 5.9 %collective-permute-start.5 = (f32[18,258]{1,0:T(8,128)S(1)}, f32[18,258]{1,0:T(8,128)S(1)}, u32[]{:S(2)}, u32[]{:S(2)}) collective-permute-start(f32[18,258]{1,0:T(8,128)S(1)} %get-tuple-element.27), channel_id=1, source_target_pairs={{256,0},{512,256},{768,512},{257,1},{513,257},{769,513},{258,2},{5... | collective-permute-start | bytes 55736 | tf_op jit(solution)/shard_map/ppermute | solution.py:33
  28.6 0.9 copy-start.3
  29.5 0.8 copy-start.2
  30.6 0.7 copy-start.4
  31.7 0.7 copy-start.6
  33.2 5.6 %collective-permute-start.6 = (f32[8,16]{1,0:T(8,128)S(1)}, f32[8,16]{1,0:T(8,128)S(1)}, u32[]{:S(2)}, u32[]{:S(2)}) collective-permute-start(f32[8,16]{1,0:T(8,128)S(1)} %bitcast.235), channel_id=1, source_target_pairs={{0,1},{1,2},{2,3},{3,4},{4,5},{5,6},{6,7},{7,8},{8,9},{9,10},{10,1... | collective-permute-start | bytes 1544 | tf_op jit(solution)/shard_map/ppermute | solution.py:32
  37.6 5.5 %collective-permute-start.7 = (f32[8,16]{1,0:T(8,128)S(1)}, f32[8,16]{1,0:T(8,128)S(1)}, u32[]{:S(2)}, u32[]{:S(2)}) collective-permute-start(f32[8,16]{1,0:T(8,128)S(1)} %bitcast.245), channel_id=1, source_target_pairs={{1,0},{2,1},{3,2},{4,3},{5,4},{6,5},{7,6},{8,7},{9,8},{10,9},{11,1... | collective-permute-start | bytes 1544 | tf_op jit(solution)/shard_map/ppermute | solution.py:33
  43.3 5.6 %collective-permute-start.8 = (f32[8,258]{1,0:T(8,128)S(1)}, f32[8,258]{1,0:T(8,128)S(1)}, u32[]{:S(2)}, u32[]{:S(2)}) collective-permute-start(f32[8,258]{1,0:T(8,128)S(1)} %get-tuple-element.40), channel_id=1, source_target_pairs={{0,32},{32,64},{64,96},{96,128},{128,160},{160,192},{192,224},{1,3... | collective-permute-start | bytes 24776 | tf_op jit(solution)/shard_map/ppermute | solution.py:32
  45.3 5.0 %collective-permute-start.9 = (f32[8,258]{1,0:T(8,128)S(1)}, f32[8,258]{1,0:T(8,128)S(1)}, u32[]{:S(2)}, u32[]{:S(2)}) collective-permute-start(f32[8,258]{1,0:T(8,128)S(1)} %get-tuple-element.41), channel_id=1, source_target_pairs={{32,0},{64,32},{96,64},{128,96},{160,128},{192,160},{224,192},{33,... | collective-permute-start | bytes 24776 | tf_op jit(solution)/shard_map/ppermute | solution.py:33
  50.4 5.0 %collective-permute-start.10 = (f32[18,258]{1,0:T(8,128)S(1)}, f32[18,258]{1,0:T(8,128)S(1)}, u32[]{:S(2)}, u32[]{:S(2)}) collective-permute-start(f32[18,258]{1,0:T(8,128)S(1)} %get-tuple-element.24), channel_id=1, source_target_pairs={{0,256},{256,512},{512,768},{1,257},{257,513},{513,769},{2,258},{2... | collective-permute-start | bytes 55736 | tf_op jit(solution)/shard_map/ppermute | solution.py:32
  53.8 5.9 %collective-permute-start.11 = (f32[18,258]{1,0:T(8,128)S(1)}, f32[18,258]{1,0:T(8,128)S(1)}, u32[]{:S(2)}, u32[]{:S(2)}) collective-permute-start(f32[18,258]{1,0:T(8,128)S(1)} %get-tuple-element.25), channel_id=1, source_target_pairs={{256,0},{512,256},{768,512},{257,1},{513,257},{769,513},{258,2},{5... | collective-permute-start | bytes 55736 | tf_op jit(solution)/shard_map/ppermute | solution.py:33
  62.3 6.0 %collective-permute-start.12 = (f32[8,16]{1,0:T(8,128)S(1)}, f32[8,16]{1,0:T(8,128)S(1)}, u32[]{:S(2)}, u32[]{:S(2)}) collective-permute-start(f32[8,16]{1,0:T(8,128)S(1)} %bitcast.237), channel_id=1, source_target_pairs={{0,1},{1,2},{2,3},{3,4},{4,5},{5,6},{6,7},{7,8},{8,9},{9,10},{10,1... | collective-permute-start | bytes 1544 | tf_op jit(solution)/shard_map/ppermute | solution.py:32
  67.0 7.0 %collective-permute-start.13 = (f32[8,16]{1,0:T(8,128)S(1)}, f32[8,16]{1,0:T(8,128)S(1)}, u32[]{:S(2)}, u32[]{:S(2)}) collective-permute-start(f32[8,16]{1,0:T(8,128)S(1)} %bitcast.247), channel_id=1, source_target_pairs={{1,0},{2,1},{3,2},{4,3},{5,4},{6,5},{7,6},{8,7},{9,8},{10,9},{11,1... | collective-permute-start | bytes 1544 | tf_op jit(solution)/shard_map/ppermute | solution.py:33
  74.2 5.6 %collective-permute-start.14 = (f32[8,258]{1,0:T(8,128)S(1)}, f32[8,258]{1,0:T(8,128)S(1)}, u32[]{:S(2)}, u32[]{:S(2)}) collective-permute-start(f32[8,258]{1,0:T(8,128)S(1)} %get-tuple-element.38), channel_id=1, source_target_pairs={{0,32},{32,64},{64,96},{96,128},{128,160},{160,192},{192,224},{1,3... | collective-permute-start | bytes 24776 | tf_op jit(solution)/shard_map/ppermute | solution.py:32
  76.2 5.0 %collective-permute-start.15 = (f32[8,258]{1,0:T(8,128)S(1)}, f32[8,258]{1,0:T(8,128)S(1)}, u32[]{:S(2)}, u32[]{:S(2)}) collective-permute-start(f32[8,258]{1,0:T(8,128)S(1)} %get-tuple-element.39), channel_id=1, source_target_pairs={{32,0},{64,32},{96,64},{128,96},{160,128},{192,160},{224,192},{33,... | collective-permute-start | bytes 24776 | tf_op jit(solution)/shard_map/ppermute | solution.py:33
  81.3 4.7 %collective-permute-start.16 = (f32[18,258]{1,0:T(8,128)S(1)}, f32[18,258]{1,0:T(8,128)S(1)}, u32[]{:S(2)}, u32[]{:S(2)}) collective-permute-start(f32[18,258]{1,0:T(8,128)S(1)} %get-tuple-element.22), channel_id=1, source_target_pairs={{0,256},{256,512},{512,768},{1,257},{257,513},{513,769},{2,258},{2... | collective-permute-start | bytes 55736 | tf_op jit(solution)/shard_map/ppermute | solution.py:32
  84.4 5.9 %collective-permute-start.17 = (f32[18,258]{1,0:T(8,128)S(1)}, f32[18,258]{1,0:T(8,128)S(1)}, u32[]{:S(2)}, u32[]{:S(2)}) collective-permute-start(f32[18,258]{1,0:T(8,128)S(1)} %get-tuple-element.23), channel_id=1, source_target_pairs={{256,0},{512,256},{768,512},{257,1},{513,257},{769,513},{258,2},{5... | collective-permute-start | bytes 55736 | tf_op jit(solution)/shard_map/ppermute | solution.py:33
  93.0 6.6 %collective-permute-start.18 = (f32[8,16]{1,0:T(8,128)S(1)}, f32[8,16]{1,0:T(8,128)S(1)}, u32[]{:S(2)}, u32[]{:S(2)}) collective-permute-start(f32[8,16]{1,0:T(8,128)S(1)} %bitcast.239), channel_id=1, source_target_pairs={{0,1},{1,2},{2,3},{3,4},{4,5},{5,6},{6,7},{7,8},{8,9},{9,10},{10,1... | collective-permute-start | bytes 1544 | tf_op jit(solution)/shard_map/ppermute | solution.py:32
  98.2 5.5 %collective-permute-start.19 = (f32[8,16]{1,0:T(8,128)S(1)}, f32[8,16]{1,0:T(8,128)S(1)}, u32[]{:S(2)}, u32[]{:S(2)}) collective-permute-start(f32[8,16]{1,0:T(8,128)S(1)} %bitcast.249), channel_id=1, source_target_pairs={{1,0},{2,1},{3,2},{4,3},{5,4},{6,5},{7,6},{8,7},{9,8},{10,9},{11,1... | collective-permute-start | bytes 1544 | tf_op jit(solution)/shard_map/ppermute | solution.py:33
  104.0 5.6 %collective-permute-start.20 = (f32[8,258]{1,0:T(8,128)S(1)}, f32[8,258]{1,0:T(8,128)S(1)}, u32[]{:S(2)}, u32[]{:S(2)}) collective-permute-start(f32[8,258]{1,0:T(8,128)S(1)} %get-tuple-element.36), channel_id=1, source_target_pairs={{0,32},{32,64},{64,96},{96,128},{128,160},{160,192},{192,224},{1,3... | collective-permute-start | bytes 24776 | tf_op jit(solution)/shard_map/ppermute | solution.py:32
  106.0 5.0 %collective-permute-start.21 = (f32[8,258]{1,0:T(8,128)S(1)}, f32[8,258]{1,0:T(8,128)S(1)}, u32[]{:S(2)}, u32[]{:S(2)}) collective-permute-start(f32[8,258]{1,0:T(8,128)S(1)} %get-tuple-element.37), channel_id=1, source_target_pairs={{32,0},{64,32},{96,64},{128,96},{160,128},{192,160},{224,192},{33,... | collective-permute-start | bytes 24776 | tf_op jit(solution)/shard_map/ppermute | solution.py:33
  111.1 5.9 %collective-permute-start.23 = (f32[18,258]{1,0:T(8,128)S(1)}, f32[18,258]{1,0:T(8,128)S(1)}, u32[]{:S(2)}, u32[]{:S(2)}) collective-permute-start(f32[18,258]{1,0:T(8,128)S(1)} %get-tuple-element.18), channel_id=1, source_target_pairs={{256,0},{512,256},{768,512},{257,1},{513,257},{769,513},{258,2},{5... | collective-permute-start | bytes 55736 | tf_op jit(solution)/shard_map/ppermute | solution.py:33
  112.4 6.2 %collective-permute-start.22 = (f32[18,258]{1,0:T(8,128)S(1)}, f32[18,258]{1,0:T(8,128)S(1)}, u32[]{:S(2)}, u32[]{:S(2)}) collective-permute-start(f32[18,258]{1,0:T(8,128)S(1)} %get-tuple-element.19), channel_id=1, source_target_pairs={{0,256},{256,512},{512,768},{1,257},{257,513},{513,769},{2,258},{2... | collective-permute-start | bytes 55736 | tf_op jit(solution)/shard_map/ppermute | solution.py:32
  121.2 5.5 %collective-permute-start.24 = (f32[8,16]{1,0:T(8,128)S(1)}, f32[8,16]{1,0:T(8,128)S(1)}, u32[]{:S(2)}, u32[]{:S(2)}) collective-permute-start(f32[8,16]{1,0:T(8,128)S(1)} %bitcast.241), channel_id=1, source_target_pairs={{0,1},{1,2},{2,3},{3,4},{4,5},{5,6},{6,7},{7,8},{8,9},{9,10},{10,1... | collective-permute-start | bytes 1544 | tf_op jit(solution)/shard_map/ppermute | solution.py:32
  125.2 5.5 %collective-permute-start.25 = (f32[8,16]{1,0:T(8,128)S(1)}, f32[8,16]{1,0:T(8,128)S(1)}, u32[]{:S(2)}, u32[]{:S(2)}) collective-permute-start(f32[8,16]{1,0:T(8,128)S(1)} %bitcast.251), channel_id=1, source_target_pairs={{1,0},{2,1},{3,2},{4,3},{5,4},{6,5},{7,6},{8,7},{9,8},{10,9},{11,1... | collective-permute-start | bytes 1544 | tf_op jit(solution)/shard_map/ppermute | solution.py:33
  131.0 5.6 %collective-permute-start.26 = (f32[8,258]{1,0:T(8,128)S(1)}, f32[8,258]{1,0:T(8,128)S(1)}, u32[]{:S(2)}, u32[]{:S(2)}) collective-permute-start(f32[8,258]{1,0:T(8,128)S(1)} %get-tuple-element.34), channel_id=1, source_target_pairs={{0,32},{32,64},{64,96},{96,128},{128,160},{160,192},{192,224},{1,3... | collective-permute-start | bytes 24776 | tf_op jit(solution)/shard_map/ppermute | solution.py:32
  132.9 5.0 %collective-permute-start.27 = (f32[8,258]{1,0:T(8,128)S(1)}, f32[8,258]{1,0:T(8,128)S(1)}, u32[]{:S(2)}, u32[]{:S(2)}) collective-permute-start(f32[8,258]{1,0:T(8,128)S(1)} %get-tuple-element.35), channel_id=1, source_target_pairs={{32,0},{64,32},{96,64},{128,96},{160,128},{192,160},{224,192},{33,... | collective-permute-start | bytes 24776 | tf_op jit(solution)/shard_map/ppermute | solution.py:33
  138.1 5.9 %collective-permute-start.28 = (f32[18,258]{1,0:T(8,128)S(1)}, f32[18,258]{1,0:T(8,128)S(1)}, u32[]{:S(2)}, u32[]{:S(2)}) collective-permute-start(f32[18,258]{1,0:T(8,128)S(1)} %get-tuple-element.16), channel_id=1, source_target_pairs={{0,256},{256,512},{512,768},{1,257},{257,513},{513,769},{2,258},{2... | collective-permute-start | bytes 55736 | tf_op jit(solution)/shard_map/ppermute | solution.py:32
  142.3 5.9 %collective-permute-start.29 = (f32[18,258]{1,0:T(8,128)S(1)}, f32[18,258]{1,0:T(8,128)S(1)}, u32[]{:S(2)}, u32[]{:S(2)}) collective-permute-start(f32[18,258]{1,0:T(8,128)S(1)} %get-tuple-element.17), channel_id=1, source_target_pairs={{256,0},{512,256},{768,512},{257,1},{513,257},{769,513},{258,2},{5... | collective-permute-start | bytes 55736 | tf_op jit(solution)/shard_map/ppermute | solution.py:33
  148.4 0.9 copy-start.5
  150.0 3.1 %collective-permute-start.30 = (f32[8192]{0:T(1024)S(1)}, f32[8192]{0:T(1024)S(1)}, u32[]{:S(2)}, u32[]{:S(2)}) collective-permute-start(f32[8192]{0:T(1024)S(1)} %bitcast.216), channel_id=1, source_target_pairs={{0,32},{32,0},{64,96},{96,64},{128,160},{160,128},{192,224},{224,1... | collective-permute-start | bytes 98312 | tf_op jit(solution)/shard_map/ppermute | solution.py:43
  153.1 5.8 %collective-permute-start.31 = (f32[8192]{0:T(1024)S(1)}, f32[8192]{0:T(1024)S(1)}, u32[]{:S(2)}, u32[]{:S(2)}) collective-permute-start(f32[8192]{0:T(1024)S(1)} %add.340), channel_id=1, source_target_pairs={{0,64},{32,96},{64,0},{96,32},{128,192},{160,224},{192,128},{224,1... | collective-permute-start | bytes 98312 | tf_op jit(solution)/shard_map/ppermute | solution.py:43
  158.9 7.3 %collective-permute-start.32 = (f32[8192]{0:T(1024)S(1)}, f32[8192]{0:T(1024)S(1)}, u32[]{:S(2)}, u32[]{:S(2)}) collective-permute-start(f32[8192]{0:T(1024)S(1)} %add.341), channel_id=1, source_target_pairs={{0,128},{32,160},{64,192},{96,224},{128,0},{160,32},{192,64},{224,... | collective-permute-start | bytes 98312 | tf_op jit(solution)/shard_map/ppermute | solution.py:43
  166.2 6.6 %collective-permute-start.33 = (f32[8192]{0:T(1024)S(1)}, f32[8192]{0:T(1024)S(1)}, u32[]{:S(2)}, u32[]{:S(2)}) collective-permute-start(f32[8192]{0:T(1024)S(1)} %add.342), channel_id=1, source_target_pairs={{0,1},{1,0},{2,3},{3,2},{4,5},{5,4},{6,7},{7,6},{8,9},{9,8},{10,11... | collective-permute-start | bytes 98312 | tf_op jit(solution)/shard_map/ppermute | solution.py:43
  172.9 8.5 %collective-permute-start.34 = (f32[8192]{0:T(1024)S(1)}, f32[8192]{0:T(1024)S(1)}, u32[]{:S(2)}, u32[]{:S(2)}) collective-permute-start(f32[8192]{0:T(1024)S(1)} %add.343), channel_id=1, source_target_pairs={{0,2},{1,3},{2,0},{3,1},{4,6},{5,7},{6,4},{7,5},{8,10},{9,11},{10,... | collective-permute-start | bytes 98312 | tf_op jit(solution)/shard_map/ppermute | solution.py:43
  181.3 11.0 %collective-permute-start.35 = (f32[8192]{0:T(1024)S(1)}, f32[8192]{0:T(1024)S(1)}, u32[]{:S(2)}, u32[]{:S(2)}) collective-permute-start(f32[8192]{0:T(1024)S(1)} %add.344), channel_id=1, source_target_pairs={{0,4},{1,5},{2,6},{3,7},{4,0},{5,1},{6,2},{7,3},{8,12},{9,13},{10,... | collective-permute-start | bytes 98312 | tf_op jit(solution)/shard_map/ppermute | solution.py:43
  192.3 30.5 %collective-permute-start.38 = (f32[8192]{0:T(1024)S(1)}, f32[8192]{0:T(1024)S(1)}, u32[]{:S(2)}, u32[]{:S(2)}) collective-permute-start(f32[8192]{0:T(1024)S(1)} %add.345), channel_id=1, source_target_pairs={{0,24},{1,25},{2,26},{3,27},{4,28},{5,29},{6,30},{7,31},{8,16},{9,... | collective-permute-start | bytes 98312 | tf_op jit(solution)/shard_map/ppermute | solution.py:43
  208.7 24.3 %collective-permute-start.37 = (f32[8192]{0:T(1024)S(1)}, f32[8192]{0:T(1024)S(1)}, u32[]{:S(2)}, u32[]{:S(2)}) collective-permute-start(f32[8192]{0:T(1024)S(1)} %add.345), channel_id=1, source_target_pairs={{0,16},{1,17},{2,18},{3,19},{4,20},{5,21},{6,22},{7,23},{8,24},{9,... | collective-permute-start | bytes 98312 | tf_op jit(solution)/shard_map/ppermute | solution.py:43
  218.8 15.5 %collective-permute-start.36 = (f32[8192]{0:T(1024)S(1)}, f32[8192]{0:T(1024)S(1)}, u32[]{:S(2)}, u32[]{:S(2)}) collective-permute-start(f32[8192]{0:T(1024)S(1)} %add.345), channel_id=1, source_target_pairs={{0,8},{1,9},{2,10},{3,11},{4,12},{5,13},{6,14},{7,15},{8,0},{9,1},... | collective-permute-start | bytes 98312 | tf_op jit(solution)/shard_map/ppermute | solution.py:43
  234.4 5.8 %collective-permute-start.39 = (f32[8192]{0:T(1024)S(1)}, f32[8192]{0:T(1024)S(1)}, u32[]{:S(2)}, u32[]{:S(2)}) collective-permute-start(f32[8192]{0:T(1024)S(1)} %add_add_fusion), channel_id=1, source_target_pairs={{0,256},{256,0},{512,768},{768,512},{1,257},{257,1},{513,769},{769... | collective-permute-start | bytes 98312 | tf_op jit(solution)/shard_map/ppermute | solution.py:43
  240.2 7.3 %collective-permute-start.40 = (f32[8192]{0:T(1024)S(1)}, f32[8192]{0:T(1024)S(1)}, u32[]{:S(2)}, u32[]{:S(2)}) collective-permute-start(f32[8192]{0:T(1024)S(1)} %add.349), channel_id=1, source_target_pairs={{0,512},{256,768},{512,0},{768,256},{1,513},{257,769},{513,1},{769... | collective-permute-start | bytes 98312 | tf_op jit(solution)/shard_map/ppermute | solution.py:43
  248.2 0.5 copy-start.13

commit v4 on v2

--- a/solution.py
+++ b/solution.py
@@ -38,13 +38,22 @@
     return cells
 
 
+def group_partner(index, size, pairing):
+    group = index // size
+    return index + (pairing(group) - group) * size
+
+
 def butterfly_sum(value, axes):
     for axis in axes:
         count = lax.axis_size(axis)
+        size = count // 4
         stride = 1
-        while stride < count:
+        while stride < size:
             value = value + lax.ppermute(value, axis, [(i, i ^ stride) for i in range(count)])
             stride *= 2
+        for pairing in (lambda g: 3 - g, lambda g: g ^ 1):
+            pairs = [(i, group_partner(i, size, pairing)) for i in range(count)]
+            value = value + lax.ppermute(value, axis, pairs)
     return value
 
 

time: 250 us -> 241 us (0.964)
  starting transfers between devices: 150 us -> 139 us
  waiting for transfers between devices: 73.1 us -> 76 us
    ppermute x10 -> x4, starting transfers between devices: 67.9 us -> 22.3 us  [butterfly_sum(): lax.ppermute(value, axis, [(i, i ^ stride) for i in range(count)])]
    ppermute x0 -> x6, starting transfers between devices: none -> 34.6 us  [butterfly_sum(): value = value + lax.ppermute(value, axis, pairs)]
    ppermute x0 -> x6, waiting for transfers between devices: none -> 24.1 us  [butterfly_sum(): value = value + lax.ppermute(value, axis, pairs)]
    ppermute x10 -> x4, waiting for transfers between devices: 28 us -> 6.81 us  [butterfly_sum(): lax.ppermute(value, axis, [(i, i ^ stride) for i in range(count)])]
where the time goes in v4:
time: 241 us; the launch traced here: 240 us
  starting transfers between devices  139 us (58%)
  waiting for transfers between devices  76 us (32%)
  local copies, waits for them, and re-layouts  9.34 us (4%)
  matrix products  8.83 us (4%)
  other arithmetic  5.29 us (2%)
    ppermute x15, starting transfers between devices, padded_2(): lax.ppermute(jnp.squeeze(tail, dim), axis, [(i, i + 1) for i in range(end...  50.6 us
    ppermute x15, waiting for transfers between devices, padded_2(): lax.ppermute(jnp.squeeze(head, dim), axis, [(i + 1, i) for i in range(end...  41 us
    ppermute x6, starting transfers between devices, butterfly_sum(): value = value + lax.ppermute(value, axis, pairs)  34.6 us
    ppermute x15, starting transfers between devices, padded_2(): lax.ppermute(jnp.squeeze(head, dim), axis, [(i + 1, i) for i in range(end...  31.3 us
    ppermute x6, waiting for transfers between devices, butterfly_sum(): value = value + lax.ppermute(value, axis, pairs)  24.1 us
    ppermute x4, starting transfers between devices, butterfly_sum(): lax.ppermute(value, axis, [(i, i ^ stride) for i in range(count)])  22.3 us
    ppermute x4, waiting for transfers between devices, butterfly_sum(): lax.ppermute(value, axis, [(i, i ^ stride) for i in range(count)])  6.81 us
    unnamed x29, local copies, waits for them, and re-layouts  5.7 us
  transfers between devices with their start and end apart: 40, of which 29 were waited for; matrix products, arithmetic and copies ran while one was open for 1% of the time, Pallas kernels for 0%

profile of v4, /device:TPU:24, one launch (start us, length us, event | category | flops | bytes accessed | tf_op | source)
XLA Modules:
  0.0 240.1 jit_solution(1044711607001735638)
XLA Ops:
  4.3 1.3 collective-permute-start.1
  5.8 4.5 %collective-permute-start = (f32[8,16]{1,0:T(8,128)S(1)}, f32[8,16]{1,0:T(8,128)S(1)}, u32[]{:S(2)}, u32[]{:S(2)}) collective-permute-start(f32[8,16]{1,0:T(8,128)S(1)} %bitcast.243), channel_id=1, source_target_pairs={{0,1},{1,2},{2,3},{3,4},{4,5},{5,6},{6,7},{7,8},{8,9},{9,10},{10,1... | collective-permute-start | bytes 1544 | tf_op jit(solution)/shard_map/ppermute | solution.py:32
  10.3 1.3 collective-permute-done
  12.0 1.9 collective-permute-start.2
  14.0 3.6 %collective-permute-start.3 = (f32[8,258]{1,0:T(8,128)S(1)}, f32[8,258]{1,0:T(8,128)S(1)}, u32[]{:S(2)}, u32[]{:S(2)}) collective-permute-start(f32[8,258]{1,0:T(8,128)S(1)} %get-tuple-element.43), channel_id=1, source_target_pairs={{32,0},{64,32},{96,64},{128,96},{160,128},{192,160},{224,192},{33,... | collective-permute-start | bytes 24776 | tf_op jit(solution)/shard_map/ppermute | solution.py:33
  17.7 1.3 collective-permute-done.3
  19.1 3.4 %collective-permute-start.4 = (f32[18,258]{1,0:T(8,128)S(1)}, f32[18,258]{1,0:T(8,128)S(1)}, u32[]{:S(2)}, u32[]{:S(2)}) collective-permute-start(f32[18,258]{1,0:T(8,128)S(1)} %get-tuple-element.26), channel_id=1, source_target_pairs={{0,256},{256,512},{512,768},{1,257},{257,513},{513,769},{2,258},{2... | collective-permute-start | bytes 55736 | tf_op jit(solution)/shard_map/ppermute | solution.py:32
  22.6 1.3 collective-permute-start.5
  24.2 4.2 %collective-permute-done.5 = f32[18,258]{1,0:T(8,128)S(1)} collective-permute-done((f32[18,258]{1,0:T(8,128)S(1)}, f32[18,258]{1,0:T(8,128)S(1)}, u32[]{:S(2)}, u32[]{:S(2)}) %collective-permute-start.5) | collective-permute-done | bytes 18608 | tf_op jit(solution)/shard_map/ppermute | solution.py:33
  33.2 4.2 %collective-permute-start.6 = (f32[8,16]{1,0:T(8,128)S(1)}, f32[8,16]{1,0:T(8,128)S(1)}, u32[]{:S(2)}, u32[]{:S(2)}) collective-permute-start(f32[8,16]{1,0:T(8,128)S(1)} %bitcast.235), channel_id=1, source_target_pairs={{0,1},{1,2},{2,3},{3,4},{4,5},{5,6},{6,7},{7,8},{8,9},{9,10},{10,1... | collective-permute-start | bytes 1544 | tf_op jit(solution)/shard_map/ppermute | solution.py:32
  37.6 1.3 collective-permute-start.7
  39.0 4.1 %collective-permute-done.7 = f32[8,16]{1,0:T(8,128)S(1)} collective-permute-done((f32[8,16]{1,0:T(8,128)S(1)}, f32[8,16]{1,0:T(8,128)S(1)}, u32[]{:S(2)}, u32[]{:S(2)}) %collective-permute-start.7) | collective-permute-done | bytes 544 | tf_op jit(solution)/shard_map/ppermute | solution.py:33
  43.3 1.9 collective-permute-start.8
  45.3 3.6 %collective-permute-start.9 = (f32[8,258]{1,0:T(8,128)S(1)}, f32[8,258]{1,0:T(8,128)S(1)}, u32[]{:S(2)}, u32[]{:S(2)}) collective-permute-start(f32[8,258]{1,0:T(8,128)S(1)} %get-tuple-element.41), channel_id=1, source_target_pairs={{32,0},{64,32},{96,64},{128,96},{160,128},{192,160},{224,192},{33,... | collective-permute-start | bytes 24776 | tf_op jit(solution)/shard_map/ppermute | solution.py:33
  49.0 1.3 collective-permute-done.9
  50.4 3.4 %collective-permute-start.10 = (f32[18,258]{1,0:T(8,128)S(1)}, f32[18,258]{1,0:T(8,128)S(1)}, u32[]{:S(2)}, u32[]{:S(2)}) collective-permute-start(f32[18,258]{1,0:T(8,128)S(1)} %get-tuple-element.24), channel_id=1, source_target_pairs={{0,256},{256,512},{512,768},{1,257},{257,513},{513,769},{2,258},{2... | collective-permute-start | bytes 55736 | tf_op jit(solution)/shard_map/ppermute | solution.py:32
  53.8 1.3 collective-permute-start.11
  55.4 4.2 %collective-permute-done.11 = f32[18,258]{1,0:T(8,128)S(1)} collective-permute-done((f32[18,258]{1,0:T(8,128)S(1)}, f32[18,258]{1,0:T(8,128)S(1)}, u32[]{:S(2)}, u32[]{:S(2)}) %collective-permute-start.11) | collective-permute-done | bytes 18608 | tf_op jit(solution)/shard_map/ppermute | solution.py:33
  62.3 4.6 %collective-permute-start.12 = (f32[8,16]{1,0:T(8,128)S(1)}, f32[8,16]{1,0:T(8,128)S(1)}, u32[]{:S(2)}, u32[]{:S(2)}) collective-permute-start(f32[8,16]{1,0:T(8,128)S(1)} %bitcast.237), channel_id=1, source_target_pairs={{0,1},{1,2},{2,3},{3,4},{4,5},{5,6},{6,7},{7,8},{8,9},{9,10},{10,1... | collective-permute-start | bytes 1544 | tf_op jit(solution)/shard_map/ppermute | solution.py:32
  67.0 1.3 collective-permute-start.13
  68.4 5.5 %collective-permute-done.13 = f32[8,16]{1,0:T(8,128)S(1)} collective-permute-done((f32[8,16]{1,0:T(8,128)S(1)}, f32[8,16]{1,0:T(8,128)S(1)}, u32[]{:S(2)}, u32[]{:S(2)}) %collective-permute-start.13) | collective-permute-done | bytes 544 | tf_op jit(solution)/shard_map/ppermute | solution.py:33
  74.2 1.9 collective-permute-start.14
  76.2 3.6 %collective-permute-start.15 = (f32[8,258]{1,0:T(8,128)S(1)}, f32[8,258]{1,0:T(8,128)S(1)}, u32[]{:S(2)}, u32[]{:S(2)}) collective-permute-start(f32[8,258]{1,0:T(8,128)S(1)} %get-tuple-element.39), channel_id=1, source_target_pairs={{32,0},{64,32},{96,64},{128,96},{160,128},{192,160},{224,192},{33,... | collective-permute-start | bytes 24776 | tf_op jit(solution)/shard_map/ppermute | solution.py:33
  79.9 1.3 collective-permute-done.15
  81.3 3.1 %collective-permute-start.16 = (f32[18,258]{1,0:T(8,128)S(1)}, f32[18,258]{1,0:T(8,128)S(1)}, u32[]{:S(2)}, u32[]{:S(2)}) collective-permute-start(f32[18,258]{1,0:T(8,128)S(1)} %get-tuple-element.22), channel_id=1, source_target_pairs={{0,256},{256,512},{512,768},{1,257},{257,513},{513,769},{2,258},{2... | collective-permute-start | bytes 55736 | tf_op jit(solution)/shard_map/ppermute | solution.py:32
  84.4 1.3 collective-permute-start.17
  86.0 4.2 %collective-permute-done.17 = f32[18,258]{1,0:T(8,128)S(1)} collective-permute-done((f32[18,258]{1,0:T(8,128)S(1)}, f32[18,258]{1,0:T(8,128)S(1)}, u32[]{:S(2)}, u32[]{:S(2)}) %collective-permute-start.17) | collective-permute-done | bytes 18608 | tf_op jit(solution)/shard_map/ppermute | solution.py:33
  93.0 5.1 %collective-permute-start.18 = (f32[8,16]{1,0:T(8,128)S(1)}, f32[8,16]{1,0:T(8,128)S(1)}, u32[]{:S(2)}, u32[]{:S(2)}) collective-permute-start(f32[8,16]{1,0:T(8,128)S(1)} %bitcast.239), channel_id=1, source_target_pairs={{0,1},{1,2},{2,3},{3,4},{4,5},{5,6},{6,7},{7,8},{8,9},{9,10},{10,1... | collective-permute-start | bytes 1544 | tf_op jit(solution)/shard_map/ppermute | solution.py:32
  98.2 1.3 collective-permute-start.19
  99.7 4.1 %collective-permute-done.19 = f32[8,16]{1,0:T(8,128)S(1)} collective-permute-done((f32[8,16]{1,0:T(8,128)S(1)}, f32[8,16]{1,0:T(8,128)S(1)}, u32[]{:S(2)}, u32[]{:S(2)}) %collective-permute-start.19) | collective-permute-done | bytes 544 | tf_op jit(solution)/shard_map/ppermute | solution.py:33
  104.0 1.9 collective-permute-start.20
  106.0 3.6 %collective-permute-start.21 = (f32[8,258]{1,0:T(8,128)S(1)}, f32[8,258]{1,0:T(8,128)S(1)}, u32[]{:S(2)}, u32[]{:S(2)}) collective-permute-start(f32[8,258]{1,0:T(8,128)S(1)} %get-tuple-element.37), channel_id=1, source_target_pairs={{32,0},{64,32},{96,64},{128,96},{160,128},{192,160},{224,192},{33,... | collective-permute-start | bytes 24776 | tf_op jit(solution)/shard_map/ppermute | solution.py:33
  109.7 1.3 collective-permute-done.21
  111.1 1.3 collective-permute-start.23
  112.4 4.5 %collective-permute-start.22 = (f32[18,258]{1,0:T(8,128)S(1)}, f32[18,258]{1,0:T(8,128)S(1)}, u32[]{:S(2)}, u32[]{:S(2)}) collective-permute-start(f32[18,258]{1,0:T(8,128)S(1)} %get-tuple-element.19), channel_id=1, source_target_pairs={{0,256},{256,512},{512,768},{1,257},{257,513},{513,769},{2,258},{2... | collective-permute-start | bytes 55736 | tf_op jit(solution)/shard_map/ppermute | solution.py:32
  116.9 1.6 collective-permute-done.22
  121.2 3.9 %collective-permute-start.24 = (f32[8,16]{1,0:T(8,128)S(1)}, f32[8,16]{1,0:T(8,128)S(1)}, u32[]{:S(2)}, u32[]{:S(2)}) collective-permute-start(f32[8,16]{1,0:T(8,128)S(1)} %bitcast.241), channel_id=1, source_target_pairs={{0,1},{1,2},{2,3},{3,4},{4,5},{5,6},{6,7},{7,8},{8,9},{9,10},{10,1... | collective-permute-start | bytes 1544 | tf_op jit(solution)/shard_map/ppermute | solution.py:32
  125.2 1.5 collective-permute-start.25
  126.8 3.9 %collective-permute-done.25 = f32[8,16]{1,0:T(8,128)S(1)} collective-permute-done((f32[8,16]{1,0:T(8,128)S(1)}, f32[8,16]{1,0:T(8,128)S(1)}, u32[]{:S(2)}, u32[]{:S(2)}) %collective-permute-start.25) | collective-permute-done | bytes 544 | tf_op jit(solution)/shard_map/ppermute | solution.py:33
  131.0 1.9 collective-permute-start.26
  132.9 3.6 %collective-permute-start.27 = (f32[8,258]{1,0:T(8,128)S(1)}, f32[8,258]{1,0:T(8,128)S(1)}, u32[]{:S(2)}, u32[]{:S(2)}) collective-permute-start(f32[8,258]{1,0:T(8,128)S(1)} %get-tuple-element.35), channel_id=1, source_target_pairs={{32,0},{64,32},{96,64},{128,96},{160,128},{192,160},{224,192},{33,... | collective-permute-start | bytes 24776 | tf_op jit(solution)/shard_map/ppermute | solution.py:33
  136.7 1.3 collective-permute-done.27
  138.1 4.2 %collective-permute-start.28 = (f32[18,258]{1,0:T(8,128)S(1)}, f32[18,258]{1,0:T(8,128)S(1)}, u32[]{:S(2)}, u32[]{:S(2)}) collective-permute-start(f32[18,258]{1,0:T(8,128)S(1)} %get-tuple-element.16), channel_id=1, source_target_pairs={{0,256},{256,512},{512,768},{1,257},{257,513},{513,769},{2,258},{2... | collective-permute-start | bytes 55736 | tf_op jit(solution)/shard_map/ppermute | solution.py:32
  142.3 1.3 collective-permute-start.29
  143.9 4.2 %collective-permute-done.29 = f32[18,258]{1,0:T(8,128)S(1)} collective-permute-done((f32[18,258]{1,0:T(8,128)S(1)}, f32[18,258]{1,0:T(8,128)S(1)}, u32[]{:S(2)}, u32[]{:S(2)}) %collective-permute-start.29) | collective-permute-done | bytes 18608 | tf_op jit(solution)/shard_map/ppermute | solution.py:33
  150.0 1.9 collective-permute-start.30
  153.1 2.0 collective-permute-start.31
  155.1 5.0 %collective-permute-done.31 = f32[8192]{0:T(1024)S(1)} collective-permute-done((f32[8192]{0:T(1024)S(1)}, f32[8192]{0:T(1024)S(1)}, u32[]{:S(2)}, u32[]{:S(2)}) %collective-permute-start.31) | collective-permute-done | bytes 32800 | tf_op jit(solution)/shard_map/ppermute | solution.py:56
  160.1 1.9 collective-permute-start.32
  162.1 3.8 %collective-permute-done.32 = f32[8192]{0:T(1024)S(1)} collective-permute-done((f32[8192]{0:T(1024)S(1)}, f32[8192]{0:T(1024)S(1)}, u32[]{:S(2)}, u32[]{:S(2)}) %collective-permute-start.32) | collective-permute-done | bytes 32800 | tf_op jit(solution)/shard_map/ppermute | solution.py:56
  165.9 4.8 %collective-permute-start.33 = (f32[8192]{0:T(1024)S(1)}, f32[8192]{0:T(1024)S(1)}, u32[]{:S(2)}, u32[]{:S(2)}) collective-permute-start(f32[8192]{0:T(1024)S(1)} %add.339), channel_id=1, source_target_pairs={{0,1},{1,0},{2,3},{3,2},{4,5},{5,4},{6,7},{7,6},{8,9},{9,8},{10,11... | collective-permute-start | bytes 98312 | tf_op jit(solution)/shard_map/ppermute | solution.py:52
  170.7 1.9 collective-permute-done.33
  172.6 6.6 %collective-permute-start.34 = (f32[8192]{0:T(1024)S(1)}, f32[8192]{0:T(1024)S(1)}, u32[]{:S(2)}, u32[]{:S(2)}) collective-permute-start(f32[8192]{0:T(1024)S(1)} %add.340), channel_id=1, source_target_pairs={{0,2},{1,3},{2,0},{3,1},{4,6},{5,7},{6,4},{7,5},{8,10},{9,11},{10,... | collective-permute-start | bytes 98312 | tf_op jit(solution)/shard_map/ppermute | solution.py:52
  179.1 1.9 collective-permute-done.34
  181.0 9.1 %collective-permute-start.35 = (f32[8192]{0:T(1024)S(1)}, f32[8192]{0:T(1024)S(1)}, u32[]{:S(2)}, u32[]{:S(2)}) collective-permute-start(f32[8192]{0:T(1024)S(1)} %add.341), channel_id=1, source_target_pairs={{0,4},{1,5},{2,6},{3,7},{4,0},{5,1},{6,2},{7,3},{8,12},{9,13},{10,... | collective-permute-start | bytes 98312 | tf_op jit(solution)/shard_map/ppermute | solution.py:52
  190.1 1.9 collective-permute-done.35
  192.0 16.4 %collective-permute-start.36 = (f32[8192]{0:T(1024)S(1)}, f32[8192]{0:T(1024)S(1)}, u32[]{:S(2)}, u32[]{:S(2)}) collective-permute-start(f32[8192]{0:T(1024)S(1)} %add.342), channel_id=1, source_target_pairs={{0,24},{1,25},{2,26},{3,27},{4,28},{5,29},{6,30},{7,31},{8,16},{9,... | collective-permute-start | bytes 98312 | tf_op jit(solution)/shard_map/ppermute | solution.py:56
  208.4 2.2 collective-permute-done.36
  210.6 10.4 %collective-permute-start.37 = (f32[8192]{0:T(1024)S(1)}, f32[8192]{0:T(1024)S(1)}, u32[]{:S(2)}, u32[]{:S(2)}) collective-permute-start(f32[8192]{0:T(1024)S(1)} %add.343), channel_id=1, source_target_pairs={{0,8},{1,9},{2,10},{3,11},{4,12},{5,13},{6,14},{7,15},{8,0},{9,1},... | collective-permute-start | bytes 98312 | tf_op jit(solution)/shard_map/ppermute | solution.py:56
  221.0 4.1 %collective-permute-done.37 = f32[8192]{0:T(1024)S(1)} collective-permute-done((f32[8192]{0:T(1024)S(1)}, f32[8192]{0:T(1024)S(1)}, u32[]{:S(2)}, u32[]{:S(2)}) %collective-permute-start.37) | collective-permute-done | bytes 32800 | tf_op jit(solution)/shard_map/ppermute | solution.py:56
  225.1 1.9 collective-permute-start.38
  227.0 5.1 %collective-permute-done.38 = f32[8192]{0:T(1024)S(1)} collective-permute-done((f32[8192]{0:T(1024)S(1)}, f32[8192]{0:T(1024)S(1)}, u32[]{:S(2)}, u32[]{:S(2)}) %collective-permute-start.38) | collective-permute-done | bytes 32800 | tf_op jit(solution)/shard_map/ppermute | solution.py:56
  232.1 1.9 collective-permute-start.39
  234.1 3.9 %collective-permute-done.39 = f32[8192]{0:T(1024)S(1)} collective-permute-done((f32[8192]{0:T(1024)S(1)}, f32[8192]{0:T(1024)S(1)}, u32[]{:S(2)}, u32[]{:S(2)}) %collective-permute-start.39) | collective-permute-done | bytes 32800 | tf_op jit(solution)/shard_map/ppermute | solution.py:56
  (180 shorter events, 25.9 us)
Async XLA Ops:
  0.6 149.0 %copy-start = (f32[8,8192]{1,0:T(8,128)S(1)}, f32[8,8192]{1,0:T(8,128)}, u32[]{:S(2)}) copy-start(f32[8,8192]{1,0:T(8,128)} %param.13) | copy-start | bytes 786436
  0.6 0.7 copy-start.9
  0.7 0.7 copy-start.7
  0.7 0.7 copy-start.8
  0.7 1.7 copy-start.10
  0.7 1.7 copy-start.1
  2.4 0.7 copy-start.11
  3.1 0.7 copy-start.12
  4.3 7.4 %collective-permute-start.1 = (f32[8,16]{1,0:T(8,128)S(1)}, f32[8,16]{1,0:T(8,128)S(1)}, u32[]{:S(2)}, u32[]{:S(2)}) collective-permute-start(f32[8,16]{1,0:T(8,128)S(1)} %bitcast.233), channel_id=1, source_target_pairs={{1,0},{2,1},{3,2},{4,3},{5,4},{6,5},{7,6},{8,7},{9,8},{10,9},{11,1... | collective-permute-start | bytes 1544 | tf_op jit(solution)/shard_map/ppermute | solution.py:33
  5.8 5.9 %collective-permute-start = (f32[8,16]{1,0:T(8,128)S(1)}, f32[8,16]{1,0:T(8,128)S(1)}, u32[]{:S(2)}, u32[]{:S(2)}) collective-permute-start(f32[8,16]{1,0:T(8,128)S(1)} %bitcast.243), channel_id=1, source_target_pairs={{0,1},{1,2},{2,3},{3,4},{4,5},{5,6},{6,7},{7,8},{8,9},{9,10},{10,1... | collective-permute-start | bytes 1544 | tf_op jit(solution)/shard_map/ppermute | solution.py:32
  12.0 5.6 %collective-permute-start.2 = (f32[8,258]{1,0:T(8,128)S(1)}, f32[8,258]{1,0:T(8,128)S(1)}, u32[]{:S(2)}, u32[]{:S(2)}) collective-permute-start(f32[8,258]{1,0:T(8,128)S(1)} %get-tuple-element.42), channel_id=1, source_target_pairs={{0,32},{32,64},{64,96},{96,128},{128,160},{160,192},{192,224},{1,3... | collective-permute-start | bytes 24776 | tf_op jit(solution)/shard_map/ppermute | solution.py:32
  14.0 5.0 %collective-permute-start.3 = (f32[8,258]{1,0:T(8,128)S(1)}, f32[8,258]{1,0:T(8,128)S(1)}, u32[]{:S(2)}, u32[]{:S(2)}) collective-permute-start(f32[8,258]{1,0:T(8,128)S(1)} %get-tuple-element.43), channel_id=1, source_target_pairs={{32,0},{64,32},{96,64},{128,96},{160,128},{192,160},{224,192},{33,... | collective-permute-start | bytes 24776 | tf_op jit(solution)/shard_map/ppermute | solution.py:33
  19.1 5.0 %collective-permute-start.4 = (f32[18,258]{1,0:T(8,128)S(1)}, f32[18,258]{1,0:T(8,128)S(1)}, u32[]{:S(2)}, u32[]{:S(2)}) collective-permute-start(f32[18,258]{1,0:T(8,128)S(1)} %get-tuple-element.26), channel_id=1, source_target_pairs={{0,256},{256,512},{512,768},{1,257},{257,513},{513,769},{2,258},{2... | collective-permute-start | bytes 55736 | tf_op jit(solution)/shard_map/ppermute | solution.py:32
  22.6 5.9 %collective-permute-start.5 = (f32[18,258]{1,0:T(8,128)S(1)}, f32[18,258]{1,0:T(8,128)S(1)}, u32[]{:S(2)}, u32[]{:S(2)}) collective-permute-start(f32[18,258]{1,0:T(8,128)S(1)} %get-tuple-element.27), channel_id=1, source_target_pairs={{256,0},{512,256},{768,512},{257,1},{513,257},{769,513},{258,2},{5... | collective-permute-start | bytes 55736 | tf_op jit(solution)/shard_map/ppermute | solution.py:33
  28.6 0.9 copy-start.3
  29.5 0.8 copy-start.2
  30.6 0.7 copy-start.4
  31.7 0.7 copy-start.6
  33.2 5.6 %collective-permute-start.6 = (f32[8,16]{1,0:T(8,128)S(1)}, f32[8,16]{1,0:T(8,128)S(1)}, u32[]{:S(2)}, u32[]{:S(2)}) collective-permute-start(f32[8,16]{1,0:T(8,128)S(1)} %bitcast.235), channel_id=1, source_target_pairs={{0,1},{1,2},{2,3},{3,4},{4,5},{5,6},{6,7},{7,8},{8,9},{9,10},{10,1... | collective-permute-start | bytes 1544 | tf_op jit(solution)/shard_map/ppermute | solution.py:32
  37.6 5.5 %collective-permute-start.7 = (f32[8,16]{1,0:T(8,128)S(1)}, f32[8,16]{1,0:T(8,128)S(1)}, u32[]{:S(2)}, u32[]{:S(2)}) collective-permute-start(f32[8,16]{1,0:T(8,128)S(1)} %bitcast.245), channel_id=1, source_target_pairs={{1,0},{2,1},{3,2},{4,3},{5,4},{6,5},{7,6},{8,7},{9,8},{10,9},{11,1... | collective-permute-start | bytes 1544 | tf_op jit(solution)/shard_map/ppermute | solution.py:33
  43.3 5.6 %collective-permute-start.8 = (f32[8,258]{1,0:T(8,128)S(1)}, f32[8,258]{1,0:T(8,128)S(1)}, u32[]{:S(2)}, u32[]{:S(2)}) collective-permute-start(f32[8,258]{1,0:T(8,128)S(1)} %get-tuple-element.40), channel_id=1, source_target_pairs={{0,32},{32,64},{64,96},{96,128},{128,160},{160,192},{192,224},{1,3... | collective-permute-start | bytes 24776 | tf_op jit(solution)/shard_map/ppermute | solution.py:32
  45.3 5.0 %collective-permute-start.9 = (f32[8,258]{1,0:T(8,128)S(1)}, f32[8,258]{1,0:T(8,128)S(1)}, u32[]{:S(2)}, u32[]{:S(2)}) collective-permute-start(f32[8,258]{1,0:T(8,128)S(1)} %get-tuple-element.41), channel_id=1, source_target_pairs={{32,0},{64,32},{96,64},{128,96},{160,128},{192,160},{224,192},{33,... | collective-permute-start | bytes 24776 | tf_op jit(solution)/shard_map/ppermute | solution.py:33
  50.4 5.0 %collective-permute-start.10 = (f32[18,258]{1,0:T(8,128)S(1)}, f32[18,258]{1,0:T(8,128)S(1)}, u32[]{:S(2)}, u32[]{:S(2)}) collective-permute-start(f32[18,258]{1,0:T(8,128)S(1)} %get-tuple-element.24), channel_id=1, source_target_pairs={{0,256},{256,512},{512,768},{1,257},{257,513},{513,769},{2,258},{2... | collective-permute-start | bytes 55736 | tf_op jit(solution)/shard_map/ppermute | solution.py:32
  53.8 5.9 %collective-permute-start.11 = (f32[18,258]{1,0:T(8,128)S(1)}, f32[18,258]{1,0:T(8,128)S(1)}, u32[]{:S(2)}, u32[]{:S(2)}) collective-permute-start(f32[18,258]{1,0:T(8,128)S(1)} %get-tuple-element.25), channel_id=1, source_target_pairs={{256,0},{512,256},{768,512},{257,1},{513,257},{769,513},{258,2},{5... | collective-permute-start | bytes 55736 | tf_op jit(solution)/shard_map/ppermute | solution.py:33
  62.3 6.0 %collective-permute-start.12 = (f32[8,16]{1,0:T(8,128)S(1)}, f32[8,16]{1,0:T(8,128)S(1)}, u32[]{:S(2)}, u32[]{:S(2)}) collective-permute-start(f32[8,16]{1,0:T(8,128)S(1)} %bitcast.237), channel_id=1, source_target_pairs={{0,1},{1,2},{2,3},{3,4},{4,5},{5,6},{6,7},{7,8},{8,9},{9,10},{10,1... | collective-permute-start | bytes 1544 | tf_op jit(solution)/shard_map/ppermute | solution.py:32
  67.0 7.0 %collective-permute-start.13 = (f32[8,16]{1,0:T(8,128)S(1)}, f32[8,16]{1,0:T(8,128)S(1)}, u32[]{:S(2)}, u32[]{:S(2)}) collective-permute-start(f32[8,16]{1,0:T(8,128)S(1)} %bitcast.247), channel_id=1, source_target_pairs={{1,0},{2,1},{3,2},{4,3},{5,4},{6,5},{7,6},{8,7},{9,8},{10,9},{11,1... | collective-permute-start | bytes 1544 | tf_op jit(solution)/shard_map/ppermute | solution.py:33
  74.2 5.6 %collective-permute-start.14 = (f32[8,258]{1,0:T(8,128)S(1)}, f32[8,258]{1,0:T(8,128)S(1)}, u32[]{:S(2)}, u32[]{:S(2)}) collective-permute-start(f32[8,258]{1,0:T(8,128)S(1)} %get-tuple-element.38), channel_id=1, source_target_pairs={{0,32},{32,64},{64,96},{96,128},{128,160},{160,192},{192,224},{1,3... | collective-permute-start | bytes 24776 | tf_op jit(solution)/shard_map/ppermute | solution.py:32
  76.2 5.0 %collective-permute-start.15 = (f32[8,258]{1,0:T(8,128)S(1)}, f32[8,258]{1,0:T(8,128)S(1)}, u32[]{:S(2)}, u32[]{:S(2)}) collective-permute-start(f32[8,258]{1,0:T(8,128)S(1)} %get-tuple-element.39), channel_id=1, source_target_pairs={{32,0},{64,32},{96,64},{128,96},{160,128},{192,160},{224,192},{33,... | collective-permute-start | bytes 24776 | tf_op jit(solution)/shard_map/ppermute | solution.py:33
  81.3 4.7 %collective-permute-start.16 = (f32[18,258]{1,0:T(8,128)S(1)}, f32[18,258]{1,0:T(8,128)S(1)}, u32[]{:S(2)}, u32[]{:S(2)}) collective-permute-start(f32[18,258]{1,0:T(8,128)S(1)} %get-tuple-element.22), channel_id=1, source_target_pairs={{0,256},{256,512},{512,768},{1,257},{257,513},{513,769},{2,258},{2... | collective-permute-start | bytes 55736 | tf_op jit(solution)/shard_map/ppermute | solution.py:32
  84.4 5.9 %collective-permute-start.17 = (f32[18,258]{1,0:T(8,128)S(1)}, f32[18,258]{1,0:T(8,128)S(1)}, u32[]{:S(2)}, u32[]{:S(2)}) collective-permute-start(f32[18,258]{1,0:T(8,128)S(1)} %get-tuple-element.23), channel_id=1, source_target_pairs={{256,0},{512,256},{768,512},{257,1},{513,257},{769,513},{258,2},{5... | collective-permute-start | bytes 55736 | tf_op jit(solution)/shard_map/ppermute | solution.py:33
  93.0 6.6 %collective-permute-start.18 = (f32[8,16]{1,0:T(8,128)S(1)}, f32[8,16]{1,0:T(8,128)S(1)}, u32[]{:S(2)}, u32[]{:S(2)}) collective-permute-start(f32[8,16]{1,0:T(8,128)S(1)} %bitcast.239), channel_id=1, source_target_pairs={{0,1},{1,2},{2,3},{3,4},{4,5},{5,6},{6,7},{7,8},{8,9},{9,10},{10,1... | collective-permute-start | bytes 1544 | tf_op jit(solution)/shard_map/ppermute | solution.py:32
  98.2 5.5 %collective-permute-start.19 = (f32[8,16]{1,0:T(8,128)S(1)}, f32[8,16]{1,0:T(8,128)S(1)}, u32[]{:S(2)}, u32[]{:S(2)}) collective-permute-start(f32[8,16]{1,0:T(8,128)S(1)} %bitcast.249), channel_id=1, source_target_pairs={{1,0},{2,1},{3,2},{4,3},{5,4},{6,5},{7,6},{8,7},{9,8},{10,9},{11,1... | collective-permute-start | bytes 1544 | tf_op jit(solution)/shard_map/ppermute | solution.py:33
  104.0 5.6 %collective-permute-start.20 = (f32[8,258]{1,0:T(8,128)S(1)}, f32[8,258]{1,0:T(8,128)S(1)}, u32[]{:S(2)}, u32[]{:S(2)}) collective-permute-start(f32[8,258]{1,0:T(8,128)S(1)} %get-tuple-element.36), channel_id=1, source_target_pairs={{0,32},{32,64},{64,96},{96,128},{128,160},{160,192},{192,224},{1,3... | collective-permute-start | bytes 24776 | tf_op jit(solution)/shard_map/ppermute | solution.py:32
  106.0 5.0 %collective-permute-start.21 = (f32[8,258]{1,0:T(8,128)S(1)}, f32[8,258]{1,0:T(8,128)S(1)}, u32[]{:S(2)}, u32[]{:S(2)}) collective-permute-start(f32[8,258]{1,0:T(8,128)S(1)} %get-tuple-element.37), channel_id=1, source_target_pairs={{32,0},{64,32},{96,64},{128,96},{160,128},{192,160},{224,192},{33,... | collective-permute-start | bytes 24776 | tf_op jit(solution)/shard_map/ppermute | solution.py:33
  111.1 5.9 %collective-permute-start.23 = (f32[18,258]{1,0:T(8,128)S(1)}, f32[18,258]{1,0:T(8,128)S(1)}, u32[]{:S(2)}, u32[]{:S(2)}) collective-permute-start(f32[18,258]{1,0:T(8,128)S(1)} %get-tuple-element.18), channel_id=1, source_target_pairs={{256,0},{512,256},{768,512},{257,1},{513,257},{769,513},{258,2},{5... | collective-permute-start | bytes 55736 | tf_op jit(solution)/shard_map/ppermute | solution.py:33
  112.4 6.2 %collective-permute-start.22 = (f32[18,258]{1,0:T(8,128)S(1)}, f32[18,258]{1,0:T(8,128)S(1)}, u32[]{:S(2)}, u32[]{:S(2)}) collective-permute-start(f32[18,258]{1,0:T(8,128)S(1)} %get-tuple-element.19), channel_id=1, source_target_pairs={{0,256},{256,512},{512,768},{1,257},{257,513},{513,769},{2,258},{2... | collective-permute-start | bytes 55736 | tf_op jit(solution)/shard_map/ppermute | solution.py:32
  121.2 5.5 %collective-permute-start.24 = (f32[8,16]{1,0:T(8,128)S(1)}, f32[8,16]{1,0:T(8,128)S(1)}, u32[]{:S(2)}, u32[]{:S(2)}) collective-permute-start(f32[8,16]{1,0:T(8,128)S(1)} %bitcast.241), channel_id=1, source_target_pairs={{0,1},{1,2},{2,3},{3,4},{4,5},{5,6},{6,7},{7,8},{8,9},{9,10},{10,1... | collective-permute-start | bytes 1544 | tf_op jit(solution)/shard_map/ppermute | solution.py:32
  125.2 5.5 %collective-permute-start.25 = (f32[8,16]{1,0:T(8,128)S(1)}, f32[8,16]{1,0:T(8,128)S(1)}, u32[]{:S(2)}, u32[]{:S(2)}) collective-permute-start(f32[8,16]{1,0:T(8,128)S(1)} %bitcast.251), channel_id=1, source_target_pairs={{1,0},{2,1},{3,2},{4,3},{5,4},{6,5},{7,6},{8,7},{9,8},{10,9},{11,1... | collective-permute-start | bytes 1544 | tf_op jit(solution)/shard_map/ppermute | solution.py:33
  131.0 5.6 %collective-permute-start.26 = (f32[8,258]{1,0:T(8,128)S(1)}, f32[8,258]{1,0:T(8,128)S(1)}, u32[]{:S(2)}, u32[]{:S(2)}) collective-permute-start(f32[8,258]{1,0:T(8,128)S(1)} %get-tuple-element.34), channel_id=1, source_target_pairs={{0,32},{32,64},{64,96},{96,128},{128,160},{160,192},{192,224},{1,3... | collective-permute-start | bytes 24776 | tf_op jit(solution)/shard_map/ppermute | solution.py:32
  132.9 5.0 %collective-permute-start.27 = (f32[8,258]{1,0:T(8,128)S(1)}, f32[8,258]{1,0:T(8,128)S(1)}, u32[]{:S(2)}, u32[]{:S(2)}) collective-permute-start(f32[8,258]{1,0:T(8,128)S(1)} %get-tuple-element.35), channel_id=1, source_target_pairs={{32,0},{64,32},{96,64},{128,96},{160,128},{192,160},{224,192},{33,... | collective-permute-start | bytes 24776 | tf_op jit(solution)/shard_map/ppermute | solution.py:33
  138.1 5.9 %collective-permute-start.28 = (f32[18,258]{1,0:T(8,128)S(1)}, f32[18,258]{1,0:T(8,128)S(1)}, u32[]{:S(2)}, u32[]{:S(2)}) collective-permute-start(f32[18,258]{1,0:T(8,128)S(1)} %get-tuple-element.16), channel_id=1, source_target_pairs={{0,256},{256,512},{512,768},{1,257},{257,513},{513,769},{2,258},{2... | collective-permute-start | bytes 55736 | tf_op jit(solution)/shard_map/ppermute | solution.py:32
  142.3 5.9 %collective-permute-start.29 = (f32[18,258]{1,0:T(8,128)S(1)}, f32[18,258]{1,0:T(8,128)S(1)}, u32[]{:S(2)}, u32[]{:S(2)}) collective-permute-start(f32[18,258]{1,0:T(8,128)S(1)} %get-tuple-element.17), channel_id=1, source_target_pairs={{256,0},{512,256},{768,512},{257,1},{513,257},{769,513},{258,2},{5... | collective-permute-start | bytes 55736 | tf_op jit(solution)/shard_map/ppermute | solution.py:33
  148.4 0.9 copy-start.5
  150.0 3.1 %collective-permute-start.30 = (f32[8192]{0:T(1024)S(1)}, f32[8192]{0:T(1024)S(1)}, u32[]{:S(2)}, u32[]{:S(2)}) collective-permute-start(f32[8192]{0:T(1024)S(1)} %bitcast.216), channel_id=1, source_target_pairs={{0,32},{32,0},{64,96},{96,64},{128,160},{160,128},{192,224},{224,1... | collective-permute-start | bytes 98312 | tf_op jit(solution)/shard_map/ppermute | solution.py:52
  153.1 7.0 %collective-permute-start.31 = (f32[8192]{0:T(1024)S(1)}, f32[8192]{0:T(1024)S(1)}, u32[]{:S(2)}, u32[]{:S(2)}) collective-permute-start(f32[8192]{0:T(1024)S(1)} %add.337), channel_id=1, source_target_pairs={{0,192},{32,224},{64,128},{96,160},{128,64},{160,96},{192,0},{224,... | collective-permute-start | bytes 98312 | tf_op jit(solution)/shard_map/ppermute | solution.py:56
  160.1 5.8 %collective-permute-start.32 = (f32[8192]{0:T(1024)S(1)}, f32[8192]{0:T(1024)S(1)}, u32[]{:S(2)}, u32[]{:S(2)}) collective-permute-start(f32[8192]{0:T(1024)S(1)} %add.338), channel_id=1, source_target_pairs={{0,64},{32,96},{64,0},{96,32},{128,192},{160,224},{192,128},{224,1... | collective-permute-start | bytes 98312 | tf_op jit(solution)/shard_map/ppermute | solution.py:56
  165.9 6.6 %collective-permute-start.33 = (f32[8192]{0:T(1024)S(1)}, f32[8192]{0:T(1024)S(1)}, u32[]{:S(2)}, u32[]{:S(2)}) collective-permute-start(f32[8192]{0:T(1024)S(1)} %add.339), channel_id=1, source_target_pairs={{0,1},{1,0},{2,3},{3,2},{4,5},{5,4},{6,7},{7,6},{8,9},{9,8},{10,11... | collective-permute-start | bytes 98312 | tf_op jit(solution)/shard_map/ppermute | solution.py:52
  172.6 8.5 %collective-permute-start.34 = (f32[8192]{0:T(1024)S(1)}, f32[8192]{0:T(1024)S(1)}, u32[]{:S(2)}, u32[]{:S(2)}) collective-permute-start(f32[8192]{0:T(1024)S(1)} %add.340), channel_id=1, source_target_pairs={{0,2},{1,3},{2,0},{3,1},{4,6},{5,7},{6,4},{7,5},{8,10},{9,11},{10,... | collective-permute-start | bytes 98312 | tf_op jit(solution)/shard_map/ppermute | solution.py:52
  181.0 11.0 %collective-permute-start.35 = (f32[8192]{0:T(1024)S(1)}, f32[8192]{0:T(1024)S(1)}, u32[]{:S(2)}, u32[]{:S(2)}) collective-permute-start(f32[8192]{0:T(1024)S(1)} %add.341), channel_id=1, source_target_pairs={{0,4},{1,5},{2,6},{3,7},{4,0},{5,1},{6,2},{7,3},{8,12},{9,13},{10,... | collective-permute-start | bytes 98312 | tf_op jit(solution)/shard_map/ppermute | solution.py:52
  192.0 18.6 %collective-permute-start.36 = (f32[8192]{0:T(1024)S(1)}, f32[8192]{0:T(1024)S(1)}, u32[]{:S(2)}, u32[]{:S(2)}) collective-permute-start(f32[8192]{0:T(1024)S(1)} %add.342), channel_id=1, source_target_pairs={{0,24},{1,25},{2,26},{3,27},{4,28},{5,29},{6,30},{7,31},{8,16},{9,... | collective-permute-start | bytes 98312 | tf_op jit(solution)/shard_map/ppermute | solution.py:56
  210.6 14.5 %collective-permute-start.37 = (f32[8192]{0:T(1024)S(1)}, f32[8192]{0:T(1024)S(1)}, u32[]{:S(2)}, u32[]{:S(2)}) collective-permute-start(f32[8192]{0:T(1024)S(1)} %add.343), channel_id=1, source_target_pairs={{0,8},{1,9},{2,10},{3,11},{4,12},{5,13},{6,14},{7,15},{8,0},{9,1},... | collective-permute-start | bytes 98312 | tf_op jit(solution)/shard_map/ppermute | solution.py:56
  225.1 7.0 %collective-permute-start.38 = (f32[8192]{0:T(1024)S(1)}, f32[8192]{0:T(1024)S(1)}, u32[]{:S(2)}, u32[]{:S(2)}) collective-permute-start(f32[8192]{0:T(1024)S(1)} %add.344), channel_id=1, source_target_pairs={{0,768},{256,512},{512,256},{768,0},{1,769},{257,513},{513,257},{7... | collective-permute-start | bytes 98312 | tf_op jit(solution)/shard_map/ppermute | solution.py:56
  232.1 5.8 %collective-permute-start.39 = (f32[8192]{0:T(1024)S(1)}, f32[8192]{0:T(1024)S(1)}, u32[]{:S(2)}, u32[]{:S(2)}) collective-permute-start(f32[8192]{0:T(1024)S(1)} %add.345), channel_id=1, source_target_pairs={{0,256},{256,0},{512,768},{768,512},{1,257},{257,1},{513,769},{769... | collective-permute-start | bytes 98312 | tf_op jit(solution)/shard_map/ppermute | solution.py:56
  238.6 0.5 copy-start.13

commit v5 on v4

--- a/solution.py
+++ b/solution.py
@@ -117,9 +117,19 @@
     return own + low_mask * left + high_mask * right
 
 
+def ghost_z(cells, width):
+    count = lax.axis_size("gz")
+    head = cells[..., :width]
+    tail = cells[..., cells.shape[-1] - width :]
+    from_prev = lax.ppermute(tail, "gz", [(i, i + 1) for i in range(count - 1)])
+    from_next = lax.ppermute(head, "gz", [(i + 1, i) for i in range(count - 1)])
+    return jnp.concatenate([from_prev, cells, from_next], axis=-1)
+
+
 def assemble(field, points):
     size_x, size_y, size_z = field.shape
-    padded = padded_2(field, (("gz", 2), ("gy", 1), ("gx", 0)), 1)
+    padded = jnp.pad(field, ((0, 0), (0, 0), (1, 1)))
+    padded = padded_2(padded, (("gy", 1), ("gx", 0)), 1)
     summed = combine(padded, 0, size_x, points)
     summed = combine(summed, 1, size_y, points)
     summed = combine(summed, 2, size_z, points)
@@ -129,7 +139,14 @@
 def per_device(right_side, coefficient, agg_weight, coarse_factor):
     points = ORDER + 1
     derivative, weights = gll_tables(ORDER)
-    size_x, size_y, size_z = right_side.shape
+    size_x, size_y, own_z = right_side.shape
+    ghost = 64
+    inputs = ghost_z(jnp.stack([right_side, coefficient]), ghost)
+    right_ext, coefficient = inputs[0], inputs[1]
+    size_z = own_z + 2 * ghost
+    first = lax.axis_index("gz") * own_z - ghost
+    global_z = first + jnp.arange(size_z, dtype=jnp.int32)
+    inside = ((global_z >= 0) & (global_z < own_z * lax.axis_size("gz")))[None, None, :]
     mat_x = jnp.asarray(np.kron(np.eye(size_x // points), derivative), dtype=jnp.float32)
     mat_y = jnp.asarray(np.kron(np.eye(size_y // points), derivative), dtype=jnp.float32)
     mat_z = jnp.asarray(np.kron(np.eye(128 // points), derivative), dtype=jnp.float32)
@@ -142,11 +159,11 @@
         coefficient * weight_x[:, None, None] * weight_y[None, :, None] * weight_z[None, None, :]
     )
     diagonal = assemble(backward_sum((scaled, scaled, scaled), squares), points)
-    inverse = 1.0 / diagonal
+    inverse = jnp.where(inside, 1.0 / diagonal, 0.0)
     theta = (eig_high + eig_low) / 2.0
     delta = (eig_high - eig_low) / 2.0
     sigma = theta / delta
-    residual = right_side
+    residual = right_ext
     direction = inverse * residual / theta
     smoothed = direction
     rho = 1.0 / sigma
@@ -159,6 +176,9 @@
             direction = rho_new * rho * direction + 2.0 * rho_new / delta * inverse * residual
             smoothed = smoothed + direction
             rho = rho_new
+    residual = residual[:, :, ghost : ghost + own_z]
+    smoothed = smoothed[:, :, ghost : ghost + own_z]
+    size_z = own_z
     aggregates = coarse_factor.shape[0]
     column_sums = jnp.sum(agg_weight * residual, axis=(0, 1))
     coarse_rhs = jnp.sum(column_sums.reshape(aggregates, size_z // aggregates), axis=1)

time: 241 us -> 208 us (0.86)
  waiting for transfers between devices: 76 us -> 57.3 us
  starting transfers between devices: 139 us -> 123 us
    ppermute x15 -> x10, waiting for transfers between devices: 41 us -> 17.8 us  [padded_2(): lax.ppermute(jnp.squeeze(head, dim), axis, [(i + 1, i) for i in range(end...]
    ppermute x15 -> x10, starting transfers between devices: 50.6 us -> 30.7 us  [padded_2(): lax.ppermute(jnp.squeeze(tail, dim), axis, [(i, i + 1) for i in range(end...]
    ppermute x6, starting transfers between devices: 34.6 us -> 48.3 us  [butterfly_sum(): value = value + lax.ppermute(value, axis, pairs)]
    ppermute x15 -> x10, starting transfers between devices: 31.3 us -> 22.9 us  [padded_2(): lax.ppermute(jnp.squeeze(head, dim), axis, [(i + 1, i) for i in range(end...]
    ppermute x4, starting transfers between devices: 22.3 us -> 15.5 us  [butterfly_sum(): lax.ppermute(value, axis, [(i, i ^ stride) for i in range(count)])]
    ppermute x0 -> x2, starting transfers between devices: none -> 5.85 us  [the longest x1 4.55 us: ghost_z(): from_prev = lax.ppermute(tail, 'gz', [(i, i + 1) for i in range(count - 1)])]
    ppermute x6, waiting for transfers between devices: 24.1 us -> 20.1 us  [butterfly_sum(): value = value + lax.ppermute(value, axis, pairs)]
    ppermute x4, waiting for transfers between devices: 6.81 us -> 10.2 us  [butterfly_sum(): lax.ppermute(value, axis, [(i, i ^ stride) for i in range(count)])]
  transfers between devices with their start and end apart: 40 -> 32, of which waited for: 29 -> 26; matrix products, arithmetic and copies ran while one was open for 1% -> 1% of each run, Pallas kernels for 0% -> 0%
where the time goes in v5:
time: 208 us; the launch traced here: 207 us
  starting transfers between devices  123 us (59%)
  waiting for transfers between devices  57.3 us (28%)
  matrix products  10.1 us (5%)
  local copies, waits for them, and re-layouts  9.31 us (4%)
  other arithmetic  5.31 us (3%)
    ppermute x6, starting transfers between devices, butterfly_sum(): value = value + lax.ppermute(value, axis, pairs)  48.3 us
    ppermute x10, starting transfers between devices, padded_2(): lax.ppermute(jnp.squeeze(tail, dim), axis, [(i, i + 1) for i in range(end...  30.7 us
    ppermute x10, starting transfers between devices, padded_2(): lax.ppermute(jnp.squeeze(head, dim), axis, [(i + 1, i) for i in range(end...  22.9 us
    ppermute x6, waiting for transfers between devices, butterfly_sum(): value = value + lax.ppermute(value, axis, pairs)  20.1 us
    ppermute x10, waiting for transfers between devices, padded_2(): lax.ppermute(jnp.squeeze(head, dim), axis, [(i + 1, i) for i in range(end...  17.8 us
    ppermute x4, starting transfers between devices, butterfly_sum(): lax.ppermute(value, axis, [(i, i ^ stride) for i in range(count)])  15.5 us
    ppermute x4, waiting for transfers between devices, butterfly_sum(): lax.ppermute(value, axis, [(i, i ^ stride) for i in range(count)])  10.2 us
    ppermute x10, waiting for transfers between devices, padded_2(): lax.ppermute(jnp.squeeze(tail, dim), axis, [(i, i + 1) for i in range(end...  6.56 us
  transfers between devices with their start and end apart: 32, of which 26 were waited for; matrix products, arithmetic and copies ran while one was open for 1% of the time, Pallas kernels for 0%

profile of v5, /device:TPU:24, one launch (start us, length us, event | category | flops | bytes accessed | tf_op | source)
XLA Modules:
  0.0 206.9 jit_solution(1981950669516903053)
XLA Ops:
  0.6 1.2 copy_bitcast_fusion
  1.9 1.3 collective-permute-start.1
  3.2 4.6 %collective-permute-start = (f32[2,8,16,64]{3,1,2,0:T(8,128)S(1)}, f32[2,8,16,64]{3,1,2,0:T(8,128)S(1)}, u32[]{:S(2)}, u32[]{:S(2)}) collective-permute-start(f32[2,8,16,64]{3,1,2,0:T(8,128)S(1)} %get-tuple-element.37), channel_id=1, source_target_pairs={{0,1},{1,2},{2,3},{3,4},{4,5},{5,6},{6,7},{7,8},{8,9},{9,10},{10,1... | collective-permute-start | bytes 196616 | tf_op jit(solution)/shard_map/ppermute | solution.py:124
  7.8 1.4 collective-permute-done.1
  9.2 1.2 collective-permute-done
  10.7 0.6 copy-done.5
  11.4 0.6 copy-done.9
  12.1 0.7 copy-done.8
  14.7 1.9 collective-permute-start.3
  16.6 2.4 %collective-permute-start.2 = (f32[8,386]{1,0:T(8,128)S(1)}, f32[8,386]{1,0:T(8,128)S(1)}, u32[]{:S(2)}, u32[]{:S(2)}) collective-permute-start(f32[8,386]{1,0:T(8,128)S(1)} %get-tuple-element.47), channel_id=1, source_target_pairs={{0,32},{32,64},{64,96},{96,128},{128,160},{160,192},{192,224},{1,3... | collective-permute-start | bytes 37064 | tf_op jit(solution)/shard_map/ppermute | solution.py:32
  19.2 2.4 %collective-permute-done.2 = f32[8,386]{1,0:T(8,128)S(1)} collective-permute-done((f32[8,386]{1,0:T(8,128)S(1)}, f32[8,386]{1,0:T(8,128)S(1)}, u32[]{:S(2)}, u32[]{:S(2)}) %collective-permute-start.2) | collective-permute-done | bytes 12384 | tf_op jit(solution)/shard_map/ppermute | solution.py:32
  21.8 3.4 %collective-permute-start.4 = (f32[18,386]{1,0:T(8,128)S(1)}, f32[18,386]{1,0:T(8,128)S(1)}, u32[]{:S(2)}, u32[]{:S(2)}) collective-permute-start(f32[18,386]{1,0:T(8,128)S(1)} %get-tuple-element.26), channel_id=1, source_target_pairs={{0,256},{256,512},{512,768},{1,257},{257,513},{513,769},{2,258},{2... | collective-permute-start | bytes 83384 | tf_op jit(solution)/shard_map/ppermute | solution.py:32
  25.4 1.3 collective-permute-start.5
  27.1 4.3 %collective-permute-done.5 = f32[18,386]{1,0:T(8,128)S(1)} collective-permute-done((f32[18,386]{1,0:T(8,128)S(1)}, f32[18,386]{1,0:T(8,128)S(1)}, u32[]{:S(2)}, u32[]{:S(2)}) %collective-permute-start.5) | collective-permute-done | bytes 27824 | tf_op jit(solution)/shard_map/ppermute | solution.py:33
  32.0 0.6 copy-done.1
  35.6 1.9 collective-permute-start.6
  37.6 3.6 %collective-permute-start.7 = (f32[8,386]{1,0:T(8,128)S(1)}, f32[8,386]{1,0:T(8,128)S(1)}, u32[]{:S(2)}, u32[]{:S(2)}) collective-permute-start(f32[8,386]{1,0:T(8,128)S(1)} %get-tuple-element.46), channel_id=1, source_target_pairs={{32,0},{64,32},{96,64},{128,96},{160,128},{192,160},{224,192},{33,... | collective-permute-start | bytes 37064 | tf_op jit(solution)/shard_map/ppermute | solution.py:33
  41.4 1.2 collective-permute-done.7
  42.7 3.4 %collective-permute-start.8 = (f32[18,386]{1,0:T(8,128)S(1)}, f32[18,386]{1,0:T(8,128)S(1)}, u32[]{:S(2)}, u32[]{:S(2)}) collective-permute-start(f32[18,386]{1,0:T(8,128)S(1)} %get-tuple-element.24), channel_id=1, source_target_pairs={{0,256},{256,512},{512,768},{1,257},{257,513},{513,769},{2,258},{2... | collective-permute-start | bytes 83384 | tf_op jit(solution)/shard_map/ppermute | solution.py:32
  46.1 1.3 collective-permute-start.9
  47.4 0.4 collective-permute-done.8
  47.9 4.3 %collective-permute-done.9 = f32[18,386]{1,0:T(8,128)S(1)} collective-permute-done((f32[18,386]{1,0:T(8,128)S(1)}, f32[18,386]{1,0:T(8,128)S(1)}, u32[]{:S(2)}, u32[]{:S(2)}) %collective-permute-start.9) | collective-permute-done | bytes 27824 | tf_op jit(solution)/shard_map/ppermute | solution.py:33
  55.2 1.9 collective-permute-start.10
  57.1 3.6 %collective-permute-start.11 = (f32[8,386]{1,0:T(8,128)S(1)}, f32[8,386]{1,0:T(8,128)S(1)}, u32[]{:S(2)}, u32[]{:S(2)}) collective-permute-start(f32[8,386]{1,0:T(8,128)S(1)} %get-tuple-element.44), channel_id=1, source_target_pairs={{32,0},{64,32},{96,64},{128,96},{160,128},{192,160},{224,192},{33,... | collective-permute-start | bytes 37064 | tf_op jit(solution)/shard_map/ppermute | solution.py:33
  61.0 1.2 collective-permute-done.11
  62.3 1.3 collective-permute-start.13
  63.6 4.5 %collective-permute-start.12 = (f32[18,386]{1,0:T(8,128)S(1)}, f32[18,386]{1,0:T(8,128)S(1)}, u32[]{:S(2)}, u32[]{:S(2)}) collective-permute-start(f32[18,386]{1,0:T(8,128)S(1)} %get-tuple-element.22), channel_id=1, source_target_pairs={{0,256},{256,512},{512,768},{1,257},{257,513},{513,769},{2,258},{2... | collective-permute-start | bytes 83384 | tf_op jit(solution)/shard_map/ppermute | solution.py:32
  68.2 1.6 collective-permute-done.12
  72.8 1.9 collective-permute-start.14
  74.7 3.6 %collective-permute-start.15 = (f32[8,386]{1,0:T(8,128)S(1)}, f32[8,386]{1,0:T(8,128)S(1)}, u32[]{:S(2)}, u32[]{:S(2)}) collective-permute-start(f32[8,386]{1,0:T(8,128)S(1)} %get-tuple-element.42), channel_id=1, source_target_pairs={{32,0},{64,32},{96,64},{128,96},{160,128},{192,160},{224,192},{33,... | collective-permute-start | bytes 37064 | tf_op jit(solution)/shard_map/ppermute | solution.py:33
  78.6 1.2 collective-permute-done.15
  79.9 1.3 collective-permute-start.17
  81.2 5.1 %collective-permute-start.16 = (f32[18,386]{1,0:T(8,128)S(1)}, f32[18,386]{1,0:T(8,128)S(1)}, u32[]{:S(2)}, u32[]{:S(2)}) collective-permute-start(f32[18,386]{1,0:T(8,128)S(1)} %get-tuple-element.19), channel_id=1, source_target_pairs={{0,256},{256,512},{512,768},{1,257},{257,513},{513,769},{2,258},{2... | collective-permute-start | bytes 83384 | tf_op jit(solution)/shard_map/ppermute | solution.py:32
  86.3 1.5 collective-permute-done.16
  90.8 1.9 collective-permute-start.18
  92.7 3.6 %collective-permute-start.19 = (f32[8,386]{1,0:T(8,128)S(1)}, f32[8,386]{1,0:T(8,128)S(1)}, u32[]{:S(2)}, u32[]{:S(2)}) collective-permute-start(f32[8,386]{1,0:T(8,128)S(1)} %get-tuple-element.40), channel_id=1, source_target_pairs={{32,0},{64,32},{96,64},{128,96},{160,128},{192,160},{224,192},{33,... | collective-permute-start | bytes 37064 | tf_op jit(solution)/shard_map/ppermute | solution.py:33
  96.6 1.2 collective-permute-done.19
  97.9 4.2 %collective-permute-start.20 = (f32[18,386]{1,0:T(8,128)S(1)}, f32[18,386]{1,0:T(8,128)S(1)}, u32[]{:S(2)}, u32[]{:S(2)}) collective-permute-start(f32[18,386]{1,0:T(8,128)S(1)} %get-tuple-element.16), channel_id=1, source_target_pairs={{0,256},{256,512},{512,768},{1,257},{257,513},{513,769},{2,258},{2... | collective-permute-start | bytes 83384 | tf_op jit(solution)/shard_map/ppermute | solution.py:32
  102.2 1.3 collective-permute-start.21
  103.9 4.3 %collective-permute-done.21 = f32[18,386]{1,0:T(8,128)S(1)} collective-permute-done((f32[18,386]{1,0:T(8,128)S(1)}, f32[18,386]{1,0:T(8,128)S(1)}, u32[]{:S(2)}, u32[]{:S(2)}) %collective-permute-start.21) | collective-permute-done | bytes 27824 | tf_op jit(solution)/shard_map/ppermute | solution.py:33
  108.9 0.7 copy-done.3
  110.5 1.9 collective-permute-start.22
  112.4 1.2 collective-permute-done.22
  113.6 9.7 %collective-permute-start.23 = (f32[8192]{0:T(1024)S(1)}, f32[8192]{0:T(1024)S(1)}, u32[]{:S(2)}, u32[]{:S(2)}) collective-permute-start(f32[8192]{0:T(1024)S(1)} %add.360), channel_id=1, source_target_pairs={{0,192},{32,224},{64,128},{96,160},{128,64},{160,96},{192,0},{224,... | collective-permute-start | bytes 98312 | tf_op jit(solution)/shard_map/ppermute | solution.py:56
  123.3 1.9 collective-permute-done.23
  125.2 2.7 %collective-permute-start.24 = (f32[8192]{0:T(1024)S(1)}, f32[8192]{0:T(1024)S(1)}, u32[]{:S(2)}, u32[]{:S(2)}) collective-permute-start(f32[8192]{0:T(1024)S(1)} %add.361), channel_id=1, source_target_pairs={{0,64},{32,96},{64,0},{96,32},{128,192},{160,224},{192,128},{224,1... | collective-permute-start | bytes 98312 | tf_op jit(solution)/shard_map/ppermute | solution.py:56
  127.9 3.1 %collective-permute-done.24 = f32[8192]{0:T(1024)S(1)} collective-permute-done((f32[8192]{0:T(1024)S(1)}, f32[8192]{0:T(1024)S(1)}, u32[]{:S(2)}, u32[]{:S(2)}) %collective-permute-start.24) | collective-permute-done | bytes 32800 | tf_op jit(solution)/shard_map/ppermute | solution.py:56
  131.0 4.3 %collective-permute-start.25 = (f32[8192]{0:T(1024)S(1)}, f32[8192]{0:T(1024)S(1)}, u32[]{:S(2)}, u32[]{:S(2)}) collective-permute-start(f32[8192]{0:T(1024)S(1)} %add.362), channel_id=1, source_target_pairs={{0,1},{1,0},{2,3},{3,2},{4,5},{5,4},{6,7},{7,6},{8,9},{9,8},{10,11... | collective-permute-start | bytes 98312 | tf_op jit(solution)/shard_map/ppermute | solution.py:52
  135.3 1.9 collective-permute-done.25
  137.2 3.4 %collective-permute-start.26 = (f32[8192]{0:T(1024)S(1)}, f32[8192]{0:T(1024)S(1)}, u32[]{:S(2)}, u32[]{:S(2)}) collective-permute-start(f32[8192]{0:T(1024)S(1)} %add.363), channel_id=1, source_target_pairs={{0,2},{1,3},{2,0},{3,1},{4,6},{5,7},{6,4},{7,5},{8,10},{9,11},{10,... | collective-permute-start | bytes 98312 | tf_op jit(solution)/shard_map/ppermute | solution.py:52
  140.6 3.3 %collective-permute-done.26 = f32[8192]{0:T(1024)S(1)} collective-permute-done((f32[8192]{0:T(1024)S(1)}, f32[8192]{0:T(1024)S(1)}, u32[]{:S(2)}, u32[]{:S(2)}) %collective-permute-start.26) | collective-permute-done | bytes 32800 | tf_op jit(solution)/shard_map/ppermute | solution.py:52
  143.9 5.9 %collective-permute-start.27 = (f32[8192]{0:T(1024)S(1)}, f32[8192]{0:T(1024)S(1)}, u32[]{:S(2)}, u32[]{:S(2)}) collective-permute-start(f32[8192]{0:T(1024)S(1)} %add.364), channel_id=1, source_target_pairs={{0,4},{1,5},{2,6},{3,7},{4,0},{5,1},{6,2},{7,3},{8,12},{9,13},{10,... | collective-permute-start | bytes 98312 | tf_op jit(solution)/shard_map/ppermute | solution.py:52
  149.8 3.8 %collective-permute-done.27 = f32[8192]{0:T(1024)S(1)} collective-permute-done((f32[8192]{0:T(1024)S(1)}, f32[8192]{0:T(1024)S(1)}, u32[]{:S(2)}, u32[]{:S(2)}) %collective-permute-start.27) | collective-permute-done | bytes 32800 | tf_op jit(solution)/shard_map/ppermute | solution.py:52
  153.6 21.9 %collective-permute-start.28 = (f32[8192]{0:T(1024)S(1)}, f32[8192]{0:T(1024)S(1)}, u32[]{:S(2)}, u32[]{:S(2)}) collective-permute-start(f32[8192]{0:T(1024)S(1)} %add.365), channel_id=1, source_target_pairs={{0,24},{1,25},{2,26},{3,27},{4,28},{5,29},{6,30},{7,31},{8,16},{9,... | collective-permute-start | bytes 98312 | tf_op jit(solution)/shard_map/ppermute | solution.py:56
  175.5 1.9 collective-permute-done.28
  177.4 8.0 %collective-permute-start.29 = (f32[8192]{0:T(1024)S(1)}, f32[8192]{0:T(1024)S(1)}, u32[]{:S(2)}, u32[]{:S(2)}) collective-permute-start(f32[8192]{0:T(1024)S(1)} %add.366), channel_id=1, source_target_pairs={{0,8},{1,9},{2,10},{3,11},{4,12},{5,13},{6,14},{7,15},{8,0},{9,1},... | collective-permute-start | bytes 98312 | tf_op jit(solution)/shard_map/ppermute | solution.py:56
  185.4 6.5 %collective-permute-done.29 = f32[8192]{0:T(1024)S(1)} collective-permute-done((f32[8192]{0:T(1024)S(1)}, f32[8192]{0:T(1024)S(1)}, u32[]{:S(2)}, u32[]{:S(2)}) %collective-permute-start.29) | collective-permute-done | bytes 32800 | tf_op jit(solution)/shard_map/ppermute | solution.py:56
  191.9 3.4 %collective-permute-start.30 = (f32[8192]{0:T(1024)S(1)}, f32[8192]{0:T(1024)S(1)}, u32[]{:S(2)}, u32[]{:S(2)}) collective-permute-start(f32[8192]{0:T(1024)S(1)} %add.367), channel_id=1, source_target_pairs={{0,768},{256,512},{512,256},{768,0},{1,769},{257,513},{513,257},{7... | collective-permute-start | bytes 98312 | tf_op jit(solution)/shard_map/ppermute | solution.py:56
  195.3 3.6 %collective-permute-done.30 = f32[8192]{0:T(1024)S(1)} collective-permute-done((f32[8192]{0:T(1024)S(1)}, f32[8192]{0:T(1024)S(1)}, u32[]{:S(2)}, u32[]{:S(2)}) %collective-permute-start.30) | collective-permute-done | bytes 32800 | tf_op jit(solution)/shard_map/ppermute | solution.py:56
  198.9 2.7 %collective-permute-start.31 = (f32[8192]{0:T(1024)S(1)}, f32[8192]{0:T(1024)S(1)}, u32[]{:S(2)}, u32[]{:S(2)}) collective-permute-start(f32[8192]{0:T(1024)S(1)} %add.368), channel_id=1, source_target_pairs={{0,256},{256,0},{512,768},{768,512},{1,257},{257,1},{513,769},{769... | collective-permute-start | bytes 98312 | tf_op jit(solution)/shard_map/ppermute | solution.py:56
  201.6 3.1 %collective-permute-done.31 = f32[8192]{0:T(1024)S(1)} collective-permute-done((f32[8192]{0:T(1024)S(1)}, f32[8192]{0:T(1024)S(1)}, u32[]{:S(2)}, u32[]{:S(2)}) %collective-permute-start.31) | collective-permute-done | bytes 32800 | tf_op jit(solution)/shard_map/ppermute | solution.py:56
  204.7 0.7 convolution_bitcast_fusion.5
  205.5 0.5 copy-done.12
  206.2 0.7 copy.165
  (146 shorter events, 19.1 us)
Async XLA Ops:
  0.6 109.5 %copy-start = (f32[8,8192]{1,0:T(8,128)S(1)}, f32[8,8192]{1,0:T(8,128)}, u32[]{:S(2)}) copy-start(f32[8,8192]{1,0:T(8,128)} %param.13) | copy-start | bytes 786436
  1.9 7.3 %collective-permute-start.1 = (f32[2,8,16,64]{3,1,2,0:T(8,128)S(1)}, f32[2,8,16,64]{3,1,2,0:T(8,128)S(1)}, u32[]{:S(2)}, u32[]{:S(2)}) collective-permute-start(f32[2,8,16,64]{3,1,2,0:T(8,128)S(1)} %get-tuple-element.38), channel_id=1, source_target_pairs={{1,0},{2,1},{3,2},{4,3},{5,4},{6,5},{7,6},{8,7},{9,8},{10,9},{11,1... | collective-permute-start | bytes 196616 | tf_op jit(solution)/shard_map/ppermute | solution.py:125
  3.2 7.2 %collective-permute-start = (f32[2,8,16,64]{3,1,2,0:T(8,128)S(1)}, f32[2,8,16,64]{3,1,2,0:T(8,128)S(1)}, u32[]{:S(2)}, u32[]{:S(2)}) collective-permute-start(f32[2,8,16,64]{3,1,2,0:T(8,128)S(1)} %get-tuple-element.37), channel_id=1, source_target_pairs={{0,1},{1,2},{2,3},{3,4},{4,5},{5,6},{6,7},{7,8},{8,9},{9,10},{10,1... | collective-permute-start | bytes 196616 | tf_op jit(solution)/shard_map/ppermute | solution.py:124
  10.6 0.7 copy-start.5
  10.6 0.7 copy-start.6
  10.6 0.7 copy-start.7
  11.3 0.7 copy-start.9
  12.0 0.8 copy-start.8
  12.8 0.7 copy-start.10
  13.5 0.7 copy-start.11
  14.7 7.0 %collective-permute-start.3 = (f32[8,386]{1,0:T(8,128)S(1)}, f32[8,386]{1,0:T(8,128)S(1)}, u32[]{:S(2)}, u32[]{:S(2)}) collective-permute-start(f32[8,386]{1,0:T(8,128)S(1)} %get-tuple-element.48), channel_id=1, source_target_pairs={{32,0},{64,32},{96,64},{128,96},{160,128},{192,160},{224,192},{33,... | collective-permute-start | bytes 37064 | tf_op jit(solution)/shard_map/ppermute | solution.py:33
  16.6 5.1 %collective-permute-start.2 = (f32[8,386]{1,0:T(8,128)S(1)}, f32[8,386]{1,0:T(8,128)S(1)}, u32[]{:S(2)}, u32[]{:S(2)}) collective-permute-start(f32[8,386]{1,0:T(8,128)S(1)} %get-tuple-element.47), channel_id=1, source_target_pairs={{0,32},{32,64},{64,96},{96,128},{128,160},{160,192},{192,224},{1,3... | collective-permute-start | bytes 37064 | tf_op jit(solution)/shard_map/ppermute | solution.py:32
  21.8 5.1 %collective-permute-start.4 = (f32[18,386]{1,0:T(8,128)S(1)}, f32[18,386]{1,0:T(8,128)S(1)}, u32[]{:S(2)}, u32[]{:S(2)}) collective-permute-start(f32[18,386]{1,0:T(8,128)S(1)} %get-tuple-element.26), channel_id=1, source_target_pairs={{0,256},{256,512},{512,768},{1,257},{257,513},{513,769},{2,258},{2... | collective-permute-start | bytes 83384 | tf_op jit(solution)/shard_map/ppermute | solution.py:32
  25.4 6.0 %collective-permute-start.5 = (f32[18,386]{1,0:T(8,128)S(1)}, f32[18,386]{1,0:T(8,128)S(1)}, u32[]{:S(2)}, u32[]{:S(2)}) collective-permute-start(f32[18,386]{1,0:T(8,128)S(1)} %get-tuple-element.27), channel_id=1, source_target_pairs={{256,0},{512,256},{768,512},{257,1},{513,257},{769,513},{258,2},{5... | collective-permute-start | bytes 83384 | tf_op jit(solution)/shard_map/ppermute | solution.py:33
  31.8 0.8 copy-start.1
  33.0 0.7 copy-start.4
  33.7 0.7 copy-start.2
  35.6 5.8 %collective-permute-start.6 = (f32[8,386]{1,0:T(8,128)S(1)}, f32[8,386]{1,0:T(8,128)S(1)}, u32[]{:S(2)}, u32[]{:S(2)}) collective-permute-start(f32[8,386]{1,0:T(8,128)S(1)} %get-tuple-element.45), channel_id=1, source_target_pairs={{0,32},{32,64},{64,96},{96,128},{128,160},{160,192},{192,224},{1,3... | collective-permute-start | bytes 37064 | tf_op jit(solution)/shard_map/ppermute | solution.py:32
  37.6 5.1 %collective-permute-start.7 = (f32[8,386]{1,0:T(8,128)S(1)}, f32[8,386]{1,0:T(8,128)S(1)}, u32[]{:S(2)}, u32[]{:S(2)}) collective-permute-start(f32[8,386]{1,0:T(8,128)S(1)} %get-tuple-element.46), channel_id=1, source_target_pairs={{32,0},{64,32},{96,64},{128,96},{160,128},{192,160},{224,192},{33,... | collective-permute-start | bytes 37064 | tf_op jit(solution)/shard_map/ppermute | solution.py:33
  42.7 5.1 %collective-permute-start.8 = (f32[18,386]{1,0:T(8,128)S(1)}, f32[18,386]{1,0:T(8,128)S(1)}, u32[]{:S(2)}, u32[]{:S(2)}) collective-permute-start(f32[18,386]{1,0:T(8,128)S(1)} %get-tuple-element.24), channel_id=1, source_target_pairs={{0,256},{256,512},{512,768},{1,257},{257,513},{513,769},{2,258},{2... | collective-permute-start | bytes 83384 | tf_op jit(solution)/shard_map/ppermute | solution.py:32
  46.1 6.0 %collective-permute-start.9 = (f32[18,386]{1,0:T(8,128)S(1)}, f32[18,386]{1,0:T(8,128)S(1)}, u32[]{:S(2)}, u32[]{:S(2)}) collective-permute-start(f32[18,386]{1,0:T(8,128)S(1)} %get-tuple-element.25), channel_id=1, source_target_pairs={{256,0},{512,256},{768,512},{257,1},{513,257},{769,513},{258,2},{5... | collective-permute-start | bytes 83384 | tf_op jit(solution)/shard_map/ppermute | solution.py:33
  55.2 5.8 %collective-permute-start.10 = (f32[8,386]{1,0:T(8,128)S(1)}, f32[8,386]{1,0:T(8,128)S(1)}, u32[]{:S(2)}, u32[]{:S(2)}) collective-permute-start(f32[8,386]{1,0:T(8,128)S(1)} %get-tuple-element.43), channel_id=1, source_target_pairs={{0,32},{32,64},{64,96},{96,128},{128,160},{160,192},{192,224},{1,3... | collective-permute-start | bytes 37064 | tf_op jit(solution)/shard_map/ppermute | solution.py:32
  57.1 5.1 %collective-permute-start.11 = (f32[8,386]{1,0:T(8,128)S(1)}, f32[8,386]{1,0:T(8,128)S(1)}, u32[]{:S(2)}, u32[]{:S(2)}) collective-permute-start(f32[8,386]{1,0:T(8,128)S(1)} %get-tuple-element.44), channel_id=1, source_target_pairs={{32,0},{64,32},{96,64},{128,96},{160,128},{192,160},{224,192},{33,... | collective-permute-start | bytes 37064 | tf_op jit(solution)/shard_map/ppermute | solution.py:33
  62.3 6.0 %collective-permute-start.13 = (f32[18,386]{1,0:T(8,128)S(1)}, f32[18,386]{1,0:T(8,128)S(1)}, u32[]{:S(2)}, u32[]{:S(2)}) collective-permute-start(f32[18,386]{1,0:T(8,128)S(1)} %get-tuple-element.23), channel_id=1, source_target_pairs={{256,0},{512,256},{768,512},{257,1},{513,257},{769,513},{258,2},{5... | collective-permute-start | bytes 83384 | tf_op jit(solution)/shard_map/ppermute | solution.py:33
  63.6 6.3 %collective-permute-start.12 = (f32[18,386]{1,0:T(8,128)S(1)}, f32[18,386]{1,0:T(8,128)S(1)}, u32[]{:S(2)}, u32[]{:S(2)}) collective-permute-start(f32[18,386]{1,0:T(8,128)S(1)} %get-tuple-element.22), channel_id=1, source_target_pairs={{0,256},{256,512},{512,768},{1,257},{257,513},{513,769},{2,258},{2... | collective-permute-start | bytes 83384 | tf_op jit(solution)/shard_map/ppermute | solution.py:32
  72.8 5.8 %collective-permute-start.14 = (f32[8,386]{1,0:T(8,128)S(1)}, f32[8,386]{1,0:T(8,128)S(1)}, u32[]{:S(2)}, u32[]{:S(2)}) collective-permute-start(f32[8,386]{1,0:T(8,128)S(1)} %get-tuple-element.41), channel_id=1, source_target_pairs={{0,32},{32,64},{64,96},{96,128},{128,160},{160,192},{192,224},{1,3... | collective-permute-start | bytes 37064 | tf_op jit(solution)/shard_map/ppermute | solution.py:32
  74.7 5.1 %collective-permute-start.15 = (f32[8,386]{1,0:T(8,128)S(1)}, f32[8,386]{1,0:T(8,128)S(1)}, u32[]{:S(2)}, u32[]{:S(2)}) collective-permute-start(f32[8,386]{1,0:T(8,128)S(1)} %get-tuple-element.42), channel_id=1, source_target_pairs={{32,0},{64,32},{96,64},{128,96},{160,128},{192,160},{224,192},{33,... | collective-permute-start | bytes 37064 | tf_op jit(solution)/shard_map/ppermute | solution.py:33
  79.9 6.4 %collective-permute-start.17 = (f32[18,386]{1,0:T(8,128)S(1)}, f32[18,386]{1,0:T(8,128)S(1)}, u32[]{:S(2)}, u32[]{:S(2)}) collective-permute-start(f32[18,386]{1,0:T(8,128)S(1)} %get-tuple-element.18), channel_id=1, source_target_pairs={{256,0},{512,256},{768,512},{257,1},{513,257},{769,513},{258,2},{5... | collective-permute-start | bytes 83384 | tf_op jit(solution)/shard_map/ppermute | solution.py:33
  81.2 6.6 %collective-permute-start.16 = (f32[18,386]{1,0:T(8,128)S(1)}, f32[18,386]{1,0:T(8,128)S(1)}, u32[]{:S(2)}, u32[]{:S(2)}) collective-permute-start(f32[18,386]{1,0:T(8,128)S(1)} %get-tuple-element.19), channel_id=1, source_target_pairs={{0,256},{256,512},{512,768},{1,257},{257,513},{513,769},{2,258},{2... | collective-permute-start | bytes 83384 | tf_op jit(solution)/shard_map/ppermute | solution.py:32
  90.8 5.8 %collective-permute-start.18 = (f32[8,386]{1,0:T(8,128)S(1)}, f32[8,386]{1,0:T(8,128)S(1)}, u32[]{:S(2)}, u32[]{:S(2)}) collective-permute-start(f32[8,386]{1,0:T(8,128)S(1)} %get-tuple-element.39), channel_id=1, source_target_pairs={{0,32},{32,64},{64,96},{96,128},{128,160},{160,192},{192,224},{1,3... | collective-permute-start | bytes 37064 | tf_op jit(solution)/shard_map/ppermute | solution.py:32
  92.7 5.1 %collective-permute-start.19 = (f32[8,386]{1,0:T(8,128)S(1)}, f32[8,386]{1,0:T(8,128)S(1)}, u32[]{:S(2)}, u32[]{:S(2)}) collective-permute-start(f32[8,386]{1,0:T(8,128)S(1)} %get-tuple-element.40), channel_id=1, source_target_pairs={{32,0},{64,32},{96,64},{128,96},{160,128},{192,160},{224,192},{33,... | collective-permute-start | bytes 37064 | tf_op jit(solution)/shard_map/ppermute | solution.py:33
  97.9 6.0 %collective-permute-start.20 = (f32[18,386]{1,0:T(8,128)S(1)}, f32[18,386]{1,0:T(8,128)S(1)}, u32[]{:S(2)}, u32[]{:S(2)}) collective-permute-start(f32[18,386]{1,0:T(8,128)S(1)} %get-tuple-element.16), channel_id=1, source_target_pairs={{0,256},{256,512},{512,768},{1,257},{257,513},{513,769},{2,258},{2... | collective-permute-start | bytes 83384 | tf_op jit(solution)/shard_map/ppermute | solution.py:32
  102.2 6.0 %collective-permute-start.21 = (f32[18,386]{1,0:T(8,128)S(1)}, f32[18,386]{1,0:T(8,128)S(1)}, u32[]{:S(2)}, u32[]{:S(2)}) collective-permute-start(f32[18,386]{1,0:T(8,128)S(1)} %get-tuple-element.17), channel_id=1, source_target_pairs={{256,0},{512,256},{768,512},{257,1},{513,257},{769,513},{258,2},{5... | collective-permute-start | bytes 83384 | tf_op jit(solution)/shard_map/ppermute | solution.py:33
  108.8 0.9 copy-start.3
  110.5 3.1 %collective-permute-start.22 = (f32[8192]{0:T(1024)S(1)}, f32[8192]{0:T(1024)S(1)}, u32[]{:S(2)}, u32[]{:S(2)}) collective-permute-start(f32[8192]{0:T(1024)S(1)} %bitcast.193), channel_id=1, source_target_pairs={{0,32},{32,0},{64,96},{96,64},{128,160},{160,128},{192,224},{224,1... | collective-permute-start | bytes 98312 | tf_op jit(solution)/shard_map/ppermute | solution.py:52
  113.6 11.6 %collective-permute-start.23 = (f32[8192]{0:T(1024)S(1)}, f32[8192]{0:T(1024)S(1)}, u32[]{:S(2)}, u32[]{:S(2)}) collective-permute-start(f32[8192]{0:T(1024)S(1)} %add.360), channel_id=1, source_target_pairs={{0,192},{32,224},{64,128},{96,160},{128,64},{160,96},{192,0},{224,... | collective-permute-start | bytes 98312 | tf_op jit(solution)/shard_map/ppermute | solution.py:56
  125.2 5.8 %collective-permute-start.24 = (f32[8192]{0:T(1024)S(1)}, f32[8192]{0:T(1024)S(1)}, u32[]{:S(2)}, u32[]{:S(2)}) collective-permute-start(f32[8192]{0:T(1024)S(1)} %add.361), channel_id=1, source_target_pairs={{0,64},{32,96},{64,0},{96,32},{128,192},{160,224},{192,128},{224,1... | collective-permute-start | bytes 98312 | tf_op jit(solution)/shard_map/ppermute | solution.py:56
  131.0 6.2 %collective-permute-start.25 = (f32[8192]{0:T(1024)S(1)}, f32[8192]{0:T(1024)S(1)}, u32[]{:S(2)}, u32[]{:S(2)}) collective-permute-start(f32[8192]{0:T(1024)S(1)} %add.362), channel_id=1, source_target_pairs={{0,1},{1,0},{2,3},{3,2},{4,5},{5,4},{6,7},{7,6},{8,9},{9,8},{10,11... | collective-permute-start | bytes 98312 | tf_op jit(solution)/shard_map/ppermute | solution.py:52
  137.2 6.7 %collective-permute-start.26 = (f32[8192]{0:T(1024)S(1)}, f32[8192]{0:T(1024)S(1)}, u32[]{:S(2)}, u32[]{:S(2)}) collective-permute-start(f32[8192]{0:T(1024)S(1)} %add.363), channel_id=1, source_target_pairs={{0,2},{1,3},{2,0},{3,1},{4,6},{5,7},{6,4},{7,5},{8,10},{9,11},{10,... | collective-permute-start | bytes 98312 | tf_op jit(solution)/shard_map/ppermute | solution.py:52
  143.9 9.7 %collective-permute-start.27 = (f32[8192]{0:T(1024)S(1)}, f32[8192]{0:T(1024)S(1)}, u32[]{:S(2)}, u32[]{:S(2)}) collective-permute-start(f32[8192]{0:T(1024)S(1)} %add.364), channel_id=1, source_target_pairs={{0,4},{1,5},{2,6},{3,7},{4,0},{5,1},{6,2},{7,3},{8,12},{9,13},{10,... | collective-permute-start | bytes 98312 | tf_op jit(solution)/shard_map/ppermute | solution.py:52
  153.6 23.7 %collective-permute-start.28 = (f32[8192]{0:T(1024)S(1)}, f32[8192]{0:T(1024)S(1)}, u32[]{:S(2)}, u32[]{:S(2)}) collective-permute-start(f32[8192]{0:T(1024)S(1)} %add.365), channel_id=1, source_target_pairs={{0,24},{1,25},{2,26},{3,27},{4,28},{5,29},{6,30},{7,31},{8,16},{9,... | collective-permute-start | bytes 98312 | tf_op jit(solution)/shard_map/ppermute | solution.py:56
  177.4 14.5 %collective-permute-start.29 = (f32[8192]{0:T(1024)S(1)}, f32[8192]{0:T(1024)S(1)}, u32[]{:S(2)}, u32[]{:S(2)}) collective-permute-start(f32[8192]{0:T(1024)S(1)} %add.366), channel_id=1, source_target_pairs={{0,8},{1,9},{2,10},{3,11},{4,12},{5,13},{6,14},{7,15},{8,0},{9,1},... | collective-permute-start | bytes 98312 | tf_op jit(solution)/shard_map/ppermute | solution.py:56
  191.9 7.0 %collective-permute-start.30 = (f32[8192]{0:T(1024)S(1)}, f32[8192]{0:T(1024)S(1)}, u32[]{:S(2)}, u32[]{:S(2)}) collective-permute-start(f32[8192]{0:T(1024)S(1)} %add.367), channel_id=1, source_target_pairs={{0,768},{256,512},{512,256},{768,0},{1,769},{257,513},{513,257},{7... | collective-permute-start | bytes 98312 | tf_op jit(solution)/shard_map/ppermute | solution.py:56
  198.9 5.8 %collective-permute-start.31 = (f32[8192]{0:T(1024)S(1)}, f32[8192]{0:T(1024)S(1)}, u32[]{:S(2)}, u32[]{:S(2)}) collective-permute-start(f32[8192]{0:T(1024)S(1)} %add.368), channel_id=1, source_target_pairs={{0,256},{256,0},{512,768},{768,512},{1,257},{257,1},{513,769},{769... | collective-permute-start | bytes 98312 | tf_op jit(solution)/shard_map/ppermute | solution.py:56
  205.4 0.5 copy-start.12

commit v6 on v5

--- a/solution.py
+++ b/solution.py
@@ -9,6 +9,7 @@
 
 
 highest = lax.Precision.HIGHEST
+local_precision = lax.Precision.HIGH
 eig_high = 4.0
 eig_low = 0.2
 gll_inner = np.array(
@@ -85,10 +86,10 @@
 def forward_parts(field, mats):
     mat_x, mat_y, mat_z = mats
     size_x, size_y, size_z = field.shape
-    grad_x = jnp.einsum("ia,ajk->ijk", mat_x, field, precision=highest)
-    grad_y = jnp.einsum("ja,iak->ijk", mat_y, field, precision=highest)
+    grad_x = jnp.einsum("ia,ajk->ijk", mat_x, field, precision=local_precision)
+    grad_y = jnp.einsum("ja,iak->ijk", mat_y, field, precision=local_precision)
     blocks = field.reshape(size_x, size_y, size_z // 128, 128)
-    grad_z = jnp.einsum("ca,ijsa->ijsc", mat_z, blocks, precision=highest).reshape(field.shape)
+    grad_z = jnp.einsum("ca,ijsa->ijsc", mat_z, blocks, precision=local_precision).reshape(field.shape)
     return (grad_x, grad_y, grad_z)
 
 
@@ -96,10 +97,10 @@
     mat_x, mat_y, mat_z = mats
     part_x, part_y, part_z = parts
     size_x, size_y, size_z = part_x.shape
-    total = jnp.einsum("ai,ajk->ijk", mat_x, part_x, precision=highest)
-    total = total + jnp.einsum("aj,iak->ijk", mat_y, part_y, precision=highest)
+    total = jnp.einsum("ai,ajk->ijk", mat_x, part_x, precision=local_precision)
+    total = total + jnp.einsum("aj,iak->ijk", mat_y, part_y, precision=local_precision)
     blocks = part_z.reshape(size_x, size_y, size_z // 128, 128)
-    total = total + jnp.einsum("ac,ijsa->ijsc", mat_z, blocks, precision=highest).reshape(
+    total = total + jnp.einsum("ac,ijsa->ijsc", mat_z, blocks, precision=local_precision).reshape(
         part_x.shape
     )
     return total

time: 208 us -> 206 us (level)
  matrix products: 10.1 us -> 7.85 us
    dot_general x27, matrix products: 9.07 us -> 6.8 us  [the longest x5 1.49 us: backward_sum(): total = jnp.einsum('ai,ajk->ijk', mat_x, part_x, precision=local_precision)]
  transfers between devices with their start and end apart: 32 -> 32, of which waited for: 26 -> 27; matrix products, arithmetic and copies ran while one was open for 1% -> 1% of each run, Pallas kernels for 0% -> 0%
where the time goes in v6:
time: 206 us; the launch traced here: 205 us
  starting transfers between devices  123 us (60%)
  waiting for transfers between devices  57.2 us (28%)
  local copies, waits for them, and re-layouts  9.64 us (5%)
  matrix products  7.85 us (4%)
  other arithmetic  5.31 us (3%)
    ppermute x6, starting transfers between devices, butterfly_sum(): value = value + lax.ppermute(value, axis, pairs)  48.3 us
    ppermute x10, starting transfers between devices, padded_2(): lax.ppermute(jnp.squeeze(tail, dim), axis, [(i, i + 1) for i in range(end...  30.5 us
    ppermute x10, starting transfers between devices, padded_2(): lax.ppermute(jnp.squeeze(head, dim), axis, [(i + 1, i) for i in range(end...  23.1 us
    ppermute x6, waiting for transfers between devices, butterfly_sum(): value = value + lax.ppermute(value, axis, pairs)  20.1 us
    ppermute x10, waiting for transfers between devices, padded_2(): lax.ppermute(jnp.squeeze(head, dim), axis, [(i + 1, i) for i in range(end...  17.9 us
    ppermute x4, starting transfers between devices, butterfly_sum(): lax.ppermute(value, axis, [(i, i ^ stride) for i in range(count)])  15.5 us
    ppermute x4, waiting for transfers between devices, butterfly_sum(): lax.ppermute(value, axis, [(i, i ^ stride) for i in range(count)])  10.2 us
    unnamed x32, local copies, waits for them, and re-layouts  6.52 us
  transfers between devices with their start and end apart: 32, of which 27 were waited for; matrix products, arithmetic and copies ran while one was open for 1% of the time, Pallas kernels for 0%

profile of v6, /device:TPU:24, one launch (start us, length us, event | category | flops | bytes accessed | tf_op | source)
XLA Modules:
  0.0 205.0 jit_solution(8241272928571296640)
XLA Ops:
  0.6 1.2 copy_bitcast_fusion
  1.9 1.3 collective-permute-start.1
  3.2 4.6 %collective-permute-start = (f32[2,8,16,64]{3,1,2,0:T(8,128)S(1)}, f32[2,8,16,64]{3,1,2,0:T(8,128)S(1)}, u32[]{:S(2)}, u32[]{:S(2)}) collective-permute-start(f32[2,8,16,64]{3,1,2,0:T(8,128)S(1)} %get-tuple-element.37), channel_id=1, source_target_pairs={{0,1},{1,2},{2,3},{3,4},{4,5},{5,6},{6,7},{7,8},{8,9},{9,10},{10,1... | collective-permute-start | bytes 196616 | tf_op jit(solution)/shard_map/ppermute | solution.py:125
  7.8 1.4 collective-permute-done.1
  9.2 1.2 collective-permute-done
  10.7 0.6 copy-done.5
  11.4 0.6 copy-done.9
  12.1 0.7 copy-done.8
  13.8 0.5 copy-done.11
  14.6 1.9 collective-permute-start.3
  16.5 2.4 %collective-permute-start.2 = (f32[8,386]{1,0:T(8,128)S(1)}, f32[8,386]{1,0:T(8,128)S(1)}, u32[]{:S(2)}, u32[]{:S(2)}) collective-permute-start(f32[8,386]{1,0:T(8,128)S(1)} %get-tuple-element.47), channel_id=1, source_target_pairs={{0,32},{32,64},{64,96},{96,128},{128,160},{160,192},{192,224},{1,3... | collective-permute-start | bytes 37064 | tf_op jit(solution)/shard_map/ppermute | solution.py:33
  19.1 2.4 %collective-permute-done.2 = f32[8,386]{1,0:T(8,128)S(1)} collective-permute-done((f32[8,386]{1,0:T(8,128)S(1)}, f32[8,386]{1,0:T(8,128)S(1)}, u32[]{:S(2)}, u32[]{:S(2)}) %collective-permute-start.2) | collective-permute-done | bytes 12384 | tf_op jit(solution)/shard_map/ppermute | solution.py:33
  21.7 3.4 %collective-permute-start.4 = (f32[18,386]{1,0:T(8,128)S(1)}, f32[18,386]{1,0:T(8,128)S(1)}, u32[]{:S(2)}, u32[]{:S(2)}) collective-permute-start(f32[18,386]{1,0:T(8,128)S(1)} %get-tuple-element.26), channel_id=1, source_target_pairs={{0,256},{256,512},{512,768},{1,257},{257,513},{513,769},{2,258},{2... | collective-permute-start | bytes 83384 | tf_op jit(solution)/shard_map/ppermute | solution.py:33
  25.3 1.3 collective-permute-start.5
  27.0 4.3 %collective-permute-done.5 = f32[18,386]{1,0:T(8,128)S(1)} collective-permute-done((f32[18,386]{1,0:T(8,128)S(1)}, f32[18,386]{1,0:T(8,128)S(1)}, u32[]{:S(2)}, u32[]{:S(2)}) %collective-permute-start.5) | collective-permute-done | bytes 27824 | tf_op jit(solution)/shard_map/ppermute | solution.py:34
  31.9 0.6 copy-done.1
  33.7 0.5 copy-done.2
  35.2 1.9 collective-permute-start.6
  37.1 3.6 %collective-permute-start.7 = (f32[8,386]{1,0:T(8,128)S(1)}, f32[8,386]{1,0:T(8,128)S(1)}, u32[]{:S(2)}, u32[]{:S(2)}) collective-permute-start(f32[8,386]{1,0:T(8,128)S(1)} %get-tuple-element.46), channel_id=1, source_target_pairs={{32,0},{64,32},{96,64},{128,96},{160,128},{192,160},{224,192},{33,... | collective-permute-start | bytes 37064 | tf_op jit(solution)/shard_map/ppermute | solution.py:34
  41.0 1.2 collective-permute-done.7
  42.3 3.4 %collective-permute-start.8 = (f32[18,386]{1,0:T(8,128)S(1)}, f32[18,386]{1,0:T(8,128)S(1)}, u32[]{:S(2)}, u32[]{:S(2)}) collective-permute-start(f32[18,386]{1,0:T(8,128)S(1)} %get-tuple-element.24), channel_id=1, source_target_pairs={{0,256},{256,512},{512,768},{1,257},{257,513},{513,769},{2,258},{2... | collective-permute-start | bytes 83384 | tf_op jit(solution)/shard_map/ppermute | solution.py:33
  45.7 1.3 collective-permute-start.9
  47.4 4.3 %collective-permute-done.9 = f32[18,386]{1,0:T(8,128)S(1)} collective-permute-done((f32[18,386]{1,0:T(8,128)S(1)}, f32[18,386]{1,0:T(8,128)S(1)}, u32[]{:S(2)}, u32[]{:S(2)}) %collective-permute-start.9) | collective-permute-done | bytes 27824 | tf_op jit(solution)/shard_map/ppermute | solution.py:34
  54.2 1.9 collective-permute-start.10
  56.2 3.6 %collective-permute-start.11 = (f32[8,386]{1,0:T(8,128)S(1)}, f32[8,386]{1,0:T(8,128)S(1)}, u32[]{:S(2)}, u32[]{:S(2)}) collective-permute-start(f32[8,386]{1,0:T(8,128)S(1)} %get-tuple-element.44), channel_id=1, source_target_pairs={{32,0},{64,32},{96,64},{128,96},{160,128},{192,160},{224,192},{33,... | collective-permute-start | bytes 37064 | tf_op jit(solution)/shard_map/ppermute | solution.py:34
  60.0 1.2 collective-permute-done.11
  61.3 1.3 collective-permute-start.13
  62.6 4.5 %collective-permute-start.12 = (f32[18,386]{1,0:T(8,128)S(1)}, f32[18,386]{1,0:T(8,128)S(1)}, u32[]{:S(2)}, u32[]{:S(2)}) collective-permute-start(f32[18,386]{1,0:T(8,128)S(1)} %get-tuple-element.22), channel_id=1, source_target_pairs={{0,256},{256,512},{512,768},{1,257},{257,513},{513,769},{2,258},{2... | collective-permute-start | bytes 83384 | tf_op jit(solution)/shard_map/ppermute | solution.py:33
  67.3 1.6 collective-permute-done.12
  71.4 1.9 collective-permute-start.14
  73.3 3.6 %collective-permute-start.15 = (f32[8,386]{1,0:T(8,128)S(1)}, f32[8,386]{1,0:T(8,128)S(1)}, u32[]{:S(2)}, u32[]{:S(2)}) collective-permute-start(f32[8,386]{1,0:T(8,128)S(1)} %get-tuple-element.42), channel_id=1, source_target_pairs={{32,0},{64,32},{96,64},{128,96},{160,128},{192,160},{224,192},{33,... | collective-permute-start | bytes 37064 | tf_op jit(solution)/shard_map/ppermute | solution.py:34
  77.2 1.2 collective-permute-done.15
  78.5 1.3 collective-permute-start.17
  79.8 4.9 %collective-permute-start.16 = (f32[18,386]{1,0:T(8,128)S(1)}, f32[18,386]{1,0:T(8,128)S(1)}, u32[]{:S(2)}, u32[]{:S(2)}) collective-permute-start(f32[18,386]{1,0:T(8,128)S(1)} %get-tuple-element.19), channel_id=1, source_target_pairs={{0,256},{256,512},{512,768},{1,257},{257,513},{513,769},{2,258},{2... | collective-permute-start | bytes 83384 | tf_op jit(solution)/shard_map/ppermute | solution.py:33
  84.8 1.6 collective-permute-done.16
  88.9 1.9 collective-permute-start.18
  90.8 3.6 %collective-permute-start.19 = (f32[8,386]{1,0:T(8,128)S(1)}, f32[8,386]{1,0:T(8,128)S(1)}, u32[]{:S(2)}, u32[]{:S(2)}) collective-permute-start(f32[8,386]{1,0:T(8,128)S(1)} %get-tuple-element.40), channel_id=1, source_target_pairs={{32,0},{64,32},{96,64},{128,96},{160,128},{192,160},{224,192},{33,... | collective-permute-start | bytes 37064 | tf_op jit(solution)/shard_map/ppermute | solution.py:34
  94.7 1.2 collective-permute-done.19
  96.0 4.2 %collective-permute-start.20 = (f32[18,386]{1,0:T(8,128)S(1)}, f32[18,386]{1,0:T(8,128)S(1)}, u32[]{:S(2)}, u32[]{:S(2)}) collective-permute-start(f32[18,386]{1,0:T(8,128)S(1)} %get-tuple-element.16), channel_id=1, source_target_pairs={{0,256},{256,512},{512,768},{1,257},{257,513},{513,769},{2,258},{2... | collective-permute-start | bytes 83384 | tf_op jit(solution)/shard_map/ppermute | solution.py:33
  100.2 1.5 collective-permute-start.21
  102.0 4.3 %collective-permute-done.21 = f32[18,386]{1,0:T(8,128)S(1)} collective-permute-done((f32[18,386]{1,0:T(8,128)S(1)}, f32[18,386]{1,0:T(8,128)S(1)}, u32[]{:S(2)}, u32[]{:S(2)}) %collective-permute-start.21) | collective-permute-done | bytes 27824 | tf_op jit(solution)/shard_map/ppermute | solution.py:34
  107.0 0.7 copy-done.3
  108.5 1.9 collective-permute-start.22
  110.5 1.2 collective-permute-done.22
  111.6 9.7 %collective-permute-start.23 = (f32[8192]{0:T(1024)S(1)}, f32[8192]{0:T(1024)S(1)}, u32[]{:S(2)}, u32[]{:S(2)}) collective-permute-start(f32[8192]{0:T(1024)S(1)} %add.360), channel_id=1, source_target_pairs={{0,192},{32,224},{64,128},{96,160},{128,64},{160,96},{192,0},{224,... | collective-permute-start | bytes 98312 | tf_op jit(solution)/shard_map/ppermute | solution.py:57
  121.3 1.9 collective-permute-done.23
  123.2 2.7 %collective-permute-start.24 = (f32[8192]{0:T(1024)S(1)}, f32[8192]{0:T(1024)S(1)}, u32[]{:S(2)}, u32[]{:S(2)}) collective-permute-start(f32[8192]{0:T(1024)S(1)} %add.361), channel_id=1, source_target_pairs={{0,64},{32,96},{64,0},{96,32},{128,192},{160,224},{192,128},{224,1... | collective-permute-start | bytes 98312 | tf_op jit(solution)/shard_map/ppermute | solution.py:57
  125.9 3.1 %collective-permute-done.24 = f32[8192]{0:T(1024)S(1)} collective-permute-done((f32[8192]{0:T(1024)S(1)}, f32[8192]{0:T(1024)S(1)}, u32[]{:S(2)}, u32[]{:S(2)}) %collective-permute-start.24) | collective-permute-done | bytes 32800 | tf_op jit(solution)/shard_map/ppermute | solution.py:57
  129.0 4.3 %collective-permute-start.25 = (f32[8192]{0:T(1024)S(1)}, f32[8192]{0:T(1024)S(1)}, u32[]{:S(2)}, u32[]{:S(2)}) collective-permute-start(f32[8192]{0:T(1024)S(1)} %add.362), channel_id=1, source_target_pairs={{0,1},{1,0},{2,3},{3,2},{4,5},{5,4},{6,7},{7,6},{8,9},{9,8},{10,11... | collective-permute-start | bytes 98312 | tf_op jit(solution)/shard_map/ppermute | solution.py:53
  133.4 1.9 collective-permute-done.25
  135.3 3.4 %collective-permute-start.26 = (f32[8192]{0:T(1024)S(1)}, f32[8192]{0:T(1024)S(1)}, u32[]{:S(2)}, u32[]{:S(2)}) collective-permute-start(f32[8192]{0:T(1024)S(1)} %add.363), channel_id=1, source_target_pairs={{0,2},{1,3},{2,0},{3,1},{4,6},{5,7},{6,4},{7,5},{8,10},{9,11},{10,... | collective-permute-start | bytes 98312 | tf_op jit(solution)/shard_map/ppermute | solution.py:53
  138.6 3.3 %collective-permute-done.26 = f32[8192]{0:T(1024)S(1)} collective-permute-done((f32[8192]{0:T(1024)S(1)}, f32[8192]{0:T(1024)S(1)}, u32[]{:S(2)}, u32[]{:S(2)}) %collective-permute-start.26) | collective-permute-done | bytes 32800 | tf_op jit(solution)/shard_map/ppermute | solution.py:53
  142.0 5.9 %collective-permute-start.27 = (f32[8192]{0:T(1024)S(1)}, f32[8192]{0:T(1024)S(1)}, u32[]{:S(2)}, u32[]{:S(2)}) collective-permute-start(f32[8192]{0:T(1024)S(1)} %add.364), channel_id=1, source_target_pairs={{0,4},{1,5},{2,6},{3,7},{4,0},{5,1},{6,2},{7,3},{8,12},{9,13},{10,... | collective-permute-start | bytes 98312 | tf_op jit(solution)/shard_map/ppermute | solution.py:53
  147.8 3.8 %collective-permute-done.27 = f32[8192]{0:T(1024)S(1)} collective-permute-done((f32[8192]{0:T(1024)S(1)}, f32[8192]{0:T(1024)S(1)}, u32[]{:S(2)}, u32[]{:S(2)}) %collective-permute-start.27) | collective-permute-done | bytes 32800 | tf_op jit(solution)/shard_map/ppermute | solution.py:53
  151.7 21.9 %collective-permute-start.28 = (f32[8192]{0:T(1024)S(1)}, f32[8192]{0:T(1024)S(1)}, u32[]{:S(2)}, u32[]{:S(2)}) collective-permute-start(f32[8192]{0:T(1024)S(1)} %add.365), channel_id=1, source_target_pairs={{0,24},{1,25},{2,26},{3,27},{4,28},{5,29},{6,30},{7,31},{8,16},{9,... | collective-permute-start | bytes 98312 | tf_op jit(solution)/shard_map/ppermute | solution.py:57
  173.5 1.9 collective-permute-done.28
  175.4 8.0 %collective-permute-start.29 = (f32[8192]{0:T(1024)S(1)}, f32[8192]{0:T(1024)S(1)}, u32[]{:S(2)}, u32[]{:S(2)}) collective-permute-start(f32[8192]{0:T(1024)S(1)} %add.366), channel_id=1, source_target_pairs={{0,8},{1,9},{2,10},{3,11},{4,12},{5,13},{6,14},{7,15},{8,0},{9,1},... | collective-permute-start | bytes 98312 | tf_op jit(solution)/shard_map/ppermute | solution.py:57
  183.5 6.5 %collective-permute-done.29 = f32[8192]{0:T(1024)S(1)} collective-permute-done((f32[8192]{0:T(1024)S(1)}, f32[8192]{0:T(1024)S(1)}, u32[]{:S(2)}, u32[]{:S(2)}) %collective-permute-start.29) | collective-permute-done | bytes 32800 | tf_op jit(solution)/shard_map/ppermute | solution.py:57
  190.0 3.4 %collective-permute-start.30 = (f32[8192]{0:T(1024)S(1)}, f32[8192]{0:T(1024)S(1)}, u32[]{:S(2)}, u32[]{:S(2)}) collective-permute-start(f32[8192]{0:T(1024)S(1)} %add.367), channel_id=1, source_target_pairs={{0,768},{256,512},{512,256},{768,0},{1,769},{257,513},{513,257},{7... | collective-permute-start | bytes 98312 | tf_op jit(solution)/shard_map/ppermute | solution.py:57
  193.4 3.6 %collective-permute-done.30 = f32[8192]{0:T(1024)S(1)} collective-permute-done((f32[8192]{0:T(1024)S(1)}, f32[8192]{0:T(1024)S(1)}, u32[]{:S(2)}, u32[]{:S(2)}) %collective-permute-start.30) | collective-permute-done | bytes 32800 | tf_op jit(solution)/shard_map/ppermute | solution.py:57
  197.0 2.7 %collective-permute-start.31 = (f32[8192]{0:T(1024)S(1)}, f32[8192]{0:T(1024)S(1)}, u32[]{:S(2)}, u32[]{:S(2)}) collective-permute-start(f32[8192]{0:T(1024)S(1)} %add.368), channel_id=1, source_target_pairs={{0,256},{256,0},{512,768},{768,512},{1,257},{257,1},{513,769},{769... | collective-permute-start | bytes 98312 | tf_op jit(solution)/shard_map/ppermute | solution.py:57
  199.7 3.1 %collective-permute-done.31 = f32[8192]{0:T(1024)S(1)} collective-permute-done((f32[8192]{0:T(1024)S(1)}, f32[8192]{0:T(1024)S(1)}, u32[]{:S(2)}, u32[]{:S(2)}) %collective-permute-start.31) | collective-permute-done | bytes 32800 | tf_op jit(solution)/shard_map/ppermute | solution.py:57
  202.8 0.7 convolution_bitcast_fusion.5
  204.3 0.7 copy.165
  (146 shorter events, 17.0 us)
Async XLA Ops:
  0.6 107.5 %copy-start = (f32[8,8192]{1,0:T(8,128)S(1)}, f32[8,8192]{1,0:T(8,128)}, u32[]{:S(2)}) copy-start(f32[8,8192]{1,0:T(8,128)} %param.13) | copy-start | bytes 786436
  1.9 7.3 %collective-permute-start.1 = (f32[2,8,16,64]{3,1,2,0:T(8,128)S(1)}, f32[2,8,16,64]{3,1,2,0:T(8,128)S(1)}, u32[]{:S(2)}, u32[]{:S(2)}) collective-permute-start(f32[2,8,16,64]{3,1,2,0:T(8,128)S(1)} %get-tuple-element.38), channel_id=1, source_target_pairs={{1,0},{2,1},{3,2},{4,3},{5,4},{6,5},{7,6},{8,7},{9,8},{10,9},{11,1... | collective-permute-start | bytes 196616 | tf_op jit(solution)/shard_map/ppermute | solution.py:126
  3.2 7.2 %collective-permute-start = (f32[2,8,16,64]{3,1,2,0:T(8,128)S(1)}, f32[2,8,16,64]{3,1,2,0:T(8,128)S(1)}, u32[]{:S(2)}, u32[]{:S(2)}) collective-permute-start(f32[2,8,16,64]{3,1,2,0:T(8,128)S(1)} %get-tuple-element.37), channel_id=1, source_target_pairs={{0,1},{1,2},{2,3},{3,4},{4,5},{5,6},{6,7},{7,8},{8,9},{9,10},{10,1... | collective-permute-start | bytes 196616 | tf_op jit(solution)/shard_map/ppermute | solution.py:125
  10.6 0.7 copy-start.5
  10.6 0.7 copy-start.6
  10.6 0.7 copy-start.7
  11.3 0.7 copy-start.9
  12.0 0.8 copy-start.8
  12.8 0.7 copy-start.10
  13.5 0.7 copy-start.11
  14.6 7.0 %collective-permute-start.3 = (f32[8,386]{1,0:T(8,128)S(1)}, f32[8,386]{1,0:T(8,128)S(1)}, u32[]{:S(2)}, u32[]{:S(2)}) collective-permute-start(f32[8,386]{1,0:T(8,128)S(1)} %get-tuple-element.48), channel_id=1, source_target_pairs={{32,0},{64,32},{96,64},{128,96},{160,128},{192,160},{224,192},{33,... | collective-permute-start | bytes 37064 | tf_op jit(solution)/shard_map/ppermute | solution.py:34
  16.5 5.1 %collective-permute-start.2 = (f32[8,386]{1,0:T(8,128)S(1)}, f32[8,386]{1,0:T(8,128)S(1)}, u32[]{:S(2)}, u32[]{:S(2)}) collective-permute-start(f32[8,386]{1,0:T(8,128)S(1)} %get-tuple-element.47), channel_id=1, source_target_pairs={{0,32},{32,64},{64,96},{96,128},{128,160},{160,192},{192,224},{1,3... | collective-permute-start | bytes 37064 | tf_op jit(solution)/shard_map/ppermute | solution.py:33
  21.7 5.1 %collective-permute-start.4 = (f32[18,386]{1,0:T(8,128)S(1)}, f32[18,386]{1,0:T(8,128)S(1)}, u32[]{:S(2)}, u32[]{:S(2)}) collective-permute-start(f32[18,386]{1,0:T(8,128)S(1)} %get-tuple-element.26), channel_id=1, source_target_pairs={{0,256},{256,512},{512,768},{1,257},{257,513},{513,769},{2,258},{2... | collective-permute-start | bytes 83384 | tf_op jit(solution)/shard_map/ppermute | solution.py:33
  25.3 6.0 %collective-permute-start.5 = (f32[18,386]{1,0:T(8,128)S(1)}, f32[18,386]{1,0:T(8,128)S(1)}, u32[]{:S(2)}, u32[]{:S(2)}) collective-permute-start(f32[18,386]{1,0:T(8,128)S(1)} %get-tuple-element.27), channel_id=1, source_target_pairs={{256,0},{512,256},{768,512},{257,1},{513,257},{769,513},{258,2},{5... | collective-permute-start | bytes 83384 | tf_op jit(solution)/shard_map/ppermute | solution.py:34
  31.7 0.8 copy-start.1
  32.8 0.7 copy-start.4
  33.5 0.7 copy-start.2
  35.2 5.8 %collective-permute-start.6 = (f32[8,386]{1,0:T(8,128)S(1)}, f32[8,386]{1,0:T(8,128)S(1)}, u32[]{:S(2)}, u32[]{:S(2)}) collective-permute-start(f32[8,386]{1,0:T(8,128)S(1)} %get-tuple-element.45), channel_id=1, source_target_pairs={{0,32},{32,64},{64,96},{96,128},{128,160},{160,192},{192,224},{1,3... | collective-permute-start | bytes 37064 | tf_op jit(solution)/shard_map/ppermute | solution.py:33
  37.1 5.1 %collective-permute-start.7 = (f32[8,386]{1,0:T(8,128)S(1)}, f32[8,386]{1,0:T(8,128)S(1)}, u32[]{:S(2)}, u32[]{:S(2)}) collective-permute-start(f32[8,386]{1,0:T(8,128)S(1)} %get-tuple-element.46), channel_id=1, source_target_pairs={{32,0},{64,32},{96,64},{128,96},{160,128},{192,160},{224,192},{33,... | collective-permute-start | bytes 37064 | tf_op jit(solution)/shard_map/ppermute | solution.py:34
  42.3 5.1 %collective-permute-start.8 = (f32[18,386]{1,0:T(8,128)S(1)}, f32[18,386]{1,0:T(8,128)S(1)}, u32[]{:S(2)}, u32[]{:S(2)}) collective-permute-start(f32[18,386]{1,0:T(8,128)S(1)} %get-tuple-element.24), channel_id=1, source_target_pairs={{0,256},{256,512},{512,768},{1,257},{257,513},{513,769},{2,258},{2... | collective-permute-start | bytes 83384 | tf_op jit(solution)/shard_map/ppermute | solution.py:33
  45.7 6.0 %collective-permute-start.9 = (f32[18,386]{1,0:T(8,128)S(1)}, f32[18,386]{1,0:T(8,128)S(1)}, u32[]{:S(2)}, u32[]{:S(2)}) collective-permute-start(f32[18,386]{1,0:T(8,128)S(1)} %get-tuple-element.25), channel_id=1, source_target_pairs={{256,0},{512,256},{768,512},{257,1},{513,257},{769,513},{258,2},{5... | collective-permute-start | bytes 83384 | tf_op jit(solution)/shard_map/ppermute | solution.py:34
  54.2 5.8 %collective-permute-start.10 = (f32[8,386]{1,0:T(8,128)S(1)}, f32[8,386]{1,0:T(8,128)S(1)}, u32[]{:S(2)}, u32[]{:S(2)}) collective-permute-start(f32[8,386]{1,0:T(8,128)S(1)} %get-tuple-element.43), channel_id=1, source_target_pairs={{0,32},{32,64},{64,96},{96,128},{128,160},{160,192},{192,224},{1,3... | collective-permute-start | bytes 37064 | tf_op jit(solution)/shard_map/ppermute | solution.py:33
  56.2 5.1 %collective-permute-start.11 = (f32[8,386]{1,0:T(8,128)S(1)}, f32[8,386]{1,0:T(8,128)S(1)}, u32[]{:S(2)}, u32[]{:S(2)}) collective-permute-start(f32[8,386]{1,0:T(8,128)S(1)} %get-tuple-element.44), channel_id=1, source_target_pairs={{32,0},{64,32},{96,64},{128,96},{160,128},{192,160},{224,192},{33,... | collective-permute-start | bytes 37064 | tf_op jit(solution)/shard_map/ppermute | solution.py:34
  61.3 6.0 %collective-permute-start.13 = (f32[18,386]{1,0:T(8,128)S(1)}, f32[18,386]{1,0:T(8,128)S(1)}, u32[]{:S(2)}, u32[]{:S(2)}) collective-permute-start(f32[18,386]{1,0:T(8,128)S(1)} %get-tuple-element.23), channel_id=1, source_target_pairs={{256,0},{512,256},{768,512},{257,1},{513,257},{769,513},{258,2},{5... | collective-permute-start | bytes 83384 | tf_op jit(solution)/shard_map/ppermute | solution.py:34
  62.6 6.3 %collective-permute-start.12 = (f32[18,386]{1,0:T(8,128)S(1)}, f32[18,386]{1,0:T(8,128)S(1)}, u32[]{:S(2)}, u32[]{:S(2)}) collective-permute-start(f32[18,386]{1,0:T(8,128)S(1)} %get-tuple-element.22), channel_id=1, source_target_pairs={{0,256},{256,512},{512,768},{1,257},{257,513},{513,769},{2,258},{2... | collective-permute-start | bytes 83384 | tf_op jit(solution)/shard_map/ppermute | solution.py:33
  71.4 5.8 %collective-permute-start.14 = (f32[8,386]{1,0:T(8,128)S(1)}, f32[8,386]{1,0:T(8,128)S(1)}, u32[]{:S(2)}, u32[]{:S(2)}) collective-permute-start(f32[8,386]{1,0:T(8,128)S(1)} %get-tuple-element.41), channel_id=1, source_target_pairs={{0,32},{32,64},{64,96},{96,128},{128,160},{160,192},{192,224},{1,3... | collective-permute-start | bytes 37064 | tf_op jit(solution)/shard_map/ppermute | solution.py:33
  73.3 5.1 %collective-permute-start.15 = (f32[8,386]{1,0:T(8,128)S(1)}, f32[8,386]{1,0:T(8,128)S(1)}, u32[]{:S(2)}, u32[]{:S(2)}) collective-permute-start(f32[8,386]{1,0:T(8,128)S(1)} %get-tuple-element.42), channel_id=1, source_target_pairs={{32,0},{64,32},{96,64},{128,96},{160,128},{192,160},{224,192},{33,... | collective-permute-start | bytes 37064 | tf_op jit(solution)/shard_map/ppermute | solution.py:34
  78.5 6.3 %collective-permute-start.17 = (f32[18,386]{1,0:T(8,128)S(1)}, f32[18,386]{1,0:T(8,128)S(1)}, u32[]{:S(2)}, u32[]{:S(2)}) collective-permute-start(f32[18,386]{1,0:T(8,128)S(1)} %get-tuple-element.18), channel_id=1, source_target_pairs={{256,0},{512,256},{768,512},{257,1},{513,257},{769,513},{258,2},{5... | collective-permute-start | bytes 83384 | tf_op jit(solution)/shard_map/ppermute | solution.py:34
  79.8 6.6 %collective-permute-start.16 = (f32[18,386]{1,0:T(8,128)S(1)}, f32[18,386]{1,0:T(8,128)S(1)}, u32[]{:S(2)}, u32[]{:S(2)}) collective-permute-start(f32[18,386]{1,0:T(8,128)S(1)} %get-tuple-element.19), channel_id=1, source_target_pairs={{0,256},{256,512},{512,768},{1,257},{257,513},{513,769},{2,258},{2... | collective-permute-start | bytes 83384 | tf_op jit(solution)/shard_map/ppermute | solution.py:33
  88.9 5.8 %collective-permute-start.18 = (f32[8,386]{1,0:T(8,128)S(1)}, f32[8,386]{1,0:T(8,128)S(1)}, u32[]{:S(2)}, u32[]{:S(2)}) collective-permute-start(f32[8,386]{1,0:T(8,128)S(1)} %get-tuple-element.39), channel_id=1, source_target_pairs={{0,32},{32,64},{64,96},{96,128},{128,160},{160,192},{192,224},{1,3... | collective-permute-start | bytes 37064 | tf_op jit(solution)/shard_map/ppermute | solution.py:33
  90.8 5.1 %collective-permute-start.19 = (f32[8,386]{1,0:T(8,128)S(1)}, f32[8,386]{1,0:T(8,128)S(1)}, u32[]{:S(2)}, u32[]{:S(2)}) collective-permute-start(f32[8,386]{1,0:T(8,128)S(1)} %get-tuple-element.40), channel_id=1, source_target_pairs={{32,0},{64,32},{96,64},{128,96},{160,128},{192,160},{224,192},{33,... | collective-permute-start | bytes 37064 | tf_op jit(solution)/shard_map/ppermute | solution.py:34
  96.0 6.0 %collective-permute-start.20 = (f32[18,386]{1,0:T(8,128)S(1)}, f32[18,386]{1,0:T(8,128)S(1)}, u32[]{:S(2)}, u32[]{:S(2)}) collective-permute-start(f32[18,386]{1,0:T(8,128)S(1)} %get-tuple-element.16), channel_id=1, source_target_pairs={{0,256},{256,512},{512,768},{1,257},{257,513},{513,769},{2,258},{2... | collective-permute-start | bytes 83384 | tf_op jit(solution)/shard_map/ppermute | solution.py:33
  100.2 6.0 %collective-permute-start.21 = (f32[18,386]{1,0:T(8,128)S(1)}, f32[18,386]{1,0:T(8,128)S(1)}, u32[]{:S(2)}, u32[]{:S(2)}) collective-permute-start(f32[18,386]{1,0:T(8,128)S(1)} %get-tuple-element.17), channel_id=1, source_target_pairs={{256,0},{512,256},{768,512},{257,1},{513,257},{769,513},{258,2},{5... | collective-permute-start | bytes 83384 | tf_op jit(solution)/shard_map/ppermute | solution.py:34
  106.8 0.9 copy-start.3
  108.5 3.1 %collective-permute-start.22 = (f32[8192]{0:T(1024)S(1)}, f32[8192]{0:T(1024)S(1)}, u32[]{:S(2)}, u32[]{:S(2)}) collective-permute-start(f32[8192]{0:T(1024)S(1)} %bitcast.193), channel_id=1, source_target_pairs={{0,32},{32,0},{64,96},{96,64},{128,160},{160,128},{192,224},{224,1... | collective-permute-start | bytes 98312 | tf_op jit(solution)/shard_map/ppermute | solution.py:53
  111.6 11.6 %collective-permute-start.23 = (f32[8192]{0:T(1024)S(1)}, f32[8192]{0:T(1024)S(1)}, u32[]{:S(2)}, u32[]{:S(2)}) collective-permute-start(f32[8192]{0:T(1024)S(1)} %add.360), channel_id=1, source_target_pairs={{0,192},{32,224},{64,128},{96,160},{128,64},{160,96},{192,0},{224,... | collective-permute-start | bytes 98312 | tf_op jit(solution)/shard_map/ppermute | solution.py:57
  123.2 5.8 %collective-permute-start.24 = (f32[8192]{0:T(1024)S(1)}, f32[8192]{0:T(1024)S(1)}, u32[]{:S(2)}, u32[]{:S(2)}) collective-permute-start(f32[8192]{0:T(1024)S(1)} %add.361), channel_id=1, source_target_pairs={{0,64},{32,96},{64,0},{96,32},{128,192},{160,224},{192,128},{224,1... | collective-permute-start | bytes 98312 | tf_op jit(solution)/shard_map/ppermute | solution.py:57
  129.0 6.2 %collective-permute-start.25 = (f32[8192]{0:T(1024)S(1)}, f32[8192]{0:T(1024)S(1)}, u32[]{:S(2)}, u32[]{:S(2)}) collective-permute-start(f32[8192]{0:T(1024)S(1)} %add.362), channel_id=1, source_target_pairs={{0,1},{1,0},{2,3},{3,2},{4,5},{5,4},{6,7},{7,6},{8,9},{9,8},{10,11... | collective-permute-start | bytes 98312 | tf_op jit(solution)/shard_map/ppermute | solution.py:53
  135.3 6.7 %collective-permute-start.26 = (f32[8192]{0:T(1024)S(1)}, f32[8192]{0:T(1024)S(1)}, u32[]{:S(2)}, u32[]{:S(2)}) collective-permute-start(f32[8192]{0:T(1024)S(1)} %add.363), channel_id=1, source_target_pairs={{0,2},{1,3},{2,0},{3,1},{4,6},{5,7},{6,4},{7,5},{8,10},{9,11},{10,... | collective-permute-start | bytes 98312 | tf_op jit(solution)/shard_map/ppermute | solution.py:53
  142.0 9.7 %collective-permute-start.27 = (f32[8192]{0:T(1024)S(1)}, f32[8192]{0:T(1024)S(1)}, u32[]{:S(2)}, u32[]{:S(2)}) collective-permute-start(f32[8192]{0:T(1024)S(1)} %add.364), channel_id=1, source_target_pairs={{0,4},{1,5},{2,6},{3,7},{4,0},{5,1},{6,2},{7,3},{8,12},{9,13},{10,... | collective-permute-start | bytes 98312 | tf_op jit(solution)/shard_map/ppermute | solution.py:53
  151.7 23.7 %collective-permute-start.28 = (f32[8192]{0:T(1024)S(1)}, f32[8192]{0:T(1024)S(1)}, u32[]{:S(2)}, u32[]{:S(2)}) collective-permute-start(f32[8192]{0:T(1024)S(1)} %add.365), channel_id=1, source_target_pairs={{0,24},{1,25},{2,26},{3,27},{4,28},{5,29},{6,30},{7,31},{8,16},{9,... | collective-permute-start | bytes 98312 | tf_op jit(solution)/shard_map/ppermute | solution.py:57
  175.4 14.5 %collective-permute-start.29 = (f32[8192]{0:T(1024)S(1)}, f32[8192]{0:T(1024)S(1)}, u32[]{:S(2)}, u32[]{:S(2)}) collective-permute-start(f32[8192]{0:T(1024)S(1)} %add.366), channel_id=1, source_target_pairs={{0,8},{1,9},{2,10},{3,11},{4,12},{5,13},{6,14},{7,15},{8,0},{9,1},... | collective-permute-start | bytes 98312 | tf_op jit(solution)/shard_map/ppermute | solution.py:57
  190.0 7.0 %collective-permute-start.30 = (f32[8192]{0:T(1024)S(1)}, f32[8192]{0:T(1024)S(1)}, u32[]{:S(2)}, u32[]{:S(2)}) collective-permute-start(f32[8192]{0:T(1024)S(1)} %add.367), channel_id=1, source_target_pairs={{0,768},{256,512},{512,256},{768,0},{1,769},{257,513},{513,257},{7... | collective-permute-start | bytes 98312 | tf_op jit(solution)/shard_map/ppermute | solution.py:57
  197.0 5.8 %collective-permute-start.31 = (f32[8192]{0:T(1024)S(1)}, f32[8192]{0:T(1024)S(1)}, u32[]{:S(2)}, u32[]{:S(2)}) collective-permute-start(f32[8192]{0:T(1024)S(1)} %add.368), channel_id=1, source_target_pairs={{0,256},{256,0},{512,768},{768,512},{1,257},{257,1},{513,769},{769... | collective-permute-start | bytes 98312 | tf_op jit(solution)/shard_map/ppermute | solution.py:57
  203.5 0.5 copy-start.12

commit v7 on v6

--- a/solution.py
+++ b/solution.py
@@ -118,13 +118,16 @@
     return own + low_mask * left + high_mask * right
 
 
-def ghost_z(cells, width):
+def ghost_z(arrays, width):
     count = lax.axis_size("gz")
-    head = cells[..., :width]
-    tail = cells[..., cells.shape[-1] - width :]
+    head = jnp.stack([cells[..., :width] for cells in arrays])
+    tail = jnp.stack([cells[..., cells.shape[-1] - width :] for cells in arrays])
     from_prev = lax.ppermute(tail, "gz", [(i, i + 1) for i in range(count - 1)])
     from_next = lax.ppermute(head, "gz", [(i + 1, i) for i in range(count - 1)])
-    return jnp.concatenate([from_prev, cells, from_next], axis=-1)
+    return [
+        jnp.concatenate([from_prev[k], cells, from_next[k]], axis=-1)
+        for k, cells in enumerate(arrays)
+    ]
 
 
 def assemble(field, points):
@@ -142,8 +145,7 @@
     derivative, weights = gll_tables(ORDER)
     size_x, size_y, own_z = right_side.shape
     ghost = 64
-    inputs = ghost_z(jnp.stack([right_side, coefficient]), ghost)
-    right_ext, coefficient = inputs[0], inputs[1]
+    right_ext, coefficient = ghost_z([right_side, coefficient], ghost)
     size_z = own_z + 2 * ghost
     first = lax.axis_index("gz") * own_z - ghost
     global_z = first + jnp.arange(size_z, dtype=jnp.int32)

time: 206 us -> 205 us (level)
    unnamed x32 -> x36, local copies, waits for them, and re-layouts: 6.52 us -> 6.91 us
where the time goes in v7:
time: 205 us; the launch traced here: 204 us
  starting transfers between devices  123 us (60%)
  waiting for transfers between devices  57.2 us (28%)
  local copies, waits for them, and re-layouts  8.96 us (4%)
  matrix products  7.8 us (4%)
  other arithmetic  5.2 us (3%)
    ppermute x6, starting transfers between devices, butterfly_sum(): value = value + lax.ppermute(value, axis, pairs)  48.3 us
    ppermute x10, starting transfers between devices, padded_2(): lax.ppermute(jnp.squeeze(tail, dim), axis, [(i, i + 1) for i in range(end...  30.5 us
    ppermute x10, starting transfers between devices, padded_2(): lax.ppermute(jnp.squeeze(head, dim), axis, [(i + 1, i) for i in range(end...  23.1 us
    ppermute x6, waiting for transfers between devices, butterfly_sum(): value = value + lax.ppermute(value, axis, pairs)  20.1 us
    ppermute x10, waiting for transfers between devices, padded_2(): lax.ppermute(jnp.squeeze(head, dim), axis, [(i + 1, i) for i in range(end...  17.9 us
    ppermute x4, starting transfers between devices, butterfly_sum(): lax.ppermute(value, axis, [(i, i ^ stride) for i in range(count)])  15.5 us
    ppermute x4, waiting for transfers between devices, butterfly_sum(): lax.ppermute(value, axis, [(i, i ^ stride) for i in range(count)])  10.2 us
    unnamed x36, local copies, waits for them, and re-layouts  6.91 us
  transfers between devices with their start and end apart: 32, of which 27 were waited for; matrix products, arithmetic and copies ran while one was open for 1% of the time, Pallas kernels for 0%

profile of v7, /device:TPU:24, one launch (start us, length us, event | category | flops | bytes accessed | tf_op | source)
XLA Modules:
  0.0 204.2 jit_solution(10502207785084453627)
XLA Ops:
  0.7 1.1 copy.188
  1.9 1.3 collective-permute-start.1
  3.2 4.6 %collective-permute-start = (f32[2,8,16,64]{3,1,2,0:T(8,128)S(1)}, f32[2,8,16,64]{3,1,2,0:T(8,128)S(1)}, u32[]{:S(2)}, u32[]{:S(2)}) collective-permute-start(f32[2,8,16,64]{3,1,2,0:T(8,128)S(1)} %pad_maximum_fusion.35), channel_id=1, source_target_pairs={{0,1},{1,2},{2,3},{3,4},{4,5},{5,6},{6,7},{7,8},{8,9},{9,10},{10,1... | collective-permute-start | bytes 196616 | tf_op jit(solution)/shard_map/ppermute | solution.py:125
  7.8 1.4 collective-permute-done.1
  9.3 1.2 collective-permute-done
  10.5 0.6 copy-done.12
  11.3 0.7 copy-done.6
  12.9 0.5 copy-done.11
  13.7 1.9 collective-permute-start.3
  15.6 2.4 %collective-permute-start.2 = (f32[8,386]{1,0:T(8,128)S(1)}, f32[8,386]{1,0:T(8,128)S(1)}, u32[]{:S(2)}, u32[]{:S(2)}) collective-permute-start(f32[8,386]{1,0:T(8,128)S(1)} %get-tuple-element.45), channel_id=1, source_target_pairs={{0,32},{32,64},{64,96},{96,128},{128,160},{160,192},{192,224},{1,3... | collective-permute-start | bytes 37064 | tf_op jit(solution)/shard_map/ppermute | solution.py:33
  18.2 2.4 %collective-permute-done.2 = f32[8,386]{1,0:T(8,128)S(1)} collective-permute-done((f32[8,386]{1,0:T(8,128)S(1)}, f32[8,386]{1,0:T(8,128)S(1)}, u32[]{:S(2)}, u32[]{:S(2)}) %collective-permute-start.2) | collective-permute-done | bytes 12384 | tf_op jit(solution)/shard_map/ppermute | solution.py:33
  20.8 3.4 %collective-permute-start.4 = (f32[18,386]{1,0:T(8,128)S(1)}, f32[18,386]{1,0:T(8,128)S(1)}, u32[]{:S(2)}, u32[]{:S(2)}) collective-permute-start(f32[18,386]{1,0:T(8,128)S(1)} %get-tuple-element.26), channel_id=1, source_target_pairs={{0,256},{256,512},{512,768},{1,257},{257,513},{513,769},{2,258},{2... | collective-permute-start | bytes 83384 | tf_op jit(solution)/shard_map/ppermute | solution.py:33
  24.4 1.3 collective-permute-start.5
  26.1 4.3 %collective-permute-done.5 = f32[18,386]{1,0:T(8,128)S(1)} collective-permute-done((f32[18,386]{1,0:T(8,128)S(1)}, f32[18,386]{1,0:T(8,128)S(1)}, u32[]{:S(2)}, u32[]{:S(2)}) %collective-permute-start.5) | collective-permute-done | bytes 27824 | tf_op jit(solution)/shard_map/ppermute | solution.py:34
  31.0 0.6 copy-done.1
  32.8 0.5 copy-done.2
  34.3 1.9 collective-permute-start.6
  36.2 3.6 %collective-permute-start.7 = (f32[8,386]{1,0:T(8,128)S(1)}, f32[8,386]{1,0:T(8,128)S(1)}, u32[]{:S(2)}, u32[]{:S(2)}) collective-permute-start(f32[8,386]{1,0:T(8,128)S(1)} %get-tuple-element.44), channel_id=1, source_target_pairs={{32,0},{64,32},{96,64},{128,96},{160,128},{192,160},{224,192},{33,... | collective-permute-start | bytes 37064 | tf_op jit(solution)/shard_map/ppermute | solution.py:34
  40.0 1.2 collective-permute-done.7
  41.4 3.4 %collective-permute-start.8 = (f32[18,386]{1,0:T(8,128)S(1)}, f32[18,386]{1,0:T(8,128)S(1)}, u32[]{:S(2)}, u32[]{:S(2)}) collective-permute-start(f32[18,386]{1,0:T(8,128)S(1)} %get-tuple-element.24), channel_id=1, source_target_pairs={{0,256},{256,512},{512,768},{1,257},{257,513},{513,769},{2,258},{2... | collective-permute-start | bytes 83384 | tf_op jit(solution)/shard_map/ppermute | solution.py:33
  44.8 1.3 collective-permute-start.9
  46.5 4.3 %collective-permute-done.9 = f32[18,386]{1,0:T(8,128)S(1)} collective-permute-done((f32[18,386]{1,0:T(8,128)S(1)}, f32[18,386]{1,0:T(8,128)S(1)}, u32[]{:S(2)}, u32[]{:S(2)}) %collective-permute-start.9) | collective-permute-done | bytes 27824 | tf_op jit(solution)/shard_map/ppermute | solution.py:34
  53.3 1.9 collective-permute-start.10
  55.2 3.6 %collective-permute-start.11 = (f32[8,386]{1,0:T(8,128)S(1)}, f32[8,386]{1,0:T(8,128)S(1)}, u32[]{:S(2)}, u32[]{:S(2)}) collective-permute-start(f32[8,386]{1,0:T(8,128)S(1)} %get-tuple-element.42), channel_id=1, source_target_pairs={{32,0},{64,32},{96,64},{128,96},{160,128},{192,160},{224,192},{33,... | collective-permute-start | bytes 37064 | tf_op jit(solution)/shard_map/ppermute | solution.py:34
  59.1 1.2 collective-permute-done.11
  60.4 1.3 collective-permute-start.13
  61.7 4.5 %collective-permute-start.12 = (f32[18,386]{1,0:T(8,128)S(1)}, f32[18,386]{1,0:T(8,128)S(1)}, u32[]{:S(2)}, u32[]{:S(2)}) collective-permute-start(f32[18,386]{1,0:T(8,128)S(1)} %get-tuple-element.22), channel_id=1, source_target_pairs={{0,256},{256,512},{512,768},{1,257},{257,513},{513,769},{2,258},{2... | collective-permute-start | bytes 83384 | tf_op jit(solution)/shard_map/ppermute | solution.py:33
  66.4 1.6 collective-permute-done.12
  70.6 1.9 collective-permute-start.14
  72.5 3.6 %collective-permute-start.15 = (f32[8,386]{1,0:T(8,128)S(1)}, f32[8,386]{1,0:T(8,128)S(1)}, u32[]{:S(2)}, u32[]{:S(2)}) collective-permute-start(f32[8,386]{1,0:T(8,128)S(1)} %get-tuple-element.40), channel_id=1, source_target_pairs={{32,0},{64,32},{96,64},{128,96},{160,128},{192,160},{224,192},{33,... | collective-permute-start | bytes 37064 | tf_op jit(solution)/shard_map/ppermute | solution.py:34
  76.4 1.2 collective-permute-done.15
  77.7 1.3 collective-permute-start.17
  79.0 4.9 %collective-permute-start.16 = (f32[18,386]{1,0:T(8,128)S(1)}, f32[18,386]{1,0:T(8,128)S(1)}, u32[]{:S(2)}, u32[]{:S(2)}) collective-permute-start(f32[18,386]{1,0:T(8,128)S(1)} %get-tuple-element.19), channel_id=1, source_target_pairs={{0,256},{256,512},{512,768},{1,257},{257,513},{513,769},{2,258},{2... | collective-permute-start | bytes 83384 | tf_op jit(solution)/shard_map/ppermute | solution.py:33
  84.0 1.6 collective-permute-done.16
  88.1 1.9 collective-permute-start.18
  90.0 3.6 %collective-permute-start.19 = (f32[8,386]{1,0:T(8,128)S(1)}, f32[8,386]{1,0:T(8,128)S(1)}, u32[]{:S(2)}, u32[]{:S(2)}) collective-permute-start(f32[8,386]{1,0:T(8,128)S(1)} %get-tuple-element.38), channel_id=1, source_target_pairs={{32,0},{64,32},{96,64},{128,96},{160,128},{192,160},{224,192},{33,... | collective-permute-start | bytes 37064 | tf_op jit(solution)/shard_map/ppermute | solution.py:34
  93.9 1.2 collective-permute-done.19
  95.2 4.2 %collective-permute-start.20 = (f32[18,386]{1,0:T(8,128)S(1)}, f32[18,386]{1,0:T(8,128)S(1)}, u32[]{:S(2)}, u32[]{:S(2)}) collective-permute-start(f32[18,386]{1,0:T(8,128)S(1)} %get-tuple-element.16), channel_id=1, source_target_pairs={{0,256},{256,512},{512,768},{1,257},{257,513},{513,769},{2,258},{2... | collective-permute-start | bytes 83384 | tf_op jit(solution)/shard_map/ppermute | solution.py:33
  99.4 1.5 collective-permute-start.21
  101.2 4.3 %collective-permute-done.21 = f32[18,386]{1,0:T(8,128)S(1)} collective-permute-done((f32[18,386]{1,0:T(8,128)S(1)}, f32[18,386]{1,0:T(8,128)S(1)}, u32[]{:S(2)}, u32[]{:S(2)}) %collective-permute-start.21) | collective-permute-done | bytes 27824 | tf_op jit(solution)/shard_map/ppermute | solution.py:34
  106.2 0.7 copy-done.3
  107.7 1.9 collective-permute-start.22
  109.7 1.2 collective-permute-done.22
  110.8 9.7 %collective-permute-start.23 = (f32[8192]{0:T(1024)S(1)}, f32[8192]{0:T(1024)S(1)}, u32[]{:S(2)}, u32[]{:S(2)}) collective-permute-start(f32[8192]{0:T(1024)S(1)} %add.360), channel_id=1, source_target_pairs={{0,192},{32,224},{64,128},{96,160},{128,64},{160,96},{192,0},{224,... | collective-permute-start | bytes 98312 | tf_op jit(solution)/shard_map/ppermute | solution.py:57
  120.5 1.9 collective-permute-done.23
  122.4 2.7 %collective-permute-start.24 = (f32[8192]{0:T(1024)S(1)}, f32[8192]{0:T(1024)S(1)}, u32[]{:S(2)}, u32[]{:S(2)}) collective-permute-start(f32[8192]{0:T(1024)S(1)} %add.361), channel_id=1, source_target_pairs={{0,64},{32,96},{64,0},{96,32},{128,192},{160,224},{192,128},{224,1... | collective-permute-start | bytes 98312 | tf_op jit(solution)/shard_map/ppermute | solution.py:57
  125.1 3.1 %collective-permute-done.24 = f32[8192]{0:T(1024)S(1)} collective-permute-done((f32[8192]{0:T(1024)S(1)}, f32[8192]{0:T(1024)S(1)}, u32[]{:S(2)}, u32[]{:S(2)}) %collective-permute-start.24) | collective-permute-done | bytes 32800 | tf_op jit(solution)/shard_map/ppermute | solution.py:57
  128.2 4.3 %collective-permute-start.25 = (f32[8192]{0:T(1024)S(1)}, f32[8192]{0:T(1024)S(1)}, u32[]{:S(2)}, u32[]{:S(2)}) collective-permute-start(f32[8192]{0:T(1024)S(1)} %add.362), channel_id=1, source_target_pairs={{0,1},{1,0},{2,3},{3,2},{4,5},{5,4},{6,7},{7,6},{8,9},{9,8},{10,11... | collective-permute-start | bytes 98312 | tf_op jit(solution)/shard_map/ppermute | solution.py:53
  132.6 1.9 collective-permute-done.25
  134.5 3.4 %collective-permute-start.26 = (f32[8192]{0:T(1024)S(1)}, f32[8192]{0:T(1024)S(1)}, u32[]{:S(2)}, u32[]{:S(2)}) collective-permute-start(f32[8192]{0:T(1024)S(1)} %add.363), channel_id=1, source_target_pairs={{0,2},{1,3},{2,0},{3,1},{4,6},{5,7},{6,4},{7,5},{8,10},{9,11},{10,... | collective-permute-start | bytes 98312 | tf_op jit(solution)/shard_map/ppermute | solution.py:53
  137.8 3.3 %collective-permute-done.26 = f32[8192]{0:T(1024)S(1)} collective-permute-done((f32[8192]{0:T(1024)S(1)}, f32[8192]{0:T(1024)S(1)}, u32[]{:S(2)}, u32[]{:S(2)}) %collective-permute-start.26) | collective-permute-done | bytes 32800 | tf_op jit(solution)/shard_map/ppermute | solution.py:53
  141.2 5.9 %collective-permute-start.27 = (f32[8192]{0:T(1024)S(1)}, f32[8192]{0:T(1024)S(1)}, u32[]{:S(2)}, u32[]{:S(2)}) collective-permute-start(f32[8192]{0:T(1024)S(1)} %add.364), channel_id=1, source_target_pairs={{0,4},{1,5},{2,6},{3,7},{4,0},{5,1},{6,2},{7,3},{8,12},{9,13},{10,... | collective-permute-start | bytes 98312 | tf_op jit(solution)/shard_map/ppermute | solution.py:53
  147.0 3.8 %collective-permute-done.27 = f32[8192]{0:T(1024)S(1)} collective-permute-done((f32[8192]{0:T(1024)S(1)}, f32[8192]{0:T(1024)S(1)}, u32[]{:S(2)}, u32[]{:S(2)}) %collective-permute-start.27) | collective-permute-done | bytes 32800 | tf_op jit(solution)/shard_map/ppermute | solution.py:53
  150.9 21.8 %collective-permute-start.28 = (f32[8192]{0:T(1024)S(1)}, f32[8192]{0:T(1024)S(1)}, u32[]{:S(2)}, u32[]{:S(2)}) collective-permute-start(f32[8192]{0:T(1024)S(1)} %add.365), channel_id=1, source_target_pairs={{0,24},{1,25},{2,26},{3,27},{4,28},{5,29},{6,30},{7,31},{8,16},{9,... | collective-permute-start | bytes 98312 | tf_op jit(solution)/shard_map/ppermute | solution.py:57
  172.7 1.9 collective-permute-done.28
  174.6 8.0 %collective-permute-start.29 = (f32[8192]{0:T(1024)S(1)}, f32[8192]{0:T(1024)S(1)}, u32[]{:S(2)}, u32[]{:S(2)}) collective-permute-start(f32[8192]{0:T(1024)S(1)} %add.366), channel_id=1, source_target_pairs={{0,8},{1,9},{2,10},{3,11},{4,12},{5,13},{6,14},{7,15},{8,0},{9,1},... | collective-permute-start | bytes 98312 | tf_op jit(solution)/shard_map/ppermute | solution.py:57
  182.7 6.5 %collective-permute-done.29 = f32[8192]{0:T(1024)S(1)} collective-permute-done((f32[8192]{0:T(1024)S(1)}, f32[8192]{0:T(1024)S(1)}, u32[]{:S(2)}, u32[]{:S(2)}) %collective-permute-start.29) | collective-permute-done | bytes 32800 | tf_op jit(solution)/shard_map/ppermute | solution.py:57
  189.2 3.4 %collective-permute-start.30 = (f32[8192]{0:T(1024)S(1)}, f32[8192]{0:T(1024)S(1)}, u32[]{:S(2)}, u32[]{:S(2)}) collective-permute-start(f32[8192]{0:T(1024)S(1)} %add.367), channel_id=1, source_target_pairs={{0,768},{256,512},{512,256},{768,0},{1,769},{257,513},{513,257},{7... | collective-permute-start | bytes 98312 | tf_op jit(solution)/shard_map/ppermute | solution.py:57
  192.5 3.6 %collective-permute-done.30 = f32[8192]{0:T(1024)S(1)} collective-permute-done((f32[8192]{0:T(1024)S(1)}, f32[8192]{0:T(1024)S(1)}, u32[]{:S(2)}, u32[]{:S(2)}) %collective-permute-start.30) | collective-permute-done | bytes 32800 | tf_op jit(solution)/shard_map/ppermute | solution.py:57
  196.2 2.7 %collective-permute-start.31 = (f32[8192]{0:T(1024)S(1)}, f32[8192]{0:T(1024)S(1)}, u32[]{:S(2)}, u32[]{:S(2)}) collective-permute-start(f32[8192]{0:T(1024)S(1)} %add.368), channel_id=1, source_target_pairs={{0,256},{256,0},{512,768},{768,512},{1,257},{257,1},{513,769},{769... | collective-permute-start | bytes 98312 | tf_op jit(solution)/shard_map/ppermute | solution.py:57
  198.9 3.1 %collective-permute-done.31 = f32[8192]{0:T(1024)S(1)} collective-permute-done((f32[8192]{0:T(1024)S(1)}, f32[8192]{0:T(1024)S(1)}, u32[]{:S(2)}, u32[]{:S(2)}) %collective-permute-start.31) | collective-permute-done | bytes 32800 | tf_op jit(solution)/shard_map/ppermute | solution.py:57
  202.0 0.7 convolution_bitcast_fusion.5
  202.7 0.5 copy-done.13
  203.5 0.7 copy.256
  (150 shorter events, 16.5 us)
Async XLA Ops:
  0.6 106.7 %copy-start = (f32[8,8192]{1,0:T(8,128)S(1)}, f32[8,8192]{1,0:T(8,128)}, u32[]{:S(2)}) copy-start(f32[8,8192]{1,0:T(8,128)} %param.13) | copy-start | bytes 786436
  0.6 1.1 copy-start.5
  1.9 7.3 %collective-permute-start.1 = (f32[2,8,16,64]{3,1,2,0:T(8,128)S(1)}, f32[2,8,16,64]{3,1,2,0:T(8,128)S(1)}, u32[]{:S(2)}, u32[]{:S(2)}) collective-permute-start(f32[2,8,16,64]{3,1,2,0:T(8,128)S(1)} %pad_maximum_fusion.36), channel_id=1, source_target_pairs={{1,0},{2,1},{3,2},{4,3},{5,4},{6,5},{7,6},{8,7},{9,8},{10,9},{11,1... | collective-permute-start | bytes 196616 | tf_op jit(solution)/shard_map/ppermute | solution.py:126
  3.2 7.2 %collective-permute-start = (f32[2,8,16,64]{3,1,2,0:T(8,128)S(1)}, f32[2,8,16,64]{3,1,2,0:T(8,128)S(1)}, u32[]{:S(2)}, u32[]{:S(2)}) collective-permute-start(f32[2,8,16,64]{3,1,2,0:T(8,128)S(1)} %pad_maximum_fusion.35), channel_id=1, source_target_pairs={{0,1},{1,2},{2,3},{3,4},{4,5},{5,6},{6,7},{7,8},{8,9},{9,10},{10,1... | collective-permute-start | bytes 196616 | tf_op jit(solution)/shard_map/ppermute | solution.py:125
  10.5 0.7 copy-start.12
  10.5 0.7 copy-start.8
  10.5 0.7 copy-start.9
  11.1 0.8 copy-start.6
  11.1 0.8 copy-start.7
  12.0 0.7 copy-start.10
  12.7 0.7 copy-start.11
  13.7 7.0 %collective-permute-start.3 = (f32[8,386]{1,0:T(8,128)S(1)}, f32[8,386]{1,0:T(8,128)S(1)}, u32[]{:S(2)}, u32[]{:S(2)}) collective-permute-start(f32[8,386]{1,0:T(8,128)S(1)} %get-tuple-element.46), channel_id=1, source_target_pairs={{32,0},{64,32},{96,64},{128,96},{160,128},{192,160},{224,192},{33,... | collective-permute-start | bytes 37064 | tf_op jit(solution)/shard_map/ppermute | solution.py:34
  15.6 5.1 %collective-permute-start.2 = (f32[8,386]{1,0:T(8,128)S(1)}, f32[8,386]{1,0:T(8,128)S(1)}, u32[]{:S(2)}, u32[]{:S(2)}) collective-permute-start(f32[8,386]{1,0:T(8,128)S(1)} %get-tuple-element.45), channel_id=1, source_target_pairs={{0,32},{32,64},{64,96},{96,128},{128,160},{160,192},{192,224},{1,3... | collective-permute-start | bytes 37064 | tf_op jit(solution)/shard_map/ppermute | solution.py:33
  20.8 5.1 %collective-permute-start.4 = (f32[18,386]{1,0:T(8,128)S(1)}, f32[18,386]{1,0:T(8,128)S(1)}, u32[]{:S(2)}, u32[]{:S(2)}) collective-permute-start(f32[18,386]{1,0:T(8,128)S(1)} %get-tuple-element.26), channel_id=1, source_target_pairs={{0,256},{256,512},{512,768},{1,257},{257,513},{513,769},{2,258},{2... | collective-permute-start | bytes 83384 | tf_op jit(solution)/shard_map/ppermute | solution.py:33
  24.4 6.0 %collective-permute-start.5 = (f32[18,386]{1,0:T(8,128)S(1)}, f32[18,386]{1,0:T(8,128)S(1)}, u32[]{:S(2)}, u32[]{:S(2)}) collective-permute-start(f32[18,386]{1,0:T(8,128)S(1)} %get-tuple-element.27), channel_id=1, source_target_pairs={{256,0},{512,256},{768,512},{257,1},{513,257},{769,513},{258,2},{5... | collective-permute-start | bytes 83384 | tf_op jit(solution)/shard_map/ppermute | solution.py:34
  30.8 0.8 copy-start.1
  31.9 0.7 copy-start.4
  32.6 0.7 copy-start.2
  34.3 5.8 %collective-permute-start.6 = (f32[8,386]{1,0:T(8,128)S(1)}, f32[8,386]{1,0:T(8,128)S(1)}, u32[]{:S(2)}, u32[]{:S(2)}) collective-permute-start(f32[8,386]{1,0:T(8,128)S(1)} %get-tuple-element.43), channel_id=1, source_target_pairs={{0,32},{32,64},{64,96},{96,128},{128,160},{160,192},{192,224},{1,3... | collective-permute-start | bytes 37064 | tf_op jit(solution)/shard_map/ppermute | solution.py:33
  36.2 5.1 %collective-permute-start.7 = (f32[8,386]{1,0:T(8,128)S(1)}, f32[8,386]{1,0:T(8,128)S(1)}, u32[]{:S(2)}, u32[]{:S(2)}) collective-permute-start(f32[8,386]{1,0:T(8,128)S(1)} %get-tuple-element.44), channel_id=1, source_target_pairs={{32,0},{64,32},{96,64},{128,96},{160,128},{192,160},{224,192},{33,... | collective-permute-start | bytes 37064 | tf_op jit(solution)/shard_map/ppermute | solution.py:34
  41.4 5.1 %collective-permute-start.8 = (f32[18,386]{1,0:T(8,128)S(1)}, f32[18,386]{1,0:T(8,128)S(1)}, u32[]{:S(2)}, u32[]{:S(2)}) collective-permute-start(f32[18,386]{1,0:T(8,128)S(1)} %get-tuple-element.24), channel_id=1, source_target_pairs={{0,256},{256,512},{512,768},{1,257},{257,513},{513,769},{2,258},{2... | collective-permute-start | bytes 83384 | tf_op jit(solution)/shard_map/ppermute | solution.py:33
  44.8 6.0 %collective-permute-start.9 = (f32[18,386]{1,0:T(8,128)S(1)}, f32[18,386]{1,0:T(8,128)S(1)}, u32[]{:S(2)}, u32[]{:S(2)}) collective-permute-start(f32[18,386]{1,0:T(8,128)S(1)} %get-tuple-element.25), channel_id=1, source_target_pairs={{256,0},{512,256},{768,512},{257,1},{513,257},{769,513},{258,2},{5... | collective-permute-start | bytes 83384 | tf_op jit(solution)/shard_map/ppermute | solution.py:34
  53.3 5.8 %collective-permute-start.10 = (f32[8,386]{1,0:T(8,128)S(1)}, f32[8,386]{1,0:T(8,128)S(1)}, u32[]{:S(2)}, u32[]{:S(2)}) collective-permute-start(f32[8,386]{1,0:T(8,128)S(1)} %get-tuple-element.41), channel_id=1, source_target_pairs={{0,32},{32,64},{64,96},{96,128},{128,160},{160,192},{192,224},{1,3... | collective-permute-start | bytes 37064 | tf_op jit(solution)/shard_map/ppermute | solution.py:33
  55.2 5.1 %collective-permute-start.11 = (f32[8,386]{1,0:T(8,128)S(1)}, f32[8,386]{1,0:T(8,128)S(1)}, u32[]{:S(2)}, u32[]{:S(2)}) collective-permute-start(f32[8,386]{1,0:T(8,128)S(1)} %get-tuple-element.42), channel_id=1, source_target_pairs={{32,0},{64,32},{96,64},{128,96},{160,128},{192,160},{224,192},{33,... | collective-permute-start | bytes 37064 | tf_op jit(solution)/shard_map/ppermute | solution.py:34
  60.4 6.0 %collective-permute-start.13 = (f32[18,386]{1,0:T(8,128)S(1)}, f32[18,386]{1,0:T(8,128)S(1)}, u32[]{:S(2)}, u32[]{:S(2)}) collective-permute-start(f32[18,386]{1,0:T(8,128)S(1)} %get-tuple-element.23), channel_id=1, source_target_pairs={{256,0},{512,256},{768,512},{257,1},{513,257},{769,513},{258,2},{5... | collective-permute-start | bytes 83384 | tf_op jit(solution)/shard_map/ppermute | solution.py:34
  61.7 6.3 %collective-permute-start.12 = (f32[18,386]{1,0:T(8,128)S(1)}, f32[18,386]{1,0:T(8,128)S(1)}, u32[]{:S(2)}, u32[]{:S(2)}) collective-permute-start(f32[18,386]{1,0:T(8,128)S(1)} %get-tuple-element.22), channel_id=1, source_target_pairs={{0,256},{256,512},{512,768},{1,257},{257,513},{513,769},{2,258},{2... | collective-permute-start | bytes 83384 | tf_op jit(solution)/shard_map/ppermute | solution.py:33
  70.6 5.8 %collective-permute-start.14 = (f32[8,386]{1,0:T(8,128)S(1)}, f32[8,386]{1,0:T(8,128)S(1)}, u32[]{:S(2)}, u32[]{:S(2)}) collective-permute-start(f32[8,386]{1,0:T(8,128)S(1)} %get-tuple-element.39), channel_id=1, source_target_pairs={{0,32},{32,64},{64,96},{96,128},{128,160},{160,192},{192,224},{1,3... | collective-permute-start | bytes 37064 | tf_op jit(solution)/shard_map/ppermute | solution.py:33
  72.5 5.1 %collective-permute-start.15 = (f32[8,386]{1,0:T(8,128)S(1)}, f32[8,386]{1,0:T(8,128)S(1)}, u32[]{:S(2)}, u32[]{:S(2)}) collective-permute-start(f32[8,386]{1,0:T(8,128)S(1)} %get-tuple-element.40), channel_id=1, source_target_pairs={{32,0},{64,32},{96,64},{128,96},{160,128},{192,160},{224,192},{33,... | collective-permute-start | bytes 37064 | tf_op jit(solution)/shard_map/ppermute | solution.py:34
  77.7 6.3 %collective-permute-start.17 = (f32[18,386]{1,0:T(8,128)S(1)}, f32[18,386]{1,0:T(8,128)S(1)}, u32[]{:S(2)}, u32[]{:S(2)}) collective-permute-start(f32[18,386]{1,0:T(8,128)S(1)} %get-tuple-element.18), channel_id=1, source_target_pairs={{256,0},{512,256},{768,512},{257,1},{513,257},{769,513},{258,2},{5... | collective-permute-start | bytes 83384 | tf_op jit(solution)/shard_map/ppermute | solution.py:34
  79.0 6.6 %collective-permute-start.16 = (f32[18,386]{1,0:T(8,128)S(1)}, f32[18,386]{1,0:T(8,128)S(1)}, u32[]{:S(2)}, u32[]{:S(2)}) collective-permute-start(f32[18,386]{1,0:T(8,128)S(1)} %get-tuple-element.19), channel_id=1, source_target_pairs={{0,256},{256,512},{512,768},{1,257},{257,513},{513,769},{2,258},{2... | collective-permute-start | bytes 83384 | tf_op jit(solution)/shard_map/ppermute | solution.py:33
  88.1 5.8 %collective-permute-start.18 = (f32[8,386]{1,0:T(8,128)S(1)}, f32[8,386]{1,0:T(8,128)S(1)}, u32[]{:S(2)}, u32[]{:S(2)}) collective-permute-start(f32[8,386]{1,0:T(8,128)S(1)} %get-tuple-element.37), channel_id=1, source_target_pairs={{0,32},{32,64},{64,96},{96,128},{128,160},{160,192},{192,224},{1,3... | collective-permute-start | bytes 37064 | tf_op jit(solution)/shard_map/ppermute | solution.py:33
  90.0 5.1 %collective-permute-start.19 = (f32[8,386]{1,0:T(8,128)S(1)}, f32[8,386]{1,0:T(8,128)S(1)}, u32[]{:S(2)}, u32[]{:S(2)}) collective-permute-start(f32[8,386]{1,0:T(8,128)S(1)} %get-tuple-element.38), channel_id=1, source_target_pairs={{32,0},{64,32},{96,64},{128,96},{160,128},{192,160},{224,192},{33,... | collective-permute-start | bytes 37064 | tf_op jit(solution)/shard_map/ppermute | solution.py:34
  95.2 6.0 %collective-permute-start.20 = (f32[18,386]{1,0:T(8,128)S(1)}, f32[18,386]{1,0:T(8,128)S(1)}, u32[]{:S(2)}, u32[]{:S(2)}) collective-permute-start(f32[18,386]{1,0:T(8,128)S(1)} %get-tuple-element.16), channel_id=1, source_target_pairs={{0,256},{256,512},{512,768},{1,257},{257,513},{513,769},{2,258},{2... | collective-permute-start | bytes 83384 | tf_op jit(solution)/shard_map/ppermute | solution.py:33
  99.4 6.0 %collective-permute-start.21 = (f32[18,386]{1,0:T(8,128)S(1)}, f32[18,386]{1,0:T(8,128)S(1)}, u32[]{:S(2)}, u32[]{:S(2)}) collective-permute-start(f32[18,386]{1,0:T(8,128)S(1)} %get-tuple-element.17), channel_id=1, source_target_pairs={{256,0},{512,256},{768,512},{257,1},{513,257},{769,513},{258,2},{5... | collective-permute-start | bytes 83384 | tf_op jit(solution)/shard_map/ppermute | solution.py:34
  106.0 0.9 copy-start.3
  107.7 3.1 %collective-permute-start.22 = (f32[8192]{0:T(1024)S(1)}, f32[8192]{0:T(1024)S(1)}, u32[]{:S(2)}, u32[]{:S(2)}) collective-permute-start(f32[8192]{0:T(1024)S(1)} %bitcast.193), channel_id=1, source_target_pairs={{0,32},{32,0},{64,96},{96,64},{128,160},{160,128},{192,224},{224,1... | collective-permute-start | bytes 98312 | tf_op jit(solution)/shard_map/ppermute | solution.py:53
  110.8 11.6 %collective-permute-start.23 = (f32[8192]{0:T(1024)S(1)}, f32[8192]{0:T(1024)S(1)}, u32[]{:S(2)}, u32[]{:S(2)}) collective-permute-start(f32[8192]{0:T(1024)S(1)} %add.360), channel_id=1, source_target_pairs={{0,192},{32,224},{64,128},{96,160},{128,64},{160,96},{192,0},{224,... | collective-permute-start | bytes 98312 | tf_op jit(solution)/shard_map/ppermute | solution.py:57
  122.4 5.8 %collective-permute-start.24 = (f32[8192]{0:T(1024)S(1)}, f32[8192]{0:T(1024)S(1)}, u32[]{:S(2)}, u32[]{:S(2)}) collective-permute-start(f32[8192]{0:T(1024)S(1)} %add.361), channel_id=1, source_target_pairs={{0,64},{32,96},{64,0},{96,32},{128,192},{160,224},{192,128},{224,1... | collective-permute-start | bytes 98312 | tf_op jit(solution)/shard_map/ppermute | solution.py:57
  128.2 6.2 %collective-permute-start.25 = (f32[8192]{0:T(1024)S(1)}, f32[8192]{0:T(1024)S(1)}, u32[]{:S(2)}, u32[]{:S(2)}) collective-permute-start(f32[8192]{0:T(1024)S(1)} %add.362), channel_id=1, source_target_pairs={{0,1},{1,0},{2,3},{3,2},{4,5},{5,4},{6,7},{7,6},{8,9},{9,8},{10,11... | collective-permute-start | bytes 98312 | tf_op jit(solution)/shard_map/ppermute | solution.py:53
  134.5 6.7 %collective-permute-start.26 = (f32[8192]{0:T(1024)S(1)}, f32[8192]{0:T(1024)S(1)}, u32[]{:S(2)}, u32[]{:S(2)}) collective-permute-start(f32[8192]{0:T(1024)S(1)} %add.363), channel_id=1, source_target_pairs={{0,2},{1,3},{2,0},{3,1},{4,6},{5,7},{6,4},{7,5},{8,10},{9,11},{10,... | collective-permute-start | bytes 98312 | tf_op jit(solution)/shard_map/ppermute | solution.py:53
  141.2 9.7 %collective-permute-start.27 = (f32[8192]{0:T(1024)S(1)}, f32[8192]{0:T(1024)S(1)}, u32[]{:S(2)}, u32[]{:S(2)}) collective-permute-start(f32[8192]{0:T(1024)S(1)} %add.364), channel_id=1, source_target_pairs={{0,4},{1,5},{2,6},{3,7},{4,0},{5,1},{6,2},{7,3},{8,12},{9,13},{10,... | collective-permute-start | bytes 98312 | tf_op jit(solution)/shard_map/ppermute | solution.py:53
  150.9 23.7 %collective-permute-start.28 = (f32[8192]{0:T(1024)S(1)}, f32[8192]{0:T(1024)S(1)}, u32[]{:S(2)}, u32[]{:S(2)}) collective-permute-start(f32[8192]{0:T(1024)S(1)} %add.365), channel_id=1, source_target_pairs={{0,24},{1,25},{2,26},{3,27},{4,28},{5,29},{6,30},{7,31},{8,16},{9,... | collective-permute-start | bytes 98312 | tf_op jit(solution)/shard_map/ppermute | solution.py:57
  174.6 14.5 %collective-permute-start.29 = (f32[8192]{0:T(1024)S(1)}, f32[8192]{0:T(1024)S(1)}, u32[]{:S(2)}, u32[]{:S(2)}) collective-permute-start(f32[8192]{0:T(1024)S(1)} %add.366), channel_id=1, source_target_pairs={{0,8},{1,9},{2,10},{3,11},{4,12},{5,13},{6,14},{7,15},{8,0},{9,1},... | collective-permute-start | bytes 98312 | tf_op jit(solution)/shard_map/ppermute | solution.py:57
  189.2 7.0 %collective-permute-start.30 = (f32[8192]{0:T(1024)S(1)}, f32[8192]{0:T(1024)S(1)}, u32[]{:S(2)}, u32[]{:S(2)}) collective-permute-start(f32[8192]{0:T(1024)S(1)} %add.367), channel_id=1, source_target_pairs={{0,768},{256,512},{512,256},{768,0},{1,769},{257,513},{513,257},{7... | collective-permute-start | bytes 98312 | tf_op jit(solution)/shard_map/ppermute | solution.py:57
  196.2 5.8 %collective-permute-start.31 = (f32[8192]{0:T(1024)S(1)}, f32[8192]{0:T(1024)S(1)}, u32[]{:S(2)}, u32[]{:S(2)}) collective-permute-start(f32[8192]{0:T(1024)S(1)} %add.368), channel_id=1, source_target_pairs={{0,256},{256,0},{512,768},{768,512},{1,257},{257,1},{513,769},{769... | collective-permute-start | bytes 98312 | tf_op jit(solution)/shard_map/ppermute | solution.py:57
  202.7 0.5 copy-start.13

commit v8 on v7

--- a/solution.py
+++ b/solution.py
@@ -133,7 +133,7 @@
 def assemble(field, points):
     size_x, size_y, size_z = field.shape
     padded = jnp.pad(field, ((0, 0), (0, 0), (1, 1)))
-    padded = padded_2(padded, (("gy", 1), ("gx", 0)), 1)
+    padded = padded_2(padded, (("gx", 0), ("gy", 1)), 1)
     summed = combine(padded, 0, size_x, points)
     summed = combine(summed, 1, size_y, points)
     summed = combine(summed, 2, size_z, points)

time: 205 us -> 202 us (0.985)
  starting transfers between devices: 123 us -> 113 us
  waiting for transfers between devices: 57.2 us -> 63.8 us
    ppermute x10, waiting for transfers between devices: 17.9 us -> 28.7 us  [padded_2(): lax.ppermute(jnp.squeeze(head, dim), axis, [(i + 1, i) for i in range(end...]
    ppermute x6, starting transfers between devices: 48.3 us -> 38.1 us  [butterfly_sum(): value = value + lax.ppermute(value, axis, pairs)]
    ppermute x10, starting transfers between devices: 30.5 us -> 23.3 us  [padded_2(): lax.ppermute(jnp.squeeze(tail, dim), axis, [(i, i + 1) for i in range(end...]
    ppermute x4, starting transfers between devices: 15.5 us -> 22.1 us  [butterfly_sum(): lax.ppermute(value, axis, [(i, i ^ stride) for i in range(count)])]
    ppermute x10, waiting for transfers between devices: 6.44 us -> 0.41 us  [padded_2(): lax.ppermute(jnp.squeeze(tail, dim), axis, [(i, i + 1) for i in range(end...]
    ppermute x4, waiting for transfers between devices: 10.2 us -> 6.9 us  [butterfly_sum(): lax.ppermute(value, axis, [(i, i ^ stride) for i in range(count)])]
    ppermute x1, waiting for transfers between devices: 1.4 us -> 4.31 us  [ghost_z(): from_next = lax.ppermute(head, 'gz', [(i + 1, i) for i in range(count - 1)])]
    unnamed x36 -> x37, local copies, waits for them, and re-layouts: 6.91 us -> 7.08 us
where the time goes in v8:
time: 202 us; the launch traced here: 200 us
  starting transfers between devices  113 us (56%)
  waiting for transfers between devices  63.8 us (32%)
  local copies, waits for them, and re-layouts  9.84 us (5%)
  matrix products  7.79 us (4%)
  other arithmetic  3.93 us (2%)
    ppermute x6, starting transfers between devices, butterfly_sum(): value = value + lax.ppermute(value, axis, pairs)  38.1 us
    ppermute x10, waiting for transfers between devices, padded_2(): lax.ppermute(jnp.squeeze(head, dim), axis, [(i + 1, i) for i in range(end...  28.7 us
    ppermute x10, starting transfers between devices, padded_2(): lax.ppermute(jnp.squeeze(head, dim), axis, [(i + 1, i) for i in range(end...  24.7 us
    ppermute x10, starting transfers between devices, padded_2(): lax.ppermute(jnp.squeeze(tail, dim), axis, [(i, i + 1) for i in range(end...  23.3 us
    ppermute x4, starting transfers between devices, butterfly_sum(): lax.ppermute(value, axis, [(i, i ^ stride) for i in range(count)])  22.1 us
    ppermute x6, waiting for transfers between devices, butterfly_sum(): value = value + lax.ppermute(value, axis, pairs)  22.1 us
    unnamed x37, local copies, waits for them, and re-layouts  7.08 us
    ppermute x4, waiting for transfers between devices, butterfly_sum(): lax.ppermute(value, axis, [(i, i ^ stride) for i in range(count)])  6.9 us
  transfers between devices with their start and end apart: 32, of which 27 were waited for; matrix products, arithmetic and copies ran while one was open for 1% of the time, Pallas kernels for 0%

profile of v8, /device:TPU:24, one launch (start us, length us, event | category | flops | bytes accessed | tf_op | source)
XLA Modules:
  0.0 200.5 jit_solution(17047089760974597029)
XLA Ops:
  0.7 1.1 copy.89
  1.9 3.8 %collective-permute-start = (f32[2,8,16,64]{3,1,2,0:T(8,128)S(1)}, f32[2,8,16,64]{3,1,2,0:T(8,128)S(1)}, u32[]{:S(2)}, u32[]{:S(2)}) collective-permute-start(f32[2,8,16,64]{3,1,2,0:T(8,128)S(1)} %pad_maximum_fusion.7), channel_id=1, source_target_pairs={{0,1},{1,2},{2,3},{3,4},{4,5},{5,6},{6,7},{7,8},{8,9},{9,10},{10,1... | collective-permute-start | bytes 196616 | tf_op jit(solution)/shard_map/ppermute | solution.py:125
  5.8 1.3 collective-permute-start.1
  7.1 1.4 collective-permute-done
  8.5 4.3 %collective-permute-done.1 = f32[2,8,16,64]{3,1,2,0:T(8,128)S(1)} collective-permute-done((f32[2,8,16,64]{3,1,2,0:T(8,128)S(1)}, f32[2,8,16,64]{3,1,2,0:T(8,128)S(1)}, u32[]{:S(2)}, u32[]{:S(2)}) %collective-permute-start.1) | collective-permute-done | bytes 65568 | tf_op jit(solution)/shard_map/ppermute | solution.py:126
  12.9 0.6 copy-done.12
  13.7 0.5 copy-done.10
  14.4 0.6 copy-done.6
  16.2 3.4 %collective-permute-start.2 = (f32[16,386]{1,0:T(8,128)S(1)}, f32[16,386]{1,0:T(8,128)S(1)}, u32[]{:S(2)}, u32[]{:S(2)}) collective-permute-start(f32[16,386]{1,0:T(8,128)S(1)} %bitcast.216), channel_id=1, source_target_pairs={{0,256},{256,512},{512,768},{1,257},{257,513},{513,769},{2,258},{2... | collective-permute-start | bytes 74120 | tf_op jit(solution)/shard_map/ppermute | solution.py:33
  19.6 1.3 collective-permute-start.3
  21.2 4.2 %collective-permute-done.3 = f32[16,386]{1,0:T(8,128)S(1)} collective-permute-done((f32[16,386]{1,0:T(8,128)S(1)}, f32[16,386]{1,0:T(8,128)S(1)}, u32[]{:S(2)}, u32[]{:S(2)}) %collective-permute-start.3) | collective-permute-done | bytes 24736 | tf_op jit(solution)/shard_map/ppermute | solution.py:34
  25.5 1.9 collective-permute-start.4
  27.4 3.6 %collective-permute-start.5 = (f32[10,386]{1,0:T(8,128)S(1)}, f32[10,386]{1,0:T(8,128)S(1)}, u32[]{:S(2)}, u32[]{:S(2)}) collective-permute-start(f32[10,386]{1,0:T(8,128)S(1)} %get-tuple-element.23), channel_id=1, source_target_pairs={{32,0},{64,32},{96,64},{128,96},{160,128},{192,160},{224,192},{33,... | collective-permute-start | bytes 46328 | tf_op jit(solution)/shard_map/ppermute | solution.py:34
  31.1 1.6 collective-permute-done.5
  34.0 0.6 copy-done.4
  35.1 0.5 copy-done.1
  36.7 3.4 %collective-permute-start.6 = (f32[16,386]{1,0:T(8,128)S(1)}, f32[16,386]{1,0:T(8,128)S(1)}, u32[]{:S(2)}, u32[]{:S(2)}) collective-permute-start(f32[16,386]{1,0:T(8,128)S(1)} %get-tuple-element.33), channel_id=1, source_target_pairs={{0,256},{256,512},{512,768},{1,257},{257,513},{513,769},{2,258},{2... | collective-permute-start | bytes 74120 | tf_op jit(solution)/shard_map/ppermute | solution.py:33
  40.1 1.3 collective-permute-start.7
  41.8 4.2 %collective-permute-done.7 = f32[16,386]{1,0:T(8,128)S(1)} collective-permute-done((f32[16,386]{1,0:T(8,128)S(1)}, f32[16,386]{1,0:T(8,128)S(1)}, u32[]{:S(2)}, u32[]{:S(2)}) %collective-permute-start.7) | collective-permute-done | bytes 24736 | tf_op jit(solution)/shard_map/ppermute | solution.py:34
  46.0 1.9 collective-permute-start.8
  47.9 3.6 %collective-permute-start.9 = (f32[10,386]{1,0:T(8,128)S(1)}, f32[10,386]{1,0:T(8,128)S(1)}, u32[]{:S(2)}, u32[]{:S(2)}) collective-permute-start(f32[10,386]{1,0:T(8,128)S(1)} %get-tuple-element.21), channel_id=1, source_target_pairs={{32,0},{64,32},{96,64},{128,96},{160,128},{192,160},{224,192},{33,... | collective-permute-start | bytes 46328 | tf_op jit(solution)/shard_map/ppermute | solution.py:34
  51.6 1.6 collective-permute-done.9
  55.7 3.1 %collective-permute-start.10 = (f32[16,386]{1,0:T(8,128)S(1)}, f32[16,386]{1,0:T(8,128)S(1)}, u32[]{:S(2)}, u32[]{:S(2)}) collective-permute-start(f32[16,386]{1,0:T(8,128)S(1)} %get-tuple-element.31), channel_id=1, source_target_pairs={{0,256},{256,512},{512,768},{1,257},{257,513},{513,769},{2,258},{2... | collective-permute-start | bytes 74120 | tf_op jit(solution)/shard_map/ppermute | solution.py:33
  58.8 1.3 collective-permute-start.11
  60.4 4.2 %collective-permute-done.11 = f32[16,386]{1,0:T(8,128)S(1)} collective-permute-done((f32[16,386]{1,0:T(8,128)S(1)}, f32[16,386]{1,0:T(8,128)S(1)}, u32[]{:S(2)}, u32[]{:S(2)}) %collective-permute-start.11) | collective-permute-done | bytes 24736 | tf_op jit(solution)/shard_map/ppermute | solution.py:34
  64.6 1.9 collective-permute-start.12
  66.6 3.6 %collective-permute-start.13 = (f32[10,386]{1,0:T(8,128)S(1)}, f32[10,386]{1,0:T(8,128)S(1)}, u32[]{:S(2)}, u32[]{:S(2)}) collective-permute-start(f32[10,386]{1,0:T(8,128)S(1)} %get-tuple-element.19), channel_id=1, source_target_pairs={{32,0},{64,32},{96,64},{128,96},{160,128},{192,160},{224,192},{33,... | collective-permute-start | bytes 46328 | tf_op jit(solution)/shard_map/ppermute | solution.py:34
  70.2 1.6 collective-permute-done.13
  74.4 1.9 collective-permute-start.14
  76.3 1.3 collective-permute-start.15
  78.0 4.2 %collective-permute-done.15 = f32[16,386]{1,0:T(8,128)S(1)} collective-permute-done((f32[16,386]{1,0:T(8,128)S(1)}, f32[16,386]{1,0:T(8,128)S(1)}, u32[]{:S(2)}, u32[]{:S(2)}) %collective-permute-start.15) | collective-permute-done | bytes 24736 | tf_op jit(solution)/shard_map/ppermute | solution.py:34
  82.2 1.9 collective-permute-start.16
  84.1 3.6 %collective-permute-start.17 = (f32[10,386]{1,0:T(8,128)S(1)}, f32[10,386]{1,0:T(8,128)S(1)}, u32[]{:S(2)}, u32[]{:S(2)}) collective-permute-start(f32[10,386]{1,0:T(8,128)S(1)} %get-tuple-element.17), channel_id=1, source_target_pairs={{32,0},{64,32},{96,64},{128,96},{160,128},{192,160},{224,192},{33,... | collective-permute-start | bytes 46328 | tf_op jit(solution)/shard_map/ppermute | solution.py:34
  87.8 1.6 collective-permute-done.17
  91.8 1.9 collective-permute-start.18
  93.7 1.3 collective-permute-start.19
  95.3 4.2 %collective-permute-done.19 = f32[16,386]{1,0:T(8,128)S(1)} collective-permute-done((f32[16,386]{1,0:T(8,128)S(1)}, f32[16,386]{1,0:T(8,128)S(1)}, u32[]{:S(2)}, u32[]{:S(2)}) %collective-permute-start.19) | collective-permute-done | bytes 24736 | tf_op jit(solution)/shard_map/ppermute | solution.py:34
  99.6 1.9 collective-permute-start.20
  101.5 3.6 %collective-permute-start.21 = (f32[10,386]{1,0:T(8,128)S(1)}, f32[10,386]{1,0:T(8,128)S(1)}, u32[]{:S(2)}, u32[]{:S(2)}) collective-permute-start(f32[10,386]{1,0:T(8,128)S(1)} %get-tuple-element.15), channel_id=1, source_target_pairs={{32,0},{64,32},{96,64},{128,96},{160,128},{192,160},{224,192},{33,... | collective-permute-start | bytes 46328 | tf_op jit(solution)/shard_map/ppermute | solution.py:34
  105.3 1.4 collective-permute-done.21
  107.3 0.7 copy-done.3
  108.8 1.9 collective-permute-start.22
  110.7 1.2 collective-permute-done.22
  111.9 3.5 %collective-permute-start.23 = (f32[8192]{0:T(1024)S(1)}, f32[8192]{0:T(1024)S(1)}, u32[]{:S(2)}, u32[]{:S(2)}) collective-permute-start(f32[8192]{0:T(1024)S(1)} %add.360), channel_id=1, source_target_pairs={{0,192},{32,224},{64,128},{96,160},{128,64},{160,96},{192,0},{224,... | collective-permute-start | bytes 98312 | tf_op jit(solution)/shard_map/ppermute | solution.py:57
  115.4 3.5 %collective-permute-done.23 = f32[8192]{0:T(1024)S(1)} collective-permute-done((f32[8192]{0:T(1024)S(1)}, f32[8192]{0:T(1024)S(1)}, u32[]{:S(2)}, u32[]{:S(2)}) %collective-permute-start.23) | collective-permute-done | bytes 32800 | tf_op jit(solution)/shard_map/ppermute | solution.py:57
  118.9 2.5 %collective-permute-start.24 = (f32[8192]{0:T(1024)S(1)}, f32[8192]{0:T(1024)S(1)}, u32[]{:S(2)}, u32[]{:S(2)}) collective-permute-start(f32[8192]{0:T(1024)S(1)} %add.361), channel_id=1, source_target_pairs={{0,64},{32,96},{64,0},{96,32},{128,192},{160,224},{192,128},{224,1... | collective-permute-start | bytes 98312 | tf_op jit(solution)/shard_map/ppermute | solution.py:57
  121.4 3.3 %collective-permute-done.24 = f32[8192]{0:T(1024)S(1)} collective-permute-done((f32[8192]{0:T(1024)S(1)}, f32[8192]{0:T(1024)S(1)}, u32[]{:S(2)}, u32[]{:S(2)}) %collective-permute-start.24) | collective-permute-done | bytes 32800 | tf_op jit(solution)/shard_map/ppermute | solution.py:57
  124.7 3.8 %collective-permute-start.25 = (f32[8192]{0:T(1024)S(1)}, f32[8192]{0:T(1024)S(1)}, u32[]{:S(2)}, u32[]{:S(2)}) collective-permute-start(f32[8192]{0:T(1024)S(1)} %add.362), channel_id=1, source_target_pairs={{0,1},{1,0},{2,3},{3,2},{4,5},{5,4},{6,7},{7,6},{8,9},{9,8},{10,11... | collective-permute-start | bytes 98312 | tf_op jit(solution)/shard_map/ppermute | solution.py:53
  128.5 2.0 collective-permute-done.25
  130.5 7.3 %collective-permute-start.26 = (f32[8192]{0:T(1024)S(1)}, f32[8192]{0:T(1024)S(1)}, u32[]{:S(2)}, u32[]{:S(2)}) collective-permute-start(f32[8192]{0:T(1024)S(1)} %add.363), channel_id=1, source_target_pairs={{0,2},{1,3},{2,0},{3,1},{4,6},{5,7},{6,4},{7,5},{8,10},{9,11},{10,... | collective-permute-start | bytes 98312 | tf_op jit(solution)/shard_map/ppermute | solution.py:53
  137.9 1.9 collective-permute-done.26
  139.7 9.1 %collective-permute-start.27 = (f32[8192]{0:T(1024)S(1)}, f32[8192]{0:T(1024)S(1)}, u32[]{:S(2)}, u32[]{:S(2)}) collective-permute-start(f32[8192]{0:T(1024)S(1)} %add.364), channel_id=1, source_target_pairs={{0,4},{1,5},{2,6},{3,7},{4,0},{5,1},{6,2},{7,3},{8,12},{9,13},{10,... | collective-permute-start | bytes 98312 | tf_op jit(solution)/shard_map/ppermute | solution.py:53
  148.8 1.9 collective-permute-done.27
  150.7 18.1 %collective-permute-start.28 = (f32[8192]{0:T(1024)S(1)}, f32[8192]{0:T(1024)S(1)}, u32[]{:S(2)}, u32[]{:S(2)}) collective-permute-start(f32[8192]{0:T(1024)S(1)} %add.365), channel_id=1, source_target_pairs={{0,24},{1,25},{2,26},{3,27},{4,28},{5,29},{6,30},{7,31},{8,16},{9,... | collective-permute-start | bytes 98312 | tf_op jit(solution)/shard_map/ppermute | solution.py:57
  168.9 1.9 collective-permute-done.28
  170.8 10.2 %collective-permute-start.29 = (f32[8192]{0:T(1024)S(1)}, f32[8192]{0:T(1024)S(1)}, u32[]{:S(2)}, u32[]{:S(2)}) collective-permute-start(f32[8192]{0:T(1024)S(1)} %add.366), channel_id=1, source_target_pairs={{0,8},{1,9},{2,10},{3,11},{4,12},{5,13},{6,14},{7,15},{8,0},{9,1},... | collective-permute-start | bytes 98312 | tf_op jit(solution)/shard_map/ppermute | solution.py:57
  181.1 4.4 %collective-permute-done.29 = f32[8192]{0:T(1024)S(1)} collective-permute-done((f32[8192]{0:T(1024)S(1)}, f32[8192]{0:T(1024)S(1)}, u32[]{:S(2)}, u32[]{:S(2)}) %collective-permute-start.29) | collective-permute-done | bytes 32800 | tf_op jit(solution)/shard_map/ppermute | solution.py:57
  185.4 1.9 collective-permute-start.30
  187.3 5.1 %collective-permute-done.30 = f32[8192]{0:T(1024)S(1)} collective-permute-done((f32[8192]{0:T(1024)S(1)}, f32[8192]{0:T(1024)S(1)}, u32[]{:S(2)}, u32[]{:S(2)}) %collective-permute-start.30) | collective-permute-done | bytes 32800 | tf_op jit(solution)/shard_map/ppermute | solution.py:57
  192.4 1.9 collective-permute-start.31
  194.4 3.9 %collective-permute-done.31 = f32[8192]{0:T(1024)S(1)} collective-permute-done((f32[8192]{0:T(1024)S(1)}, f32[8192]{0:T(1024)S(1)}, u32[]{:S(2)}, u32[]{:S(2)}) %collective-permute-start.31) | collective-permute-done | bytes 32800 | tf_op jit(solution)/shard_map/ppermute | solution.py:57
  198.2 0.7 convolution_bitcast_fusion.5
  199.0 0.5 copy-done.13
  199.8 0.7 copy.144
  (151 shorter events, 15.4 us)
Async XLA Ops:
  0.6 107.8 %copy-start = (f32[8,8192]{1,0:T(8,128)S(1)}, f32[8,8192]{1,0:T(8,128)}, u32[]{:S(2)}) copy-start(f32[8,8192]{1,0:T(8,128)} %param.13) | copy-start | bytes 786436
  0.6 1.1 copy-start.5
  1.9 6.6 %collective-permute-start = (f32[2,8,16,64]{3,1,2,0:T(8,128)S(1)}, f32[2,8,16,64]{3,1,2,0:T(8,128)S(1)}, u32[]{:S(2)}, u32[]{:S(2)}) collective-permute-start(f32[2,8,16,64]{3,1,2,0:T(8,128)S(1)} %pad_maximum_fusion.7), channel_id=1, source_target_pairs={{0,1},{1,2},{2,3},{3,4},{4,5},{5,6},{6,7},{7,8},{8,9},{9,10},{10,1... | collective-permute-start | bytes 196616 | tf_op jit(solution)/shard_map/ppermute | solution.py:125
  5.8 7.0 %collective-permute-start.1 = (f32[2,8,16,64]{3,1,2,0:T(8,128)S(1)}, f32[2,8,16,64]{3,1,2,0:T(8,128)S(1)}, u32[]{:S(2)}, u32[]{:S(2)}) collective-permute-start(f32[2,8,16,64]{3,1,2,0:T(8,128)S(1)} %pad_maximum_fusion.8), channel_id=1, source_target_pairs={{1,0},{2,1},{3,2},{4,3},{5,4},{6,5},{7,6},{8,7},{9,8},{10,9},{11,1... | collective-permute-start | bytes 196616 | tf_op jit(solution)/shard_map/ppermute | solution.py:126
  12.8 0.7 copy-start.12
  12.8 0.7 copy-start.8
  12.9 0.7 copy-start.9
  13.5 0.7 copy-start.10
  14.2 0.8 copy-start.6
  14.2 0.8 copy-start.7
  15.1 0.7 copy-start.11
  16.2 5.0 %collective-permute-start.2 = (f32[16,386]{1,0:T(8,128)S(1)}, f32[16,386]{1,0:T(8,128)S(1)}, u32[]{:S(2)}, u32[]{:S(2)}) collective-permute-start(f32[16,386]{1,0:T(8,128)S(1)} %bitcast.216), channel_id=1, source_target_pairs={{0,256},{256,512},{512,768},{1,257},{257,513},{513,769},{2,258},{2... | collective-permute-start | bytes 74120 | tf_op jit(solution)/shard_map/ppermute | solution.py:33
  19.6 5.8 %collective-permute-start.3 = (f32[16,386]{1,0:T(8,128)S(1)}, f32[16,386]{1,0:T(8,128)S(1)}, u32[]{:S(2)}, u32[]{:S(2)}) collective-permute-start(f32[16,386]{1,0:T(8,128)S(1)} %bitcast.217), channel_id=1, source_target_pairs={{256,0},{512,256},{768,512},{257,1},{513,257},{769,513},{258,2},{5... | collective-permute-start | bytes 74120 | tf_op jit(solution)/shard_map/ppermute | solution.py:34
  25.5 5.6 %collective-permute-start.4 = (f32[10,386]{1,0:T(8,128)S(1)}, f32[10,386]{1,0:T(8,128)S(1)}, u32[]{:S(2)}, u32[]{:S(2)}) collective-permute-start(f32[10,386]{1,0:T(8,128)S(1)} %get-tuple-element.22), channel_id=1, source_target_pairs={{0,32},{32,64},{64,96},{96,128},{128,160},{160,192},{192,224},{1,3... | collective-permute-start | bytes 46328 | tf_op jit(solution)/shard_map/ppermute | solution.py:33
  27.4 5.2 %collective-permute-start.5 = (f32[10,386]{1,0:T(8,128)S(1)}, f32[10,386]{1,0:T(8,128)S(1)}, u32[]{:S(2)}, u32[]{:S(2)}) collective-permute-start(f32[10,386]{1,0:T(8,128)S(1)} %get-tuple-element.23), channel_id=1, source_target_pairs={{32,0},{64,32},{96,64},{128,96},{160,128},{192,160},{224,192},{33,... | collective-permute-start | bytes 46328 | tf_op jit(solution)/shard_map/ppermute | solution.py:34
  33.0 0.7 copy-start.2
  33.9 0.7 copy-start.4
  34.8 0.8 copy-start.1
  36.7 5.0 %collective-permute-start.6 = (f32[16,386]{1,0:T(8,128)S(1)}, f32[16,386]{1,0:T(8,128)S(1)}, u32[]{:S(2)}, u32[]{:S(2)}) collective-permute-start(f32[16,386]{1,0:T(8,128)S(1)} %get-tuple-element.33), channel_id=1, source_target_pairs={{0,256},{256,512},{512,768},{1,257},{257,513},{513,769},{2,258},{2... | collective-permute-start | bytes 74120 | tf_op jit(solution)/shard_map/ppermute | solution.py:33
  40.1 5.8 %collective-permute-start.7 = (f32[16,386]{1,0:T(8,128)S(1)}, f32[16,386]{1,0:T(8,128)S(1)}, u32[]{:S(2)}, u32[]{:S(2)}) collective-permute-start(f32[16,386]{1,0:T(8,128)S(1)} %get-tuple-element.34), channel_id=1, source_target_pairs={{256,0},{512,256},{768,512},{257,1},{513,257},{769,513},{258,2},{5... | collective-permute-start | bytes 74120 | tf_op jit(solution)/shard_map/ppermute | solution.py:34
  46.0 5.6 %collective-permute-start.8 = (f32[10,386]{1,0:T(8,128)S(1)}, f32[10,386]{1,0:T(8,128)S(1)}, u32[]{:S(2)}, u32[]{:S(2)}) collective-permute-start(f32[10,386]{1,0:T(8,128)S(1)} %get-tuple-element.20), channel_id=1, source_target_pairs={{0,32},{32,64},{64,96},{96,128},{128,160},{160,192},{192,224},{1,3... | collective-permute-start | bytes 46328 | tf_op jit(solution)/shard_map/ppermute | solution.py:33
  47.9 5.2 %collective-permute-start.9 = (f32[10,386]{1,0:T(8,128)S(1)}, f32[10,386]{1,0:T(8,128)S(1)}, u32[]{:S(2)}, u32[]{:S(2)}) collective-permute-start(f32[10,386]{1,0:T(8,128)S(1)} %get-tuple-element.21), channel_id=1, source_target_pairs={{32,0},{64,32},{96,64},{128,96},{160,128},{192,160},{224,192},{33,... | collective-permute-start | bytes 46328 | tf_op jit(solution)/shard_map/ppermute | solution.py:34
  55.7 4.7 %collective-permute-start.10 = (f32[16,386]{1,0:T(8,128)S(1)}, f32[16,386]{1,0:T(8,128)S(1)}, u32[]{:S(2)}, u32[]{:S(2)}) collective-permute-start(f32[16,386]{1,0:T(8,128)S(1)} %get-tuple-element.31), channel_id=1, source_target_pairs={{0,256},{256,512},{512,768},{1,257},{257,513},{513,769},{2,258},{2... | collective-permute-start | bytes 74120 | tf_op jit(solution)/shard_map/ppermute | solution.py:33
  58.8 5.8 %collective-permute-start.11 = (f32[16,386]{1,0:T(8,128)S(1)}, f32[16,386]{1,0:T(8,128)S(1)}, u32[]{:S(2)}, u32[]{:S(2)}) collective-permute-start(f32[16,386]{1,0:T(8,128)S(1)} %get-tuple-element.32), channel_id=1, source_target_pairs={{256,0},{512,256},{768,512},{257,1},{513,257},{769,513},{258,2},{5... | collective-permute-start | bytes 74120 | tf_op jit(solution)/shard_map/ppermute | solution.py:34
  64.6 5.6 %collective-permute-start.12 = (f32[10,386]{1,0:T(8,128)S(1)}, f32[10,386]{1,0:T(8,128)S(1)}, u32[]{:S(2)}, u32[]{:S(2)}) collective-permute-start(f32[10,386]{1,0:T(8,128)S(1)} %get-tuple-element.18), channel_id=1, source_target_pairs={{0,32},{32,64},{64,96},{96,128},{128,160},{160,192},{192,224},{1,3... | collective-permute-start | bytes 46328 | tf_op jit(solution)/shard_map/ppermute | solution.py:33
  66.6 5.2 %collective-permute-start.13 = (f32[10,386]{1,0:T(8,128)S(1)}, f32[10,386]{1,0:T(8,128)S(1)}, u32[]{:S(2)}, u32[]{:S(2)}) collective-permute-start(f32[10,386]{1,0:T(8,128)S(1)} %get-tuple-element.19), channel_id=1, source_target_pairs={{32,0},{64,32},{96,64},{128,96},{160,128},{192,160},{224,192},{33,... | collective-permute-start | bytes 46328 | tf_op jit(solution)/shard_map/ppermute | solution.py:34
  74.4 3.5 %collective-permute-start.14 = (f32[16,386]{1,0:T(8,128)S(1)}, f32[16,386]{1,0:T(8,128)S(1)}, u32[]{:S(2)}, u32[]{:S(2)}) collective-permute-start(f32[16,386]{1,0:T(8,128)S(1)} %get-tuple-element.29), channel_id=1, source_target_pairs={{0,256},{256,512},{512,768},{1,257},{257,513},{513,769},{2,258},{2... | collective-permute-start | bytes 74120 | tf_op jit(solution)/shard_map/ppermute | solution.py:33
  76.3 5.8 %collective-permute-start.15 = (f32[16,386]{1,0:T(8,128)S(1)}, f32[16,386]{1,0:T(8,128)S(1)}, u32[]{:S(2)}, u32[]{:S(2)}) collective-permute-start(f32[16,386]{1,0:T(8,128)S(1)} %get-tuple-element.30), channel_id=1, source_target_pairs={{256,0},{512,256},{768,512},{257,1},{513,257},{769,513},{258,2},{5... | collective-permute-start | bytes 74120 | tf_op jit(solution)/shard_map/ppermute | solution.py:34
  82.2 5.6 %collective-permute-start.16 = (f32[10,386]{1,0:T(8,128)S(1)}, f32[10,386]{1,0:T(8,128)S(1)}, u32[]{:S(2)}, u32[]{:S(2)}) collective-permute-start(f32[10,386]{1,0:T(8,128)S(1)} %get-tuple-element.16), channel_id=1, source_target_pairs={{0,32},{32,64},{64,96},{96,128},{128,160},{160,192},{192,224},{1,3... | collective-permute-start | bytes 46328 | tf_op jit(solution)/shard_map/ppermute | solution.py:33
  84.1 5.2 %collective-permute-start.17 = (f32[10,386]{1,0:T(8,128)S(1)}, f32[10,386]{1,0:T(8,128)S(1)}, u32[]{:S(2)}, u32[]{:S(2)}) collective-permute-start(f32[10,386]{1,0:T(8,128)S(1)} %get-tuple-element.17), channel_id=1, source_target_pairs={{32,0},{64,32},{96,64},{128,96},{160,128},{192,160},{224,192},{33,... | collective-permute-start | bytes 46328 | tf_op jit(solution)/shard_map/ppermute | solution.py:34
  91.8 3.5 %collective-permute-start.18 = (f32[16,386]{1,0:T(8,128)S(1)}, f32[16,386]{1,0:T(8,128)S(1)}, u32[]{:S(2)}, u32[]{:S(2)}) collective-permute-start(f32[16,386]{1,0:T(8,128)S(1)} %get-tuple-element.27), channel_id=1, source_target_pairs={{0,256},{256,512},{512,768},{1,257},{257,513},{513,769},{2,258},{2... | collective-permute-start | bytes 74120 | tf_op jit(solution)/shard_map/ppermute | solution.py:33
  93.7 5.8 %collective-permute-start.19 = (f32[16,386]{1,0:T(8,128)S(1)}, f32[16,386]{1,0:T(8,128)S(1)}, u32[]{:S(2)}, u32[]{:S(2)}) collective-permute-start(f32[16,386]{1,0:T(8,128)S(1)} %get-tuple-element.28), channel_id=1, source_target_pairs={{256,0},{512,256},{768,512},{257,1},{513,257},{769,513},{258,2},{5... | collective-permute-start | bytes 74120 | tf_op jit(solution)/shard_map/ppermute | solution.py:34
  99.6 5.7 %collective-permute-start.20 = (f32[10,386]{1,0:T(8,128)S(1)}, f32[10,386]{1,0:T(8,128)S(1)}, u32[]{:S(2)}, u32[]{:S(2)}) collective-permute-start(f32[10,386]{1,0:T(8,128)S(1)} %get-tuple-element.14), channel_id=1, source_target_pairs={{0,32},{32,64},{64,96},{96,128},{128,160},{160,192},{192,224},{1,3... | collective-permute-start | bytes 46328 | tf_op jit(solution)/shard_map/ppermute | solution.py:33
  101.5 5.2 %collective-permute-start.21 = (f32[10,386]{1,0:T(8,128)S(1)}, f32[10,386]{1,0:T(8,128)S(1)}, u32[]{:S(2)}, u32[]{:S(2)}) collective-permute-start(f32[10,386]{1,0:T(8,128)S(1)} %get-tuple-element.15), channel_id=1, source_target_pairs={{32,0},{64,32},{96,64},{128,96},{160,128},{192,160},{224,192},{33,... | collective-permute-start | bytes 46328 | tf_op jit(solution)/shard_map/ppermute | solution.py:34
  107.1 0.9 copy-start.3
  108.8 3.1 %collective-permute-start.22 = (f32[8192]{0:T(1024)S(1)}, f32[8192]{0:T(1024)S(1)}, u32[]{:S(2)}, u32[]{:S(2)}) collective-permute-start(f32[8192]{0:T(1024)S(1)} %bitcast.203), channel_id=1, source_target_pairs={{0,32},{32,0},{64,96},{96,64},{128,160},{160,128},{192,224},{224,1... | collective-permute-start | bytes 98312 | tf_op jit(solution)/shard_map/ppermute | solution.py:53
  111.9 7.0 %collective-permute-start.23 = (f32[8192]{0:T(1024)S(1)}, f32[8192]{0:T(1024)S(1)}, u32[]{:S(2)}, u32[]{:S(2)}) collective-permute-start(f32[8192]{0:T(1024)S(1)} %add.360), channel_id=1, source_target_pairs={{0,192},{32,224},{64,128},{96,160},{128,64},{160,96},{192,0},{224,... | collective-permute-start | bytes 98312 | tf_op jit(solution)/shard_map/ppermute | solution.py:57
  118.9 5.8 %collective-permute-start.24 = (f32[8192]{0:T(1024)S(1)}, f32[8192]{0:T(1024)S(1)}, u32[]{:S(2)}, u32[]{:S(2)}) collective-permute-start(f32[8192]{0:T(1024)S(1)} %add.361), channel_id=1, source_target_pairs={{0,64},{32,96},{64,0},{96,32},{128,192},{160,224},{192,128},{224,1... | collective-permute-start | bytes 98312 | tf_op jit(solution)/shard_map/ppermute | solution.py:57
  124.7 5.8 %collective-permute-start.25 = (f32[8192]{0:T(1024)S(1)}, f32[8192]{0:T(1024)S(1)}, u32[]{:S(2)}, u32[]{:S(2)}) collective-permute-start(f32[8192]{0:T(1024)S(1)} %add.362), channel_id=1, source_target_pairs={{0,1},{1,0},{2,3},{3,2},{4,5},{5,4},{6,7},{7,6},{8,9},{9,8},{10,11... | collective-permute-start | bytes 98312 | tf_op jit(solution)/shard_map/ppermute | solution.py:53
  130.5 9.2 %collective-permute-start.26 = (f32[8192]{0:T(1024)S(1)}, f32[8192]{0:T(1024)S(1)}, u32[]{:S(2)}, u32[]{:S(2)}) collective-permute-start(f32[8192]{0:T(1024)S(1)} %add.363), channel_id=1, source_target_pairs={{0,2},{1,3},{2,0},{3,1},{4,6},{5,7},{6,4},{7,5},{8,10},{9,11},{10,... | collective-permute-start | bytes 98312 | tf_op jit(solution)/shard_map/ppermute | solution.py:53
  139.7 11.0 %collective-permute-start.27 = (f32[8192]{0:T(1024)S(1)}, f32[8192]{0:T(1024)S(1)}, u32[]{:S(2)}, u32[]{:S(2)}) collective-permute-start(f32[8192]{0:T(1024)S(1)} %add.364), channel_id=1, source_target_pairs={{0,4},{1,5},{2,6},{3,7},{4,0},{5,1},{6,2},{7,3},{8,12},{9,13},{10,... | collective-permute-start | bytes 98312 | tf_op jit(solution)/shard_map/ppermute | solution.py:53
  150.7 20.1 %collective-permute-start.28 = (f32[8192]{0:T(1024)S(1)}, f32[8192]{0:T(1024)S(1)}, u32[]{:S(2)}, u32[]{:S(2)}) collective-permute-start(f32[8192]{0:T(1024)S(1)} %add.365), channel_id=1, source_target_pairs={{0,24},{1,25},{2,26},{3,27},{4,28},{5,29},{6,30},{7,31},{8,16},{9,... | collective-permute-start | bytes 98312 | tf_op jit(solution)/shard_map/ppermute | solution.py:57
  170.8 14.6 %collective-permute-start.29 = (f32[8192]{0:T(1024)S(1)}, f32[8192]{0:T(1024)S(1)}, u32[]{:S(2)}, u32[]{:S(2)}) collective-permute-start(f32[8192]{0:T(1024)S(1)} %add.366), channel_id=1, source_target_pairs={{0,8},{1,9},{2,10},{3,11},{4,12},{5,13},{6,14},{7,15},{8,0},{9,1},... | collective-permute-start | bytes 98312 | tf_op jit(solution)/shard_map/ppermute | solution.py:57
  185.4 7.0 %collective-permute-start.30 = (f32[8192]{0:T(1024)S(1)}, f32[8192]{0:T(1024)S(1)}, u32[]{:S(2)}, u32[]{:S(2)}) collective-permute-start(f32[8192]{0:T(1024)S(1)} %add.367), channel_id=1, source_target_pairs={{0,768},{256,512},{512,256},{768,0},{1,769},{257,513},{513,257},{7... | collective-permute-start | bytes 98312 | tf_op jit(solution)/shard_map/ppermute | solution.py:57
  192.4 5.8 %collective-permute-start.31 = (f32[8192]{0:T(1024)S(1)}, f32[8192]{0:T(1024)S(1)}, u32[]{:S(2)}, u32[]{:S(2)}) collective-permute-start(f32[8192]{0:T(1024)S(1)} %add.368), channel_id=1, source_target_pairs={{0,256},{256,0},{512,768},{768,512},{1,257},{257,1},{513,769},{769... | collective-permute-start | bytes 98312 | tf_op jit(solution)/shard_map/ppermute | solution.py:57
  198.9 0.5 copy-start.13
